TPU v7x, 512 devices: a whole 4x8x8 slice. The times are simulated.
512 devices in a mesh: freq: 16 (over z, core), row: 32 (over x, y).
Axes of the slice: x: 4, y: 8, z: 8, core: 2. Of those that a mesh axis runs over, the one named last changes fastest.
Arguments:
- vis_values: bfloat16 [16, 2048, 2, 128], P('freq', 'row'), may hold values from -6 to 6
- kernel_u: bfloat16 [16, 2048, 7, 128], P('freq', 'row'), may hold values from 0.049804688 to 1
- kernel_v: bfloat16 [16, 2048, 7, 128], P('freq', 'row'), may hold values from 0.049804688 to 1
- offset_u: int32 [16, 2048, 128], P('freq', 'row'), may hold values from 0 to 9
- offset_v: int32 [16, 2048, 128], P('freq', 'row'), may hold values from 0 to 121
- block_owner: int32 [16, 2048, 1], P('freq', 'row'), may hold values from 0 to 31; in each aligned block of 64 rows (0 to 63, 64 to 127, ..., all dimensions but the last counted through in order) at most 8 rows name the same one
- tile_slot: int32 [16, 2048], P('freq', 'row'), may hold values from 0 to 255
- channel_freq: float32 [16], P('freq'), may hold values from 0.856 to 1.712
Outputs:
- taylor: bfloat16 [3, 4096, 4096], P(None, 'freq', 'row')
Inputs may be any that keep to these rules, and one draw needn't show every extreme that they name: `block_owner`: among the 64 blocks of one channel held by one index of row, at most 8 name the same owner, a bound that some block reaches.
All inputs are finite; a program needn't handle non-finite values.
Results may differ from a plain program's by a relative error of at most 0.024.
Values may be sent and summed in bfloat16 or wider, within the bound.
No kernel may reach another device: no remote copies, remote signals or barrier semaphores. Data moves between devices by JAX's collectives and lax.ppermute only.
A program may use at most 64 MiB of HBM per device.

v0:
```python
from functools import partial
import math

import jax
import jax.numpy as jnp
from jax import lax
from jax.sharding import PartitionSpec as P

GRID = 4096
TU = 16
TV = 128


def for_sending(shard):
    return jax.tree.map(lambda a: a.astype(jnp.bfloat16) if a.dtype == jnp.float32 else a, shard)


def dft_tables(length):
    outer_len = 32
    inner_len = length // outer_len
    index_outer = jnp.arange(outer_len, dtype=jnp.int32)
    index_inner = jnp.arange(inner_len, dtype=jnp.int32)
    full_turn = 2.0 * math.pi
    angle_outer = (
        full_turn
        * (index_outer[:, None] * index_outer[None, :] % outer_len).astype(jnp.float32)
        / outer_len
    )
    angle_twist = (
        full_turn
        * (index_outer[:, None] * index_inner[None, :] % length).astype(jnp.float32)
        / length
    )
    angle_inner = (
        full_turn
        * (index_inner[:, None] * index_inner[None, :] % inner_len).astype(jnp.float32)
        / inner_len
    )
    return (
        jnp.cos(angle_outer),
        jnp.sin(angle_outer),
        jnp.cos(angle_twist),
        jnp.sin(angle_twist),
        jnp.cos(angle_inner),
        jnp.sin(angle_inner),
    )


def transform_last(real_part, imag_part):
    row_total, length = real_part.shape
    outer_len = 32
    inner_len = length // outer_len
    cos_outer, sin_outer, cos_twist, sin_twist, cos_inner, sin_inner = dft_tables(length)
    product = partial(jnp.einsum, precision=lax.Precision.HIGHEST)
    real_part = real_part.reshape(row_total, outer_len, inner_len)
    imag_part = imag_part.reshape(row_total, outer_len, inner_len)
    step_real = product("rab,ak->rkb", real_part, cos_outer) - product(
        "rab,ak->rkb", imag_part, sin_outer
    )
    step_imag = product("rab,ak->rkb", real_part, sin_outer) + product(
        "rab,ak->rkb", imag_part, cos_outer
    )
    twist_real = step_real * cos_twist - step_imag * sin_twist
    twist_imag = step_real * sin_twist + step_imag * cos_twist
    out_real = product("rkb,bm->rmk", twist_real, cos_inner) - product(
        "rkb,bm->rmk", twist_imag, sin_inner
    )
    out_imag = product("rkb,bm->rmk", twist_real, sin_inner) + product(
        "rkb,bm->rmk", twist_imag, cos_inner
    )
    return (out_real.reshape(row_total, length), out_imag.reshape(row_total, length))


def transform_first_real(real_part, imag_part):
    length, col_total = real_part.shape
    outer_len = 32
    inner_len = length // outer_len
    cos_outer, sin_outer, cos_twist, sin_twist, cos_inner, sin_inner = dft_tables(length)
    product = partial(jnp.einsum, precision=lax.Precision.HIGHEST)
    real_part = real_part.reshape(outer_len, inner_len, col_total)
    imag_part = imag_part.reshape(outer_len, inner_len, col_total)
    step_real = product("abc,ak->kbc", real_part, cos_outer) - product(
        "abc,ak->kbc", imag_part, sin_outer
    )
    step_imag = product("abc,ak->kbc", real_part, sin_outer) + product(
        "abc,ak->kbc", imag_part, cos_outer
    )
    twist_real = step_real * cos_twist[:, :, None] - step_imag * sin_twist[:, :, None]
    twist_imag = step_real * sin_twist[:, :, None] + step_imag * cos_twist[:, :, None]
    out_real = product("kbc,bm->mkc", twist_real, cos_inner) - product(
        "kbc,bm->mkc", twist_imag, sin_inner
    )
    return out_real.reshape(length, col_total)


def grid_blocks(payload, offsets):
    tap_count = (payload.shape[1] - 2) // 2
    values = payload[:, :2, :].astype(jnp.float32)
    kern_u = payload[:, 2 : 2 + tap_count, :]
    kern_v = payload[:, 2 + tap_count :, :]
    row_grid = jnp.arange(TU, dtype=jnp.int32)[None, :, None]
    col_grid = jnp.arange(TV, dtype=jnp.int32)[None, None, :]
    spread_u = jnp.zeros((payload.shape[0], TU, payload.shape[2]), jnp.float32)
    spread_v = jnp.zeros((payload.shape[0], payload.shape[2], TV), jnp.bfloat16)
    for tap_index in range(tap_count):
        spread_u = spread_u + jnp.where(
            row_grid == offsets[:, 0:1, :] + tap_index,
            kern_u[:, tap_index : tap_index + 1, :].astype(jnp.float32),
            0.0,
        )
        spread_v = jnp.where(
            col_grid == offsets[:, 1, :, None] + tap_index, kern_v[:, tap_index, :, None], spread_v
        )
    left = (values[:, :, None, :] * spread_u[:, None, :, :]).astype(jnp.bfloat16)
    return jnp.einsum("spin,snj->spij", left, spread_v, preferred_element_type=jnp.float32)


def shards(
    vis_values, kernel_u, kernel_v, offset_u, offset_v, block_owner, tile_slot, channel_freq
):
    row_count = lax.axis_size("row")
    block_count = vis_values.shape[1]
    vis_count = vis_values.shape[3]
    capacity = max(2, 4 * block_count // row_count)
    slot_count = row_count * capacity
    slab_rows = GRID // row_count
    tiles_total = slab_rows // TU * (GRID // TV)
    owner_row = block_owner[0, :, 0]
    row_marks = (owner_row[:, None] == jnp.arange(row_count, dtype=jnp.int32)[None, :]).astype(
        jnp.int32
    )
    before = jnp.cumsum(row_marks, axis=0) - row_marks
    slot_rank = jnp.sum(before * row_marks, axis=1)
    target = owner_row * capacity + slot_rank
    payload = jnp.concatenate([vis_values[0], kernel_u[0], kernel_v[0]], axis=1)
    offsets = jnp.stack([offset_u[0], offset_v[0]], axis=1)
    send_tile = jnp.full((slot_count,), tiles_total, jnp.int32).at[target].set(tile_slot[0])
    send_tile = send_tile.reshape(row_count, capacity)
    send_payload = (
        jnp.zeros((slot_count,) + payload.shape[1:], jnp.bfloat16).at[target].set(payload)
    )
    send_offsets = jnp.zeros((slot_count,) + offsets.shape[1:], jnp.int32).at[target].set(offsets)
    recv_payload, recv_offsets, recv_tile = (
        lax.all_to_all(
            send_payload.reshape((row_count, capacity) + payload.shape[1:]),
            "row",
            split_axis=0,
            concat_axis=0,
            tiled=True,
        ),
        lax.all_to_all(
            send_offsets.reshape((row_count, capacity) + offsets.shape[1:]),
            "row",
            split_axis=0,
            concat_axis=0,
            tiled=True,
        ),
        lax.all_to_all(send_tile, "row", split_axis=0, concat_axis=0, tiled=True),
    )
    contribution = grid_blocks(
        recv_payload.reshape((slot_count,) + payload.shape[1:]),
        recv_offsets.reshape((slot_count,) + offsets.shape[1:]),
    )
    slab_tiles = (
        jnp.zeros((tiles_total, 2, TU, TV), jnp.float32)
        .at[recv_tile.reshape(-1)]
        .add(contribution, mode="drop")
    )
    slab_grid = (
        slab_tiles.reshape(slab_rows // TU, GRID // TV, 2, TU, TV)
        .transpose(2, 0, 3, 1, 4)
        .reshape(2, slab_rows, GRID)
    )
    spec_real, spec_imag = transform_last(slab_grid[0], slab_grid[1])
    spectrum = jnp.stack([spec_real, spec_imag]).reshape(2, slab_rows, row_count, GRID // row_count)
    image_scale = 1.0 / math.sqrt(block_count * row_count * vis_count)
    offset_freq = (channel_freq[0] - 1.284) / 0.428
    weights = jnp.stack([jnp.ones_like(offset_freq), offset_freq, offset_freq * offset_freq])
    received = lax.all_to_all(
        for_sending(spectrum), "row", split_axis=2, concat_axis=1, tiled=True
    ).astype(spectrum.dtype)
    width_here = received.shape[2] * received.shape[3]
    real_cols = received[0].reshape(GRID, width_here)
    imag_cols = received[1].reshape(GRID, width_here)
    dirty_image = transform_first_real(real_cols, imag_cols) * image_scale
    taylor_terms = (weights[:, None, None] * dirty_image[None]).astype(jnp.bfloat16)
    terms_all = taylor_terms.reshape(3, GRID, received.shape[2], received.shape[3])
    terms_all = terms_all.reshape(3, GRID, GRID // row_count).astype(jnp.float32)
    summed = lax.psum_scatter(
        terms_all.astype(jnp.bfloat16), "freq", scatter_dimension=1, tiled=True
    )
    return summed


def solution(mesh):
    return jax.shard_map(
        shards,
        mesh=mesh,
        in_specs=(
            P("freq", "row", None, None),
            P("freq", "row", None, None),
            P("freq", "row", None, None),
            P("freq", "row", None),
            P("freq", "row", None),
            P("freq", "row", None),
            P("freq", "row"),
            P("freq"),
        ),
        out_specs=P(None, "freq", "row"),
        check_vma=False,
    )
```

profile of v0, /device:TPU:6, one launch (start us, length us, event | category | flops | bytes accessed | tf_op | source)
XLA Modules:
  0.0 408.2 jit_solution(4625411051952188022)
XLA Ops:
  10.5 10.2 %all-to-all-start = ((s32[32,1,8]{2,1,0:T(1,128)}), s32[32,1,8]{2,1,0:T(1,128)S(1)}, u32[]{:S(2)}, u32[]{:S(2)}) async-start(s32[32,1,8]{2,1,0:T(1,128)} %bitcast.7), calls=%async_computation | async-start | bytes 32768 | tf_op jit(solution)/shard_map/all_to_all | solution.py:158
  22.3 6.6 %scatter_fusion.1 = s32[256,2,128]{2,1,0:T(2,128)} fusion(s32[256,2,128]{2,1,0:T(2,128)} %broadcast_in_dim.180, s32[64]{0:T(128)S(1)} %fusion.115, s32[64,2,128]{2,1,0:T(2,128)S(1)} %copy.44), kind=kCustom, calls=%fused_computation.2 | custom fusion | bytes 196864 | tf_op jit(solution)/shard_map/scatter | solution.py:142
  28.9 9.7 %all-to-all-start.2 = ((s32[32,8,2,128]{3,2,1,0:T(2,128)}), s32[32,8,2,128]{3,2,1,0:T(2,128)S(1)}, u32[]{:S(2)}, u32[]{:S(2)}) async-start(s32[32,8,2,128]{3,2,1,0:T(2,128)} %bitcast.16), calls=%async_computation.2 | async-start | bytes 524288 | tf_op jit(solution)/shard_map/all_to_all | solution.py:151
  40.6 1.1 broadcast_in_dim.179
  41.7 6.4 %scatter_fusion = bf16[256,16,128]{2,1,0:T(8,128)(2,1)} fusion(bf16[256,16,128]{2,1,0:T(8,128)(2,1)} %broadcast_in_dim.179, s32[64]{0:T(128)S(1)} %fusion.115, bf16[64,16,128]{2,1,0:T(8,128)(2,1)S(1)} %copy.41), kind=kCustom, calls=%fused_computation.1 | custom fusion | bytes 786688 | tf_op jit(solution)/shard_map/scatter | solution.py:140
  48.7 9.3 %all-to-all-start.1 = ((bf16[32,8,16,128]{3,2,1,0:T(8,128)(2,1)}), bf16[32,8,16,128]{3,2,1,0:T(8,128)(2,1)S(1)}, u32[]{:S(2)}, u32[]{:S(2)}) async-start(bf16[32,8,16,128]{3,2,1,0:T(8,128)(2,1)} %bitcast.12), calls=%async_computation.1 | async-start | bytes 2097152 | tf_op jit(solution)/shard_map/all_to_all | solution.py:144
  60.0 23.5 %all-to-all-done.1 = bf16[32,8,16,128]{3,2,1,0:T(8,128)(2,1)S(1)} async-done(((bf16[32,8,16,128]{3,2,1,0:T(8,128)(2,1)}), bf16[32,8,16,128]{3,2,1,0:T(8,128)(2,1)S(1)}, u32[]{:S(2)}, u32[]{:S(2)}) %all-to-all-start.1) | async-done | bytes 1048608 | tf_op jit(solution)/shard_map/all_to_all | solution.py:144
  84.1 1.8 select_add_fusion
  86.0 109.5 %fusion.8 = f32[256,2,16,128]{3,2,1,0:T(8,128)} fusion(s32[256,128]{1,0:T(8,128)S(1)} %bitcast.179, s32[256,128]{1,0:T(8,128)S(1)} %get-tuple-element.34, s32[256,128]{1,0:T(8,128)S(1)} %get-tuple-element.35, s32[256,128]{1,0:T(8,128)S(1)} %get-tuple-element.36, s32[256,128]{1,0:T(8,128)S(1)} %get-tuple-element.37, s32[256,128]{1,0:T(8,128)S(1)} %get-tuple-element.38, ...), kind=kOutput, calls=%fused_computation.19 | convolution fusion | flops 329252864 | bytes 7929856 | tf_op jit(solution)/shard_map/spin,snj->spij/dot_general | solution.py:115
  195.4 2.5 broadcast_in_dim.178
  197.9 35.4 %scatter_fusion.2 = f32[256,2,16,128]{3,2,1,0:T(8,128)} fusion(f32[256,2,16,128]{3,2,1,0:T(8,128)} %broadcast_in_dim.178, s32[256]{0:T(256)S(1)} %bitcast.192, f32[256,2,16,128]{3,2,1,0:T(8,128)} %fusion.8), kind=kCustom, calls=%fused_computation.3 | custom fusion | flops 1048576 | bytes 12583936 | tf_op jit(solution)/shard_map/scatter-add | solution.py:167
  233.3 2.7 fusion.175
  236.6 2.0 fusion.89
  238.6 2.0 fusion.95
  241.2 2.0 convolution_add_fusion.1
  243.2 2.5 subtract_bitcast_fusion
  245.7 3.3 fusion.33
  249.0 3.2 fusion.31
  252.2 3.3 fusion.45
  256.2 3.3 fusion.48
  260.6 2.8 copy.54
  263.3 6.8 %all-to-all-start.3 = ((bf16[2,128,32,128]{3,1,0,2:T(8,128)(2,1)}), bf16[2,128,32,128]{3,1,0,2:T(8,128)(2,1)S(1)}, u32[]{:S(2)}, u32[]{:S(2)}) async-start(bf16[2,128,32,128]{3,1,0,2:T(8,128)(2,1)} %copy.54), calls=%async_computation.3 | async-start | bytes 4194304 | tf_op jit(solution)/shard_map/all_to_all | solution.py:179
  271.1 46.1 %all-to-all-done.3 = bf16[2,128,32,128]{3,1,0,2:T(8,128)(2,1)S(1)} async-done(((bf16[2,128,32,128]{3,1,0,2:T(8,128)(2,1)}), bf16[2,128,32,128]{3,1,0,2:T(8,128)(2,1)S(1)}, u32[]{:S(2)}, u32[]{:S(2)}) %all-to-all-start.3) | async-done | bytes 2097184 | tf_op jit(solution)/shard_map/all_to_all | solution.py:179
  317.2 1.4 copy.88
  318.6 1.1 fusion.52
  320.7 1.1 convolution_subtract_fusion
  321.8 2.2 multiply_subtract_fusion
  324.0 3.1 fusion.25
  327.1 3.3 subtract_multiply_fusion
  330.4 1.2 copy.60
  331.6 2.2 multiply_convert_fusion
  333.9 67.2 %reduce-scatter.2.cloned.1.call-done = bf16[3,256,128]{2,1,0:T(8,128)(2,1)} async-done(((bf16[3,4096,128]{2,1,0:T(8,128)(2,1)}), bf16[3,256,128]{2,1,0:T(8,128)(2,1)}) %reduce-scatter.2.cloned.1.call-update) | async-done | bytes 196624 | tf_op jit(solution)/shard_map/reduce_scatter | solution.py:189
  (36 shorter events, 15.0 us)
Async XLA Ops:
  10.5 18.5 %all-to-all-start = ((s32[32,1,8]{2,1,0:T(1,128)}), s32[32,1,8]{2,1,0:T(1,128)S(1)}, u32[]{:S(2)}, u32[]{:S(2)}) async-start(s32[32,1,8]{2,1,0:T(1,128)} %bitcast.7), calls=%async_computation | async-start | bytes 32768 | tf_op jit(solution)/shard_map/all_to_all | solution.py:158
  28.9 19.7 %all-to-all-start.2 = ((s32[32,8,2,128]{3,2,1,0:T(2,128)}), s32[32,8,2,128]{3,2,1,0:T(2,128)S(1)}, u32[]{:S(2)}, u32[]{:S(2)}) async-start(s32[32,8,2,128]{3,2,1,0:T(2,128)} %bitcast.16), calls=%async_computation.2 | async-start | bytes 524288 | tf_op jit(solution)/shard_map/all_to_all | solution.py:151
  48.7 34.8 %all-to-all-start.1 = ((bf16[32,8,16,128]{3,2,1,0:T(8,128)(2,1)}), bf16[32,8,16,128]{3,2,1,0:T(8,128)(2,1)S(1)}, u32[]{:S(2)}, u32[]{:S(2)}) async-start(bf16[32,8,16,128]{3,2,1,0:T(8,128)(2,1)} %bitcast.12), calls=%async_computation.1 | async-start | bytes 2097152 | tf_op jit(solution)/shard_map/all_to_all | solution.py:144
  263.3 53.9 %all-to-all-start.3 = ((bf16[2,128,32,128]{3,1,0,2:T(8,128)(2,1)}), bf16[2,128,32,128]{3,1,0,2:T(8,128)(2,1)S(1)}, u32[]{:S(2)}, u32[]{:S(2)}) async-start(bf16[2,128,32,128]{3,1,0,2:T(8,128)(2,1)} %copy.54), calls=%async_computation.3 | async-start | bytes 4194304 | tf_op jit(solution)/shard_map/all_to_all | solution.py:179
  270.1 131.0 %reduce-scatter.2.cloned.1.call-start = ((), (), s32[]{:S(2)}) async-start(), calls=%async_computation.5 | async-start | bytes 3342336 | tf_op jit(solution)/shard_map/reduce_scatter | solution.py:189
Sparse Core Ops, SparseCore 0:
  334.0 67.0 reduce-scatter.1
where the time goes:
time: 415 us; the launch traced here: 408 us
  matrix products  143 us (34%)
  waiting for transfers between devices  137 us (33%)
  other arithmetic  45.4 us (11%)
  starting transfers between devices  36.1 us (9%)
  local copies, waits for them, and re-layouts  32.1 us (8%)
  between operations  14.6 us (4%)
    dot_general x1, matrix products, grid_blocks(): jnp.einsum('spin,snj->spij', left, spread_v, preferred_element_type=jnp.f...  109 us
    reduce_scatter x1, waiting for transfers between devices, shards(): lax.psum_scatter(terms_all.astype(jnp.bfloat16), 'freq', scatter_dimensio...  67.2 us
    all_to_all x1, waiting for transfers between devices, shards(): lax.all_to_all(for_sending(spectrum), 'row', split_axis=2, concat_axis=1,...  46.1 us
    scatter-add x1, other arithmetic, shards(): slab_tiles = jnp.zeros((tiles_total, 2, TU, TV), jnp.float32).at[recv_til...  35.4 us
    all_to_all x1, waiting for transfers between devices, shards(): lax.all_to_all(send_payload.reshape((row_count, capacity) + payload.shape...  23.5 us
    all_to_all x1, starting transfers between devices, shards(): lax.all_to_all(send_tile, 'row', split_axis=0, concat_axis=0, tiled=True)  10.2 us
    all_to_all x1, starting transfers between devices, shards(): lax.all_to_all(send_offsets.reshape((row_count, capacity) + offsets.shape...  9.71 us
    all_to_all x1, starting transfers between devices, shards(): lax.all_to_all(send_payload.reshape((row_count, capacity) + payload.shape...  9.3 us
  transfers between devices with their start and end apart: 5, of which 4 were waited for; matrix products, arithmetic and copies ran while one was open for 5% of the time, Pallas kernels for 0%

commit v1 on v0

--- a/solution.py
+++ b/solution.py
@@ -5,6 +5,8 @@
 import jax.numpy as jnp
 from jax import lax
 from jax.sharding import PartitionSpec as P
+from jax.experimental import pallas as pl
+from jax.experimental.pallas import tpu as pltpu
 
 GRID = 4096
 TU = 16
@@ -93,26 +95,58 @@
     return out_real.reshape(length, col_total)
 
 
-def grid_blocks(payload, offsets):
-    tap_count = (payload.shape[1] - 2) // 2
-    values = payload[:, :2, :].astype(jnp.float32)
-    kern_u = payload[:, 2 : 2 + tap_count, :]
-    kern_v = payload[:, 2 + tap_count :, :]
-    row_grid = jnp.arange(TU, dtype=jnp.int32)[None, :, None]
-    col_grid = jnp.arange(TV, dtype=jnp.int32)[None, None, :]
-    spread_u = jnp.zeros((payload.shape[0], TU, payload.shape[2]), jnp.float32)
-    spread_v = jnp.zeros((payload.shape[0], payload.shape[2], TV), jnp.bfloat16)
-    for tap_index in range(tap_count):
-        spread_u = spread_u + jnp.where(
-            row_grid == offsets[:, 0:1, :] + tap_index,
-            kern_u[:, tap_index : tap_index + 1, :].astype(jnp.float32),
-            0.0,
-        )
-        spread_v = jnp.where(
-            col_grid == offsets[:, 1, :, None] + tap_index, kern_v[:, tap_index, :, None], spread_v
-        )
-    left = (values[:, :, None, :] * spread_u[:, None, :, :]).astype(jnp.bfloat16)
-    return jnp.einsum("spin,snj->spij", left, spread_v, preferred_element_type=jnp.float32)
+PAY_ROWS = 19
+
+
+def grid_kernel(tile_ref, pay_ref, out_ref):
+    tiles_total = out_ref.shape[1] // TU * (out_ref.shape[2] // TV)
+    tile_cols = out_ref.shape[2] // TV
+    out_ref[...] = jnp.zeros(out_ref.shape, jnp.float32)
+
+    def body(b, carry):
+        tile = tile_ref[b]
+
+        @pl.when(tile < tiles_total)
+        def _():
+            blk = pay_ref[b].astype(jnp.float32)
+            vis = blk[0:2]
+            ku = blk[2:9]
+            kv = blk[9:16]
+            ou = blk[16:17].astype(jnp.int32)
+            ov = blk[17:18].astype(jnp.int32)
+            du = lax.broadcasted_iota(jnp.int32, (TU, blk.shape[1]), 0) - ou
+            su = jnp.zeros((TU, blk.shape[1]), jnp.float32)
+            for t in range(7):
+                su = jnp.where(du == t, ku[t : t + 1], su)
+            left = jnp.concatenate([vis[0:1] * su, vis[1:2] * su], axis=0).astype(jnp.bfloat16)
+            dv = lax.broadcasted_iota(jnp.int32, (TV, blk.shape[1]), 0) - ov
+            sv = jnp.zeros((TV, blk.shape[1]), jnp.float32)
+            for t in range(7):
+                sv = jnp.where(dv == t, kv[t : t + 1], sv)
+            sv = sv.astype(jnp.bfloat16)
+            contrib = lax.dot_general(
+                left, sv, (((1,), (1,)), ((), ())), preferred_element_type=jnp.float32
+            )
+            row0 = pl.multiple_of((tile // tile_cols) * TU, TU)
+            col0 = pl.multiple_of((tile % tile_cols) * TV, TV)
+            for p in range(2):
+                out_ref[p, pl.ds(row0, TU), pl.ds(col0, TV)] += contrib[p * TU : (p + 1) * TU]
+
+        return carry
+
+    lax.fori_loop(0, pay_ref.shape[0], body, 0)
+
+
+def grid_into_slab(tile_ids, payload, slab_rows):
+    return pl.pallas_call(
+        grid_kernel,
+        out_shape=jax.ShapeDtypeStruct((2, slab_rows, GRID), jnp.float32),
+        in_specs=[
+            pl.BlockSpec(memory_space=pltpu.SMEM),
+            pl.BlockSpec(memory_space=pltpu.VMEM),
+        ],
+        out_specs=pl.BlockSpec(memory_space=pltpu.VMEM),
+    )(tile_ids, payload)
 
 
 def shards(
@@ -132,45 +166,38 @@
     before = jnp.cumsum(row_marks, axis=0) - row_marks
     slot_rank = jnp.sum(before * row_marks, axis=1)
     target = owner_row * capacity + slot_rank
-    payload = jnp.concatenate([vis_values[0], kernel_u[0], kernel_v[0]], axis=1)
-    offsets = jnp.stack([offset_u[0], offset_v[0]], axis=1)
-    send_tile = jnp.full((slot_count,), tiles_total, jnp.int32).at[target].set(tile_slot[0])
-    send_tile = send_tile.reshape(row_count, capacity)
-    send_payload = (
-        jnp.zeros((slot_count,) + payload.shape[1:], jnp.bfloat16).at[target].set(payload)
-    )
-    send_offsets = jnp.zeros((slot_count,) + offsets.shape[1:], jnp.int32).at[target].set(offsets)
-    recv_payload, recv_offsets, recv_tile = (
-        lax.all_to_all(
-            send_payload.reshape((row_count, capacity) + payload.shape[1:]),
-            "row",
-            split_axis=0,
-            concat_axis=0,
-            tiled=True,
-        ),
-        lax.all_to_all(
-            send_offsets.reshape((row_count, capacity) + offsets.shape[1:]),
-            "row",
-            split_axis=0,
-            concat_axis=0,
-            tiled=True,
-        ),
-        lax.all_to_all(send_tile, "row", split_axis=0, concat_axis=0, tiled=True),
-    )
-    contribution = grid_blocks(
-        recv_payload.reshape((slot_count,) + payload.shape[1:]),
-        recv_offsets.reshape((slot_count,) + offsets.shape[1:]),
-    )
-    slab_tiles = (
-        jnp.zeros((tiles_total, 2, TU, TV), jnp.float32)
-        .at[recv_tile.reshape(-1)]
-        .add(contribution, mode="drop")
-    )
-    slab_grid = (
-        slab_tiles.reshape(slab_rows // TU, GRID // TV, 2, TU, TV)
-        .transpose(2, 0, 3, 1, 4)
-        .reshape(2, slab_rows, GRID)
-    )
+    tile_row = jnp.broadcast_to(
+        tile_slot[0][:, None, None].astype(jnp.bfloat16), (block_count, 1, vis_count)
+    )
+    payload = jnp.concatenate(
+        [
+            vis_values[0],
+            kernel_u[0],
+            kernel_v[0],
+            offset_u[0][:, None, :].astype(jnp.bfloat16),
+            offset_v[0][:, None, :].astype(jnp.bfloat16),
+            tile_row,
+        ],
+        axis=1,
+    )
+    pick = (target[None, :] == jnp.arange(slot_count, dtype=jnp.int32)[:, None]).astype(
+        jnp.bfloat16
+    )
+    send = jnp.einsum(
+        "sb,bkn->skn", pick, payload, preferred_element_type=jnp.float32
+    )
+    empty = 1.0 - jnp.sum(pick.astype(jnp.float32), axis=1)
+    send = send.at[:, PAY_ROWS - 1, :].add(empty[:, None] * tiles_total)
+    send = send.astype(jnp.bfloat16)
+    recv = lax.all_to_all(
+        send.reshape((row_count, capacity) + payload.shape[1:]),
+        "row",
+        split_axis=0,
+        concat_axis=0,
+        tiled=True,
+    ).reshape((slot_count,) + payload.shape[1:])
+    tile_ids = recv[:, PAY_ROWS - 1, 0].astype(jnp.int32)
+    slab_grid = grid_into_slab(tile_ids, recv, slab_rows)
     spec_real, spec_imag = transform_last(slab_grid[0], slab_grid[1])
     spectrum = jnp.stack([spec_real, spec_imag]).reshape(2, slab_rows, row_count, GRID // row_count)
     image_scale = 1.0 / math.sqrt(block_count * row_count * vis_count)

time: 415 us -> 285 us (0.69)
  matrix products: 143 us -> 34 us
  other arithmetic: 45.4 us -> 12.7 us
  local copies, waits for them, and re-layouts: 32.1 us -> 14.4 us
  starting transfers between devices: 36.1 us -> 52.7 us
  Pallas kernels: 0 us -> 9.16 us
  waiting for transfers between devices: 137 us -> 142 us
    dot_general x1, matrix products: 109 us -> 0.6 us  [shards(): jnp.einsum('sb,bkn->skn', pick, payload, preferred_element_type=jnp.float32)]
    all_to_all x1, starting transfers between devices: 6.78 us -> 42.2 us  [shards(): lax.all_to_all(for_sending(spectrum), 'row', split_axis=2, concat_axis=1,...]
    scatter-add x1, other arithmetic: 35.4 us -> 0.1 us  [shards(): send = send.at[:, PAY_ROWS - 1, :].add(empty[:, None] * tiles_total)]
    all_to_all x3 -> x1, starting transfers between devices: 29.2 us -> 10.2 us  [shards(): lax.all_to_all(send.reshape((row_count, capacity) + payload.shape[1:]), '...]
    scatter x3 -> x0, local copies, waits for them, and re-layouts: 13.9 us -> none  [the longest x1 6.58 us: shards(): jnp.zeros((slot_count,) + offsets.shape[1:], jnp.int32).at[target]]
    pallas_call x0 -> x1, Pallas kernels: none -> 9.16 us  [grid_into_slab(): pl.pallas_call(grid_kernel, out_shape=jax.ShapeDtypeStruct((2, slab_rows,...]
    all_to_all x3 -> x1, waiting for transfers between devices: 24 us -> 30.4 us  [shards(): lax.all_to_all(send.reshape((row_count, capacity) + payload.shape[1:]), '...]
    convert_element_type x1 -> x2, other arithmetic: 0.02 us -> 5.85 us  [the longest x1 5.19 us: shards(): tile_ids = recv[:, PAY_ROWS - 1, 0].astype(jnp.int32)]
  transfers between devices with their start and end apart: 5 -> 3, of which waited for: 4 -> 3; matrix products, arithmetic and copies ran while one was open for 5% -> 0% of each run, Pallas kernels for 0% -> 0%
where the time goes in v1:
time: 285 us; the launch traced here: 280 us
  waiting for transfers between devices  142 us (50%)
  starting transfers between devices  52.7 us (18%)
  matrix products  34 us (12%)
  between operations  14.5 us (5%)
  local copies, waits for them, and re-layouts  14.4 us (5%)
  other arithmetic  12.7 us (4%)
  Pallas kernels  9.16 us (3%)
    reduce_scatter x1, waiting for transfers between devices, shards(): lax.psum_scatter(terms_all.astype(jnp.bfloat16), 'freq', scatter_dimensio...  67.2 us
    all_to_all x1, waiting for transfers between devices, shards(): lax.all_to_all(for_sending(spectrum), 'row', split_axis=2, concat_axis=1,...  44.8 us
    all_to_all x1, starting transfers between devices, shards(): lax.all_to_all(for_sending(spectrum), 'row', split_axis=2, concat_axis=1,...  42.2 us
    all_to_all x1, waiting for transfers between devices, shards(): lax.all_to_all(send.reshape((row_count, capacity) + payload.shape[1:]), '...  30.4 us
    all_to_all x1, starting transfers between devices, shards(): lax.all_to_all(send.reshape((row_count, capacity) + payload.shape[1:]), '...  10.2 us
    pallas_call x1, Pallas kernels, grid_into_slab(): pl.pallas_call(grid_kernel, out_shape=jax.ShapeDtypeStruct((2, slab_rows,...  9.16 us
    unnamed x8, local copies, waits for them, and re-layouts  5.85 us
  transfers between devices with their start and end apart: 3, of which 3 were waited for; matrix products, arithmetic and copies ran while one was open for 0% of the time, Pallas kernels for 0%

profile of v1, /device:TPU:6, one launch (start us, length us, event | category | flops | bytes accessed | tf_op | source)
XLA Modules:
  0.0 280.0 jit_solution(15754450019044787606)
XLA Ops:
  7.4 0.8 select_reduce_fusion
  10.4 0.9 bitcast_dynamic-update-slice_fusion.1
  11.3 0.9 bitcast_dynamic-update-slice_fusion
  12.2 0.8 bitcast_dynamic-update-slice_fusion.4
  13.0 0.8 bitcast_dynamic-update-slice_fusion.3
  14.8 1.3 copy.35
  16.0 10.2 %all-to-all-start = ((bf16[32,8,19,128]{3,1,2,0:T(8,128)(2,1)}), bf16[32,8,19,128]{3,1,2,0:T(8,128)(2,1)S(1)}, u32[]{:S(2)}, u32[]{:S(2)}) async-start(bf16[32,8,19,128]{3,1,2,0:T(8,128)(2,1)} %copy.35), calls=%async_computation | async-start | bytes 2490368 | tf_op jit(solution)/shard_map/all_to_all | solution.py:192
  26.4 30.4 %all-to-all-done = bf16[32,8,19,128]{3,1,2,0:T(8,128)(2,1)S(1)} async-done(((bf16[32,8,19,128]{3,1,2,0:T(8,128)(2,1)}), bf16[32,8,19,128]{3,1,2,0:T(8,128)(2,1)S(1)}, u32[]{:S(2)}, u32[]{:S(2)}) %all-to-all-start) | async-done | bytes 1245216 | tf_op jit(solution)/shard_map/all_to_all | solution.py:192
  57.1 5.2 %fusion.26.tile_ref = s32[256]{0:T(256)} fusion(bf16[256,19,128]{2,1,0:T(8,128)(2,1)S(1)} %bitcast.104), kind=kLoop, calls=%fused_computation.36 | loop fusion | flops 256 | bytes 1536 | tf_op jit(solution)/shard_map/convert_element_type | solution.py:199
  62.3 9.2 %shard_map.82 = f32[2,128,4096]{2,1,0:T(8,128)} custom-call(s32[256]{0:T(256)} %fusion.26.tile_ref, bf16[256,19,128]{2,1,0:T(8,128)(2,1)} %bitcast.105), custom_call_target="tpu_custom_call" | custom-call | tf_op jit(solution)/shard_map/pallas_call | solution.py:141
  71.5 2.5 slice_bitcast_fusion
  74.4 2.0 fusion.62
  76.4 2.0 fusion.68
  78.7 2.1 convolution_add_fusion.1
  80.8 2.5 subtract_bitcast_fusion
  83.3 3.3 %fusion.6 = f32[128,128,32]{1,0,2:T(8,128)S(1)} fusion(f32[128,32,128]{2,1,0:T(8,128)S(1)} %get-tuple-element.20), kind=kOutput, calls=%fused_computation.18 | convolution fusion | flops 805535744 | bytes 4194304 | tf_op jit(solution)/shard_map/rkb,bm->rmk/dot_general | solution.py:67
  86.6 3.2 %fusion.4 = f32[128,128,32]{1,0,2:T(8,128)S(1)} fusion(f32[128,32,128]{2,1,0:T(8,128)S(1)} %get-tuple-element.20), kind=kOutput, calls=%fused_computation.16 | convolution fusion | flops 805535744 | bytes 4194304 | tf_op jit(solution)/shard_map/rkb,bm->rmk/dot_general | solution.py:70
  89.8 3.3 %fusion.18 = bf16[128,128,32]{0,1,2:T(8,128)(2,1)S(1)} fusion(f32[128,128,32]{1,0,2:T(8,128)S(1)} %fusion.6, f32[128,32,128]{2,1,0:T(8,128)S(1)} %get-tuple-element.19), kind=kOutput, calls=%fused_computation.28 | convolution fusion | flops 806584320 | bytes 5242880 | tf_op jit(solution)/shard_map/rkb,bm->rmk/dot_general | solution.py:67
  93.8 3.3 %fusion.21 = bf16[128,128,32]{0,1,2:T(8,128)(2,1)S(1)} fusion(f32[128,128,32]{1,0,2:T(8,128)S(1)} %fusion.4, f32[128,32,128]{2,1,0:T(8,128)S(1)} %get-tuple-element.19), kind=kOutput, calls=%fused_computation.29 | convolution fusion | flops 806584320 | bytes 5242880 | tf_op jit(solution)/shard_map/rkb,bm->rmk/dot_general | solution.py:70
  98.0 2.8 copy.43
  100.7 42.2 %all-to-all-start.1 = ((bf16[2,128,32,128]{3,1,0,2:T(8,128)(2,1)}), bf16[2,128,32,128]{3,1,0,2:T(8,128)(2,1)S(1)}, u32[]{:S(2)}, u32[]{:S(2)}) async-start(bf16[2,128,32,128]{3,1,0,2:T(8,128)(2,1)} %copy.43), calls=%async_computation.1 | async-start | bytes 4194304 | tf_op jit(solution)/shard_map/all_to_all | solution.py:206
  144.2 44.8 %all-to-all-done.1 = bf16[2,128,32,128]{3,1,0,2:T(8,128)(2,1)S(1)} async-done(((bf16[2,128,32,128]{3,1,0,2:T(8,128)(2,1)}), bf16[2,128,32,128]{3,1,0,2:T(8,128)(2,1)S(1)}, u32[]{:S(2)}, u32[]{:S(2)}) %all-to-all-start.1) | async-done | bytes 2097184 | tf_op jit(solution)/shard_map/all_to_all | solution.py:206
  188.9 1.4 copy.76
  190.3 1.1 fusion.25
  191.4 1.0 fusion.24
  192.4 1.1 convolution_subtract_fusion
  193.5 2.2 multiply_subtract_fusion
  195.8 3.1 %fusion = f32[128,32,128]{2,0,1:T(8,128)S(1)} fusion(f32[32,128,128]{2,0,1:T(8,128)S(1)} %get-tuple-element.18), kind=kOutput, calls=%fused_computation.4 | convolution fusion | flops 805535744 | bytes 4194304 | tf_op jit(solution)/shard_map/kbc,bm->mkc/dot_general | solution.py:92
  198.9 3.3 %subtract_multiply_fusion = f32[128,32,128]{2,0,1:T(8,128)S(1)} fusion(f32[128,32,128]{2,0,1:T(8,128)S(1)} %fusion, f32[32,128,128]{2,0,1:T(8,128)S(1)} %get-tuple-element.17), kind=kOutput, calls=%fused_computation.9 | convolution fusion | flops 806584320 | bytes 6291456 | tf_op jit(solution)/shard_map/kbc,bm->mkc/dot_general | solution.py:92
  202.2 1.2 copy.49
  203.4 2.2 multiply_convert_fusion
  205.7 67.2 %reduce-scatter.2.cloned.1.call-done = bf16[3,256,128]{2,1,0:T(8,128)(2,1)} async-done(((bf16[3,4096,128]{2,1,0:T(8,128)(2,1)}), bf16[3,256,128]{2,1,0:T(8,128)(2,1)}) %reduce-scatter.2.cloned.1.call-update) | async-done | bytes 196624 | tf_op jit(solution)/shard_map/reduce_scatter | solution.py:216
  (25 shorter events, 7.3 us)
Async XLA Ops:
  16.0 40.7 %all-to-all-start = ((bf16[32,8,19,128]{3,1,2,0:T(8,128)(2,1)}), bf16[32,8,19,128]{3,1,2,0:T(8,128)(2,1)S(1)}, u32[]{:S(2)}, u32[]{:S(2)}) async-start(bf16[32,8,19,128]{3,1,2,0:T(8,128)(2,1)} %copy.35), calls=%async_computation | async-start | bytes 2490368 | tf_op jit(solution)/shard_map/all_to_all | solution.py:192
  57.1 5.2 %copy-start = (bf16[32,8,19,128]{3,2,1,0:T(8,128)(2,1)}, bf16[32,8,19,128]{3,2,1,0:T(8,128)(2,1)S(1)}, u32[]{:S(2)}) copy-start(bf16[32,8,19,128]{3,2,1,0:T(8,128)(2,1)S(1)} %copy.36) | copy-start | bytes 3735556
  100.7 88.2 %all-to-all-start.1 = ((bf16[2,128,32,128]{3,1,0,2:T(8,128)(2,1)}), bf16[2,128,32,128]{3,1,0,2:T(8,128)(2,1)S(1)}, u32[]{:S(2)}, u32[]{:S(2)}) async-start(bf16[2,128,32,128]{3,1,0,2:T(8,128)(2,1)} %copy.43), calls=%async_computation.1 | async-start | bytes 4194304 | tf_op jit(solution)/shard_map/all_to_all | solution.py:206
  143.0 129.9 %reduce-scatter.2.cloned.1.call-start = ((), (), s32[]{:S(2)}) async-start(), calls=%async_computation.3 | async-start | bytes 3342336 | tf_op jit(solution)/shard_map/reduce_scatter | solution.py:216
Sparse Core Ops, SparseCore 0:
  205.8 67.0 reduce-scatter.1

commit v2 on v1

--- a/solution.py
+++ b/solution.py
@@ -98,55 +98,70 @@
 PAY_ROWS = 19
 
 
-def grid_kernel(tile_ref, pay_ref, out_ref):
+GROUP = 8
+
+
+def grid_kernel(order_ref, tile_ref, count_ref, pay_ref, out_ref):
     tiles_total = out_ref.shape[1] // TU * (out_ref.shape[2] // TV)
     tile_cols = out_ref.shape[2] // TV
+    lanes = pay_ref.shape[2]
     out_ref[...] = jnp.zeros(out_ref.shape, jnp.float32)
-
-    def body(b, carry):
-        tile = tile_ref[b]
-
-        @pl.when(tile < tiles_total)
-        def _():
-            blk = pay_ref[b].astype(jnp.float32)
-            vis = blk[0:2]
-            ku = blk[2:9]
-            kv = blk[9:16]
-            ou = blk[16:17].astype(jnp.int32)
-            ov = blk[17:18].astype(jnp.int32)
-            du = lax.broadcasted_iota(jnp.int32, (TU, blk.shape[1]), 0) - ou
-            su = jnp.zeros((TU, blk.shape[1]), jnp.float32)
-            for t in range(7):
-                su = jnp.where(du == t, ku[t : t + 1], su)
-            left = jnp.concatenate([vis[0:1] * su, vis[1:2] * su], axis=0).astype(jnp.bfloat16)
-            dv = lax.broadcasted_iota(jnp.int32, (TV, blk.shape[1]), 0) - ov
-            sv = jnp.zeros((TV, blk.shape[1]), jnp.float32)
-            for t in range(7):
-                sv = jnp.where(dv == t, kv[t : t + 1], sv)
-            sv = sv.astype(jnp.bfloat16)
-            contrib = lax.dot_general(
-                left, sv, (((1,), (1,)), ((), ())), preferred_element_type=jnp.float32
-            )
+    du_base = lax.broadcasted_iota(jnp.int32, (TU, lanes), 0)
+    dv_base = lax.broadcasted_iota(jnp.int32, (TV, lanes), 0)
+
+    def one_block(slot):
+        blk = pay_ref[slot].astype(jnp.float32)
+        vis = blk[0:2]
+        ku = blk[2:9]
+        kv = blk[9:16]
+        ou = blk[16:17].astype(jnp.int32)
+        ov = blk[17:18].astype(jnp.int32)
+        du = du_base - ou
+        su = jnp.zeros((TU, lanes), jnp.float32)
+        for t in range(7):
+            su = jnp.where(du == t, ku[t : t + 1], su)
+        left = jnp.concatenate([vis[0:1] * su, vis[1:2] * su], axis=0).astype(jnp.bfloat16)
+        dv = dv_base - ov
+        sv = jnp.zeros((TV, lanes), jnp.float32)
+        for t in range(7):
+            sv = jnp.where(dv == t, kv[t : t + 1], sv)
+        sv = sv.astype(jnp.bfloat16)
+        return lax.dot_general(
+            left, sv, (((1,), (1,)), ((), ())), preferred_element_type=jnp.float32
+        )
+
+    def body(i, carry):
+        slots = [order_ref[i * GROUP + g] for g in range(GROUP)]
+        contribs = [one_block(s) for s in slots]
+        for s, contrib in zip(slots, contribs):
+            tile = jnp.minimum(tile_ref[s], tiles_total - 1)
             row0 = pl.multiple_of((tile // tile_cols) * TU, TU)
             col0 = pl.multiple_of((tile % tile_cols) * TV, TV)
-            for p in range(2):
-                out_ref[p, pl.ds(row0, TU), pl.ds(col0, TV)] += contrib[p * TU : (p + 1) * TU]
-
+
+            @pl.when(tile_ref[s] < tiles_total)
+            def _():
+                for p in range(2):
+                    out_ref[p, pl.ds(row0, TU), pl.ds(col0, TV)] += contrib[
+                        p * TU : (p + 1) * TU
+                    ]
         return carry
 
-    lax.fori_loop(0, pay_ref.shape[0], body, 0)
-
-
-def grid_into_slab(tile_ids, payload, slab_rows):
+    steps = (count_ref[0] + GROUP - 1) // GROUP
+    lax.fori_loop(0, steps, body, 0)
+
+
+def grid_into_slab(order, tile_ids, count, payload, slab_rows):
     return pl.pallas_call(
         grid_kernel,
         out_shape=jax.ShapeDtypeStruct((2, slab_rows, GRID), jnp.float32),
         in_specs=[
             pl.BlockSpec(memory_space=pltpu.SMEM),
+            pl.BlockSpec(memory_space=pltpu.SMEM),
+            pl.BlockSpec(memory_space=pltpu.SMEM),
             pl.BlockSpec(memory_space=pltpu.VMEM),
         ],
         out_specs=pl.BlockSpec(memory_space=pltpu.VMEM),
-    )(tile_ids, payload)
+    )(order, tile_ids, count, payload)
 
 
 def shards(
@@ -196,26 +211,43 @@
         concat_axis=0,
         tiled=True,
     ).reshape((slot_count,) + payload.shape[1:])
-    tile_ids = recv[:, PAY_ROWS - 1, 0].astype(jnp.int32)
-    slab_grid = grid_into_slab(tile_ids, recv, slab_rows)
+    tile_ids = jnp.max(recv[:, PAY_ROWS - 1, :].astype(jnp.float32), axis=1).astype(jnp.int32)
+    filled = tile_ids < tiles_total
+    filled_i = filled.astype(jnp.int32)
+    count = jnp.sum(filled_i)
+    place = jnp.where(
+        filled, jnp.cumsum(filled_i) - 1, count + jnp.cumsum(1 - filled_i) - 1
+    )
+    order = jnp.zeros((slot_count,), jnp.int32).at[place].set(
+        jnp.arange(slot_count, dtype=jnp.int32)
+    )
+    slab_grid = grid_into_slab(order, tile_ids, count.reshape(1), recv, slab_rows)
     spec_real, spec_imag = transform_last(slab_grid[0], slab_grid[1])
-    spectrum = jnp.stack([spec_real, spec_imag]).reshape(2, slab_rows, row_count, GRID // row_count)
+    halves = 2
+    half_cols = GRID // row_count // halves
+    spectrum = jnp.stack([spec_real, spec_imag]).reshape(
+        2, slab_rows, row_count, halves, half_cols
+    )
     image_scale = 1.0 / math.sqrt(block_count * row_count * vis_count)
     offset_freq = (channel_freq[0] - 1.284) / 0.428
     weights = jnp.stack([jnp.ones_like(offset_freq), offset_freq, offset_freq * offset_freq])
-    received = lax.all_to_all(
-        for_sending(spectrum), "row", split_axis=2, concat_axis=1, tiled=True
-    ).astype(spectrum.dtype)
-    width_here = received.shape[2] * received.shape[3]
-    real_cols = received[0].reshape(GRID, width_here)
-    imag_cols = received[1].reshape(GRID, width_here)
-    dirty_image = transform_first_real(real_cols, imag_cols) * image_scale
-    taylor_terms = (weights[:, None, None] * dirty_image[None]).astype(jnp.bfloat16)
-    terms_all = taylor_terms.reshape(3, GRID, received.shape[2], received.shape[3])
-    terms_all = terms_all.reshape(3, GRID, GRID // row_count).astype(jnp.float32)
-    summed = lax.psum_scatter(
-        terms_all.astype(jnp.bfloat16), "freq", scatter_dimension=1, tiled=True
-    )
+    pieces = []
+    for h in range(halves):
+        received = lax.all_to_all(
+            for_sending(spectrum[:, :, :, h, :]), "row", split_axis=2, concat_axis=1, tiled=True
+        )
+        if h > 0:
+            received = lax.optimization_barrier((gate, received))[1]
+        received = received.astype(jnp.float32)
+        real_cols = received[0].reshape(GRID, half_cols)
+        imag_cols = received[1].reshape(GRID, half_cols)
+        dirty_image = transform_first_real(real_cols, imag_cols) * image_scale
+        taylor_terms = (weights[:, None, None] * dirty_image[None]).astype(jnp.bfloat16)
+        pieces.append(
+            lax.psum_scatter(taylor_terms, "freq", scatter_dimension=1, tiled=True)
+        )
+        gate = pieces[-1]
+    summed = jnp.concatenate(pieces, axis=2)
     return summed
 
 

time: 285 us -> 309 us (1.084)
  starting transfers between devices: 52.7 us -> 15 us
  blocking collectives: 0 us -> 29.7 us
  Pallas kernels: 9.16 us -> 21.6 us
  waiting for transfers between devices: 142 us -> 152 us
  local copies, waits for them, and re-layouts: 14.4 us -> 22.3 us
    all_to_all x1, starting transfers between devices: 42.2 us -> 4.71 us  [shards(): lax.all_to_all(for_sending(spectrum[:, :, :, h, :]), 'row', split_axis=2,...]
    reduce_scatter x1 -> x2, waiting for transfers between devices: 67.2 us -> 99.2 us  [shards(): lax.psum_scatter(taylor_terms, 'freq', scatter_dimension=1, tiled=True)]
    all_to_all x0 -> x1, blocking collectives: none -> 29.7 us  [shards(): lax.all_to_all(for_sending(spectrum[:, :, :, h, :]), 'row', split_axis=2,...]
    all_to_all x1, waiting for transfers between devices: 44.8 us -> 22.5 us  [shards(): lax.all_to_all(for_sending(spectrum[:, :, :, h, :]), 'row', split_axis=2,...]
    pallas_call x1, Pallas kernels: 9.16 us -> 21.6 us  [grid_into_slab(): pl.pallas_call(grid_kernel, out_shape=jax.ShapeDtypeStruct((2, slab_rows,...]
    dot_general x2 -> x0, matrix products: 6.43 us -> none  [the longest x1 3.28 us: transform_first_real(): product('kbc,bm->mkc', twist_real, cos_inner)]
    unnamed x0 -> x4, matrix products: none -> 4.92 us
    convert_element_type x1, other arithmetic: 5.19 us -> 0.59 us  [shards(): jnp.max(recv[:, PAY_ROWS - 1, :].astype(jnp.float32), axis=1)]
  transfers between devices with their start and end apart: 3 -> 4, of which waited for: 3 -> 4; matrix products, arithmetic and copies ran while one was open for 0% -> 0% of each run, Pallas kernels for 0% -> 0%
where the time goes in v2:
time: 309 us; the launch traced here: 304 us
  waiting for transfers between devices  152 us (49%)
  matrix products  32.8 us (11%)
  blocking collectives  29.7 us (10%)
  local copies, waits for them, and re-layouts  22.3 us (7%)
  Pallas kernels  21.6 us (7%)
  other arithmetic  15.6 us (5%)
  starting transfers between devices  15 us (5%)
  between operations  14.6 us (5%)
    reduce_scatter x2, waiting for transfers between devices, shards(): lax.psum_scatter(taylor_terms, 'freq', scatter_dimension=1, tiled=True)  99.2 us
    all_to_all x1, waiting for transfers between devices, shards(): lax.all_to_all(send.reshape((row_count, capacity) + payload.shape[1:]), '...  30.4 us
    all_to_all x1, blocking collectives, shards(): lax.all_to_all(for_sending(spectrum[:, :, :, h, :]), 'row', split_axis=2,...  29.7 us
    all_to_all x1, waiting for transfers between devices, shards(): lax.all_to_all(for_sending(spectrum[:, :, :, h, :]), 'row', split_axis=2,...  22.5 us
    pallas_call x1, Pallas kernels, grid_into_slab(): pl.pallas_call(grid_kernel, out_shape=jax.ShapeDtypeStruct((2, slab_rows,...  21.6 us
    all_to_all x1, starting transfers between devices, shards(): lax.all_to_all(send.reshape((row_count, capacity) + payload.shape[1:]), '...  10.2 us
    unnamed x15, local copies, waits for them, and re-layouts  7.26 us
  transfers between devices with their start and end apart: 4, of which 4 were waited for; matrix products, arithmetic and copies ran while one was open for 0% of the time, Pallas kernels for 0%

profile of v2, /device:TPU:6, one launch (start us, length us, event | category | flops | bytes accessed | tf_op | source)
XLA Modules:
  0.0 303.8 jit_solution(1465875217416971485)
XLA Ops:
  14.8 1.3 copy.66
  16.0 10.2 %all-to-all-start = ((bf16[32,8,19,128]{3,1,2,0:T(8,128)(2,1)}), bf16[32,8,19,128]{3,1,2,0:T(8,128)(2,1)S(1)}, u32[]{:S(2)}, u32[]{:S(2)}) async-start(bf16[32,8,19,128]{3,1,2,0:T(8,128)(2,1)} %copy.66), calls=%async_computation | async-start | bytes 2490368 | tf_op jit(solution)/shard_map/all_to_all | solution.py:207
  26.4 30.4 %all-to-all-done = bf16[32,8,19,128]{3,1,2,0:T(8,128)(2,1)S(1)} async-done(((bf16[32,8,19,128]{3,1,2,0:T(8,128)(2,1)}), bf16[32,8,19,128]{3,1,2,0:T(8,128)(2,1)S(1)}, u32[]{:S(2)}, u32[]{:S(2)}) %all-to-all-start) | async-done | bytes 1245216 | tf_op jit(solution)/shard_map/all_to_all | solution.py:207
  61.2 1.9 scatter_custom_fusion.order_ref
  63.2 21.6 %shard_map.82 = f32[2,128,4096]{2,1,0:T(8,128)} custom-call(s32[256]{0:T(256)} %scatter_custom_fusion.order_ref, s32[256]{0:T(256)} %convert_convert_fusion.tile_ref, s32[1]{0:T(128)} %bitcast.16.count_ref, bf16[256,19,128]{2,1,0:T(8,128)(2,1)} %bitcast.173), custom_call_target="tpu_custom_call" | custom-call | tf_op jit(solution)/shard_map/pallas_call | solution.py:154
  84.8 2.5 slice_bitcast_fusion
  87.7 2.0 fusion.56
  89.7 2.0 fusion.65
  92.0 2.0 convolution_add_fusion
  94.0 2.5 subtract_bitcast_fusion.1
  96.4 3.5 %fusion.2 = f32[128,128,32]{1,0,2:T(8,128)S(1)} fusion(f32[128,32,128]{2,1,0:T(8,128)S(1)} %get-tuple-element.20), kind=kOutput, calls=%fused_computation.12 | convolution fusion | flops 805535744 | bytes 4194304 | tf_op jit(solution)/shard_map/rkb,bm->rmk/dot_general | solution.py:67
  99.9 3.2 %fusion = f32[128,128,32]{1,0,2:T(8,128)S(1)} fusion(f32[128,32,128]{2,1,0:T(8,128)S(1)} %get-tuple-element.20), kind=kOutput, calls=%fused_computation.10 | convolution fusion | flops 805535744 | bytes 4194304 | tf_op jit(solution)/shard_map/rkb,bm->rmk/dot_general | solution.py:70
  103.2 3.4 %subtract_bitcast_fusion = bf16[128,128,32]{0,1,2:T(8,128)(2,1)S(1)} fusion(f32[128,128,32]{1,0,2:T(8,128)S(1)} %fusion.2, f32[128,32,128]{2,1,0:T(8,128)S(1)} %get-tuple-element.19), kind=kOutput, calls=%fused_computation.7 | convolution fusion | flops 806584320 | bytes 5242880 | tf_op jit(solution)/shard_map/rkb,bm->rmk/dot_general | solution.py:67
  107.2 3.4 %add_bitcast_fusion = bf16[128,128,32]{0,1,2:T(8,128)(2,1)S(1)} fusion(f32[128,128,32]{1,0,2:T(8,128)S(1)} %fusion, f32[128,32,128]{2,1,0:T(8,128)S(1)} %get-tuple-element.19), kind=kOutput, calls=%fused_computation.6 | convolution fusion | flops 806584320 | bytes 5242880 | tf_op jit(solution)/shard_map/rkb,bm->rmk/dot_general | solution.py:70
  110.6 1.1 copy.77
  111.9 1.2 slice_bitcast_fusion.2
  113.0 1.1 copy.78
  114.1 4.7 %all-to-all-start.1 = ((bf16[2,128,32,64]{1,3,0,2:T(8,128)(2,1)}), bf16[2,128,32,64]{1,3,0,2:T(8,128)(2,1)S(1)}, u32[]{:S(2)}, u32[]{:S(2)}) async-start(bf16[2,128,32,64]{1,3,0,2:T(8,128)(2,1)} %copy.78), calls=%async_computation.1 | async-start | bytes 2097152 | tf_op jit(solution)/shard_map/all_to_all | solution.py:236
  119.6 22.5 %all-to-all-done.1 = bf16[2,128,32,64]{1,3,0,2:T(8,128)(2,1)S(1)} async-done(((bf16[2,128,32,64]{1,3,0,2:T(8,128)(2,1)}), bf16[2,128,32,64]{1,3,0,2:T(8,128)(2,1)S(1)}, u32[]{:S(2)}, u32[]{:S(2)}) %all-to-all-start.1) | async-done | bytes 1048608 | tf_op jit(solution)/shard_map/all_to_all | solution.py:236
  146.1 1.2 fusion.34
  148.0 1.2 fusion.40
  149.4 1.8 copy.82
  151.3 2.2 multiply_convert_fusion.1
  153.6 1.1 copy-done.1
  154.9 29.7 %all_to_all.38 = bf16[2,128,32,64]{1,3,0,2:T(8,128)(2,1)S(1)} all-to-all(bf16[2,128,32,64]{1,3,0,2:T(8,128)(2,1)S(1)} %copy.83), channel_id=1, replica_groups=mesh['freq'=16,'row'=32] {'row'}, dimensions={2} | all-to-all | bytes 2097152 | tf_op jit(solution)/shard_map/all_to_all | solution.py:236
  184.7 36.3 %reduce-scatter.3.cloned.1.call-done = bf16[3,256,64]{2,1,0:T(8,128)(2,1)} async-done(((bf16[3,4096,64]{2,1,0:T(8,128)(2,1)}), bf16[3,256,64]{2,1,0:T(8,128)(2,1)}) %reduce-scatter.3.cloned.1.call-update) | async-done | bytes 98320 | tf_op jit(solution)/shard_map/reduce_scatter | solution.py:247
  224.7 1.2 fusion.36
  226.5 1.2 fusion.42
  228.0 1.8 copy.87
  229.8 2.2 multiply_convert_fusion
  232.1 62.9 %reduce-scatter.5.cloned.1.call-done = bf16[3,256,64]{2,1,0:T(8,128)(2,1)} async-done(((bf16[3,4096,64]{2,1,0:T(8,128)(2,1)}), bf16[3,256,64]{2,1,0:T(8,128)(2,1)}) %reduce-scatter.5.cloned.1.call-update) | async-done | bytes 98320 | tf_op jit(solution)/shard_map/reduce_scatter | solution.py:247
  295.0 1.7 pad_maximum_fusion
  (69 shorter events, 24.1 us)
Async XLA Ops:
  16.0 40.7 %all-to-all-start = ((bf16[32,8,19,128]{3,1,2,0:T(8,128)(2,1)}), bf16[32,8,19,128]{3,1,2,0:T(8,128)(2,1)S(1)}, u32[]{:S(2)}, u32[]{:S(2)}) async-start(bf16[32,8,19,128]{3,1,2,0:T(8,128)(2,1)} %copy.66), calls=%async_computation | async-start | bytes 2490368 | tf_op jit(solution)/shard_map/all_to_all | solution.py:207
  57.1 6.0 %copy-start = (bf16[32,8,19,128]{3,2,1,0:T(8,128)(2,1)}, bf16[32,8,19,128]{3,2,1,0:T(8,128)(2,1)S(1)}, u32[]{:S(2)}) copy-start(bf16[32,8,19,128]{3,2,1,0:T(8,128)(2,1)S(1)} %copy.67) | copy-start | bytes 3735556
  114.1 28.0 %all-to-all-start.1 = ((bf16[2,128,32,64]{1,3,0,2:T(8,128)(2,1)}), bf16[2,128,32,64]{1,3,0,2:T(8,128)(2,1)S(1)}, u32[]{:S(2)}, u32[]{:S(2)}) async-start(bf16[2,128,32,64]{1,3,0,2:T(8,128)(2,1)} %copy.78), calls=%async_computation.1 | async-start | bytes 2097152 | tf_op jit(solution)/shard_map/all_to_all | solution.py:236
  118.8 102.2 %reduce-scatter.3.cloned.1.call-start = ((), (), s32[]{:S(2)}) async-start(), calls=%async_computation.5 | async-start | bytes 3342336 | tf_op jit(solution)/shard_map/reduce_scatter | solution.py:247
  153.5 1.2 copy-start.1
  153.6 141.4 %reduce-scatter.5.cloned.1.call-start = ((), (), s32[]{:S(2)}) async-start(), calls=%async_computation.6 | async-start | bytes 3342336 | tf_op jit(solution)/shard_map/reduce_scatter | solution.py:247
  232.1 62.9 %copy-start.2 = (bf16[3,256,64]{2,1,0:T(8,128)(2,1)S(1)}, bf16[3,256,64]{2,1,0:T(8,128)(2,1)}, u32[]{:S(2)}) copy-start(bf16[3,256,64]{2,1,0:T(8,128)(2,1)} %reduce-scatter.3.cloned.1.call-done) | copy-start | bytes 294916
Sparse Core Ops, SparseCore 0:
  153.7 67.2 reduce-scatter.2
  232.2 62.7 reduce-scatter.4

commit v3 on v2

--- a/solution.py
+++ b/solution.py
@@ -4,7 +4,7 @@
 import jax
 import jax.numpy as jnp
 from jax import lax
-from jax.sharding import PartitionSpec as P
+from jax.sharding import Mesh, PartitionSpec as P
 from jax.experimental import pallas as pl
 from jax.experimental.pallas import tpu as pltpu
 
@@ -223,48 +223,48 @@
     )
     slab_grid = grid_into_slab(order, tile_ids, count.reshape(1), recv, slab_rows)
     spec_real, spec_imag = transform_last(slab_grid[0], slab_grid[1])
-    halves = 2
-    half_cols = GRID // row_count // halves
-    spectrum = jnp.stack([spec_real, spec_imag]).reshape(
-        2, slab_rows, row_count, halves, half_cols
-    )
+    spectrum = jnp.stack([spec_real, spec_imag]).reshape(2, slab_rows, row_count, GRID // row_count)
     image_scale = 1.0 / math.sqrt(block_count * row_count * vis_count)
     offset_freq = (channel_freq[0] - 1.284) / 0.428
     weights = jnp.stack([jnp.ones_like(offset_freq), offset_freq, offset_freq * offset_freq])
-    pieces = []
-    for h in range(halves):
-        received = lax.all_to_all(
-            for_sending(spectrum[:, :, :, h, :]), "row", split_axis=2, concat_axis=1, tiled=True
-        )
-        if h > 0:
-            received = lax.optimization_barrier((gate, received))[1]
-        received = received.astype(jnp.float32)
-        real_cols = received[0].reshape(GRID, half_cols)
-        imag_cols = received[1].reshape(GRID, half_cols)
-        dirty_image = transform_first_real(real_cols, imag_cols) * image_scale
-        taylor_terms = (weights[:, None, None] * dirty_image[None]).astype(jnp.bfloat16)
-        pieces.append(
-            lax.psum_scatter(taylor_terms, "freq", scatter_dimension=1, tiled=True)
-        )
-        gate = pieces[-1]
-    summed = jnp.concatenate(pieces, axis=2)
+    received = lax.all_to_all(
+        for_sending(spectrum), "row", split_axis=2, concat_axis=1, tiled=True
+    ).astype(spectrum.dtype)
+    width_here = received.shape[2] * received.shape[3]
+    real_cols = received[0].reshape(GRID, width_here)
+    imag_cols = received[1].reshape(GRID, width_here)
+    dirty_image = transform_first_real(real_cols, imag_cols) * image_scale
+    taylor_terms = (weights[:, None, None] * dirty_image[None]).astype(jnp.bfloat16)
+    chips = lax.axis_size("z")
+    pair = lax.axis_size("core")
+    core = lax.axis_index("core")
+    terms = taylor_terms.astype(jnp.float32).reshape(3, chips, pair, GRID // chips // pair, width_here)
+    keep = lax.dynamic_index_in_dim(terms, core, axis=2, keepdims=False)
+    give = lax.dynamic_index_in_dim(terms, pair - 1 - core, axis=2, keepdims=False)
+    got = lax.ppermute(give, "core", [(0, 1), (1, 0)])
+    partial_sum = (keep + got).astype(jnp.bfloat16)
+    summed = lax.psum_scatter(partial_sum, "z", scatter_dimension=1, tiled=True)
+    summed = summed.reshape(3, GRID // chips // pair, width_here)
     return summed
 
 
 def solution(mesh):
+    chips = mesh.shape["freq"] // 2
+    split = Mesh(mesh.devices.reshape(chips, 2, mesh.shape["row"]), ("z", "core", "row"))
+    freq = ("z", "core")
     return jax.shard_map(
         shards,
-        mesh=mesh,
+        mesh=split,
         in_specs=(
-            P("freq", "row", None, None),
-            P("freq", "row", None, None),
-            P("freq", "row", None, None),
-            P("freq", "row", None),
-            P("freq", "row", None),
-            P("freq", "row", None),
-            P("freq", "row"),
-            P("freq"),
+            P(freq, "row", None, None),
+            P(freq, "row", None, None),
+            P(freq, "row", None, None),
+            P(freq, "row", None),
+            P(freq, "row", None),
+            P(freq, "row", None),
+            P(freq, "row"),
+            P(freq),
         ),
-        out_specs=P(None, "freq", "row"),
+        out_specs=P(None, freq, "row"),
         check_vma=False,
     )

time: 309 us -> 257 us (0.83)
  blocking collectives: 29.7 us -> 0 us
  waiting for transfers between devices: 152 us -> 129 us
  starting transfers between devices: 15 us -> 33.8 us
  Pallas kernels: 21.6 us -> 7.39 us
    reduce_scatter x2 -> x1, waiting for transfers between devices: 99.2 us -> 46.7 us  [shards(): summed = lax.psum_scatter(partial_sum, 'z', scatter_dimension=1, tiled=True)]
    all_to_all x1 -> x0, blocking collectives: 29.7 us -> none  [shards(): lax.all_to_all(for_sending(spectrum[:, :, :, h, :]), 'row', split_axis=2,...]
    all_to_all x1, waiting for transfers between devices: 22.5 us -> 46.1 us  [shards(): lax.all_to_all(for_sending(spectrum), 'row', split_axis=2, concat_axis=1,...]
    all_to_all x1, starting transfers between devices: 4.71 us -> 21.4 us  [shards(): lax.all_to_all(for_sending(spectrum), 'row', split_axis=2, concat_axis=1,...]
    pallas_call x1, Pallas kernels: 21.6 us -> 7.39 us  [grid_into_slab(): pl.pallas_call(grid_kernel, out_shape=jax.ShapeDtypeStruct((2, slab_rows,...]
    dot_general x0 -> x2, matrix products: none -> 6.7 us  [the longest x1 3.55 us: transform_first_real(): product('kbc,bm->mkc', twist_real, cos_inner)]
    ppermute x0 -> x1, waiting for transfers between devices: none -> 5.76 us  [shards(): got = lax.ppermute(give, 'core', [(0, 1), (1, 0)])]
    unnamed x4 -> x0, matrix products: 4.92 us -> none
where the time goes in v3:
time: 257 us; the launch traced here: 253 us
  waiting for transfers between devices  129 us (50%)
  matrix products  34.3 us (13%)
  starting transfers between devices  33.8 us (13%)
  local copies, waits for them, and re-layouts  19.4 us (8%)
  between operations  14.6 us (6%)
  other arithmetic  14.2 us (6%)
  Pallas kernels  7.39 us (3%)
    reduce_scatter x1, waiting for transfers between devices, shards(): summed = lax.psum_scatter(partial_sum, 'z', scatter_dimension=1, tiled=True)  46.7 us
    all_to_all x1, waiting for transfers between devices, shards(): lax.all_to_all(for_sending(spectrum), 'row', split_axis=2, concat_axis=1,...  46.1 us
    all_to_all x1, waiting for transfers between devices, shards(): lax.all_to_all(send.reshape((row_count, capacity) + payload.shape[1:]), '...  30.4 us
    all_to_all x1, starting transfers between devices, shards(): lax.all_to_all(for_sending(spectrum), 'row', split_axis=2, concat_axis=1,...  21.4 us
    all_to_all x1, starting transfers between devices, shards(): lax.all_to_all(send.reshape((row_count, capacity) + payload.shape[1:]), '...  10.2 us
    unnamed x10, local copies, waits for them, and re-layouts  8.28 us
    pallas_call x1, Pallas kernels, grid_into_slab(): pl.pallas_call(grid_kernel, out_shape=jax.ShapeDtypeStruct((2, slab_rows,...  7.39 us
    ppermute x1, waiting for transfers between devices, shards(): got = lax.ppermute(give, 'core', [(0, 1), (1, 0)])  5.76 us
  transfers between devices with their start and end apart: 4, of which 4 were waited for; matrix products, arithmetic and copies ran while one was open for 0% of the time, Pallas kernels for 0%

profile of v3, /device:TPU:6, one launch (start us, length us, event | category | flops | bytes accessed | tf_op | source)
XLA Modules:
  0.0 252.7 jit_solution(15322859436776552981)
XLA Ops:
  11.3 0.9 bitcast_dynamic-update-slice_fusion
  14.8 1.3 copy.36
  16.0 10.2 %all-to-all-start = ((bf16[32,8,19,128]{3,1,2,0:T(8,128)(2,1)}), bf16[32,8,19,128]{3,1,2,0:T(8,128)(2,1)S(1)}, u32[]{:S(2)}, u32[]{:S(2)}) async-start(bf16[32,8,19,128]{3,1,2,0:T(8,128)(2,1)} %copy.36), calls=%async_computation | async-start | bytes 2490368 | tf_op jit(solution)/shard_map/all_to_all | solution.py:207
  26.4 30.4 %all-to-all-done = bf16[32,8,19,128]{3,1,2,0:T(8,128)(2,1)S(1)} async-done(((bf16[32,8,19,128]{3,1,2,0:T(8,128)(2,1)}), bf16[32,8,19,128]{3,1,2,0:T(8,128)(2,1)S(1)}, u32[]{:S(2)}, u32[]{:S(2)}) %all-to-all-start) | async-done | bytes 1245216 | tf_op jit(solution)/shard_map/all_to_all | solution.py:207
  57.1 1.0 slice_reduce_fusion
  61.2 1.9 scatter_custom_fusion.order_ref
  63.2 7.4 %shard_map.82 = f32[2,128,4096]{2,1,0:T(8,128)} custom-call(s32[256]{0:T(256)} %scatter_custom_fusion.order_ref, s32[256]{0:T(256)} %convert_convert_fusion.tile_ref, s32[1]{0:T(128)} %bitcast.16.count_ref, bf16[256,19,128]{2,1,0:T(8,128)(2,1)} %bitcast.121), custom_call_target="tpu_custom_call" | custom-call | tf_op jit(solution)/shard_map/pallas_call | solution.py:154
  70.6 2.5 slice_bitcast_fusion
  73.4 2.0 fusion.63
  75.4 2.0 fusion.69
  77.8 2.1 convolution_add_fusion.1
  79.8 2.5 subtract_bitcast_fusion
  82.3 3.3 %fusion.6 = f32[128,128,32]{1,0,2:T(8,128)S(1)} fusion(f32[128,32,128]{2,1,0:T(8,128)S(1)} %get-tuple-element.20), kind=kOutput, calls=%fused_computation.21 | convolution fusion | flops 805535744 | bytes 4194304 | tf_op jit(solution)/shard_map/rkb,bm->rmk/dot_general | solution.py:70
  85.7 3.2 %fusion.8 = f32[128,128,32]{1,0,2:T(8,128)S(1)} fusion(f32[128,32,128]{2,1,0:T(8,128)S(1)} %get-tuple-element.20), kind=kOutput, calls=%fused_computation.23 | convolution fusion | flops 805535744 | bytes 4194304 | tf_op jit(solution)/shard_map/rkb,bm->rmk/dot_general | solution.py:67
  88.9 3.3 %fusion.23 = bf16[128,128,32]{0,1,2:T(8,128)(2,1)S(1)} fusion(f32[128,128,32]{1,0,2:T(8,128)S(1)} %fusion.6, f32[128,32,128]{2,1,0:T(8,128)S(1)} %get-tuple-element.19), kind=kOutput, calls=%fused_computation.34 | convolution fusion | flops 806584320 | bytes 5242880 | tf_op jit(solution)/shard_map/rkb,bm->rmk/dot_general | solution.py:70
  92.8 3.3 %fusion.20 = bf16[128,128,32]{0,1,2:T(8,128)(2,1)S(1)} fusion(f32[128,128,32]{1,0,2:T(8,128)S(1)} %fusion.8, f32[128,32,128]{2,1,0:T(8,128)S(1)} %get-tuple-element.19), kind=kOutput, calls=%fused_computation.33 | convolution fusion | flops 806584320 | bytes 5242880 | tf_op jit(solution)/shard_map/rkb,bm->rmk/dot_general | solution.py:67
  97.0 2.8 %copy.44 = bf16[2,128,32,128]{3,1,0,2:T(8,128)(2,1)} copy(bf16[2,128,32,128]{1,3,2,0:T(8,128)(2,1)S(1)} %pad_maximum_fusion) | data formatting | bytes 4194304 | tf_op jit(solution)/shard_map/stack | solution.py:226
  99.8 21.4 %all-to-all-start.1 = ((bf16[2,128,32,128]{3,1,0,2:T(8,128)(2,1)}), bf16[2,128,32,128]{3,1,0,2:T(8,128)(2,1)S(1)}, u32[]{:S(2)}, u32[]{:S(2)}) async-start(bf16[2,128,32,128]{3,1,0,2:T(8,128)(2,1)} %copy.44), calls=%async_computation.1 | async-start | bytes 4194304 | tf_op jit(solution)/shard_map/all_to_all | solution.py:230
  122.4 46.1 %all-to-all-done.1 = bf16[2,128,32,128]{3,1,0,2:T(8,128)(2,1)S(1)} async-done(((bf16[2,128,32,128]{3,1,0,2:T(8,128)(2,1)}), bf16[2,128,32,128]{3,1,0,2:T(8,128)(2,1)S(1)}, u32[]{:S(2)}, u32[]{:S(2)}) %all-to-all-start.1) | async-done | bytes 2097184 | tf_op jit(solution)/shard_map/all_to_all | solution.py:230
  168.5 1.4 copy.80
  169.9 1.0 fusion.26
  170.9 1.1 fusion.27
  172.0 1.1 convolution_subtract_fusion
  173.1 2.2 multiply_subtract_fusion
  175.3 3.1 %fusion.2 = f32[128,32,128]{2,0,1:T(8,128)S(1)} fusion(f32[32,128,128]{2,0,1:T(8,128)S(1)} %get-tuple-element.18), kind=kOutput, calls=%fused_computation.9 | convolution fusion | flops 805535744 | bytes 4194304 | tf_op jit(solution)/shard_map/kbc,bm->mkc/dot_general | solution.py:92
  178.5 3.6 %subtract_multiply_fusion = f32[128,32,128]{2,0,1:T(8,128)S(1)} fusion(f32[128,32,128]{2,0,1:T(8,128)S(1)} %fusion.2, f32[32,128,128]{2,0,1:T(8,128)S(1)} %get-tuple-element.17), kind=kOutput, calls=%fused_computation.14 | convolution fusion | flops 806584320 | bytes 6291456 | tf_op jit(solution)/shard_map/kbc,bm->mkc/dot_general | solution.py:92
  182.0 1.2 copy.50
  184.3 2.4 copy-done
  186.7 1.9 collective-permute-start
  188.7 5.8 %collective-permute-done = f32[3,8,256,128]{3,2,0,1:T(8,128)} collective-permute-done((f32[3,8,256,128]{3,2,0,1:T(8,128)S(1)}, f32[3,8,256,128]{3,2,0,1:T(8,128)}, u32[]{:S(2)}, u32[]{:S(2)}) %collective-permute-start) | collective-permute-done | bytes 3145760 | tf_op jit(solution)/shard_map/ppermute | solution.py:244
  194.4 4.4 %fusion.1 = bf16[3,8,256,128]{3,2,0,1:T(8,128)(2,1)} fusion(f32[3,8,256,128]{3,2,0,1:T(8,128)} %collective-permute-done, f32[3,8,2,256,128]{4,3,0,1,2:T(8,128)} %copy-done, s32[]{:T(128)S(6)} %select_n.110), kind=kLoop, calls=%fused_computation.4 | loop fusion | flops 1572864 | bytes 7864324 | tf_op jit(solution)/shard_map/convert_element_type | solution.py:245
  198.9 46.7 %reduce-scatter.2.cloned.1.call-done = bf16[3,1,256,128]{3,2,0,1:T(8,128)(2,1)} async-done(((bf16[3,8,256,128]{3,2,0,1:T(8,128)(2,1)}), bf16[3,1,256,128]{3,2,0,1:T(8,128)(2,1)}) %reduce-scatter.2.cloned.1.call-update) | async-done | bytes 196624 | tf_op jit(solution)/shard_map/reduce_scatter | solution.py:246
  (48 shorter events, 14.6 us)
Async XLA Ops:
  16.0 40.7 %all-to-all-start = ((bf16[32,8,19,128]{3,1,2,0:T(8,128)(2,1)}), bf16[32,8,19,128]{3,1,2,0:T(8,128)(2,1)S(1)}, u32[]{:S(2)}, u32[]{:S(2)}) async-start(bf16[32,8,19,128]{3,1,2,0:T(8,128)(2,1)} %copy.36), calls=%async_computation | async-start | bytes 2490368 | tf_op jit(solution)/shard_map/all_to_all | solution.py:207
  57.1 6.0 %copy-start.1 = (bf16[32,8,19,128]{3,2,1,0:T(8,128)(2,1)}, bf16[32,8,19,128]{3,2,1,0:T(8,128)(2,1)S(1)}, u32[]{:S(2)}) copy-start(bf16[32,8,19,128]{3,2,1,0:T(8,128)(2,1)S(1)} %copy.37) | copy-start | bytes 3735556
  99.8 68.7 %all-to-all-start.1 = ((bf16[2,128,32,128]{3,1,0,2:T(8,128)(2,1)}), bf16[2,128,32,128]{3,1,0,2:T(8,128)(2,1)S(1)}, u32[]{:S(2)}, u32[]{:S(2)}) async-start(bf16[2,128,32,128]{3,1,0,2:T(8,128)(2,1)} %copy.44), calls=%async_computation.1 | async-start | bytes 4194304 | tf_op jit(solution)/shard_map/all_to_all | solution.py:230
  121.2 124.3 %reduce-scatter.2.cloned.1.call-start = ((), (), s32[]{:S(2)}) async-start(), calls=%async_computation.3 | async-start | bytes 1769472 | tf_op jit(solution)/shard_map/reduce_scatter | solution.py:246
  184.1 2.7 %copy-start = (f32[3,8,2,256,128]{4,3,0,1,2:T(8,128)}, f32[3,8,2,256,128]{4,3,0,1,2:T(8,128)S(1)}, u32[]{:S(2)}) copy-start(f32[3,8,2,256,128]{4,3,0,1,2:T(8,128)S(1)} %fusion) | copy-start | bytes 18874372
  186.7 7.7 %collective-permute-start = (f32[3,8,256,128]{3,2,0,1:T(8,128)S(1)}, f32[3,8,256,128]{3,2,0,1:T(8,128)}, u32[]{:S(2)}, u32[]{:S(2)}) collective-permute-start(f32[3,8,256,128]{3,2,0,1:T(8,128)S(1)} %dynamic-slice_bitcast_fusion), channel_id=1, source_target_pairs={{0,32},{32,0},{1,33},{33,1},{2,34},{34,2},{3,35},{35,3},{4,36},{36... | collective-permute-start | bytes 9437192 | tf_op jit(solution)/shard_map/ppermute | solution.py:244
Sparse Core Ops, SparseCore 0:
  199.0 46.5 reduce-scatter.1

commit v4 on v3

--- a/solution.py
+++ b/solution.py
@@ -53,7 +53,7 @@
     outer_len = 32
     inner_len = length // outer_len
     cos_outer, sin_outer, cos_twist, sin_twist, cos_inner, sin_inner = dft_tables(length)
-    product = partial(jnp.einsum, precision=lax.Precision.HIGHEST)
+    product = partial(jnp.einsum, precision=lax.Precision.HIGH)
     real_part = real_part.reshape(row_total, outer_len, inner_len)
     imag_part = imag_part.reshape(row_total, outer_len, inner_len)
     step_real = product("rab,ak->rkb", real_part, cos_outer) - product(
@@ -78,7 +78,7 @@
     outer_len = 32
     inner_len = length // outer_len
     cos_outer, sin_outer, cos_twist, sin_twist, cos_inner, sin_inner = dft_tables(length)
-    product = partial(jnp.einsum, precision=lax.Precision.HIGHEST)
+    product = partial(jnp.einsum, precision=lax.Precision.HIGH)
     real_part = real_part.reshape(outer_len, inner_len, col_total)
     imag_part = imag_part.reshape(outer_len, inner_len, col_total)
     step_real = product("abc,ak->kbc", real_part, cos_outer) - product(
@@ -238,11 +238,11 @@
     chips = lax.axis_size("z")
     pair = lax.axis_size("core")
     core = lax.axis_index("core")
-    terms = taylor_terms.astype(jnp.float32).reshape(3, chips, pair, GRID // chips // pair, width_here)
+    terms = taylor_terms.reshape(3, chips, pair, GRID // chips // pair, width_here)
     keep = lax.dynamic_index_in_dim(terms, core, axis=2, keepdims=False)
     give = lax.dynamic_index_in_dim(terms, pair - 1 - core, axis=2, keepdims=False)
     got = lax.ppermute(give, "core", [(0, 1), (1, 0)])
-    partial_sum = (keep + got).astype(jnp.bfloat16)
+    partial_sum = (keep.astype(jnp.float32) + got.astype(jnp.float32)).astype(jnp.bfloat16)
     summed = lax.psum_scatter(partial_sum, "z", scatter_dimension=1, tiled=True)
     summed = summed.reshape(3, GRID // chips // pair, width_here)
     return summed

time: 257 us -> 235 us (0.914); the launches traced: 253 us -> 234 us
  matrix products: 34.3 us -> 23.9 us
  waiting for transfers between devices: 129 us -> 125 us
    unnamed x10 -> x8, local copies, waits for them, and re-layouts: 8.28 us -> 5.85 us
where the time goes in v4:
time: 235 us; the launch traced here: 234 us
  waiting for transfers between devices  125 us (53%)
  starting transfers between devices  32.8 us (14%)
  matrix products  23.9 us (10%)
  local copies, waits for them, and re-layouts  18 us (8%)
  between operations  14.3 us (6%)
  other arithmetic  12.9 us (5%)
  Pallas kernels  7.03 us (3%)
    reduce_scatter x1, waiting for transfers between devices, shards(): summed = lax.psum_scatter(partial_sum, 'z', scatter_dimension=1, tiled=True)  46.2 us
    all_to_all x1, waiting for transfers between devices, shards(): lax.all_to_all(for_sending(spectrum), 'row', split_axis=2, concat_axis=1,...  45 us
    all_to_all x1, waiting for transfers between devices, shards(): lax.all_to_all(send.reshape((row_count, capacity) + payload.shape[1:]), '...  30.4 us
    all_to_all x1, starting transfers between devices, shards(): lax.all_to_all(for_sending(spectrum), 'row', split_axis=2, concat_axis=1,...  20.6 us
    all_to_all x1, starting transfers between devices, shards(): lax.all_to_all(send.reshape((row_count, capacity) + payload.shape[1:]), '...  10.2 us
    pallas_call x1, Pallas kernels, grid_into_slab(): pl.pallas_call(grid_kernel, out_shape=jax.ShapeDtypeStruct((2, slab_rows,...  7.03 us
    unnamed x8, local copies, waits for them, and re-layouts  5.85 us
  transfers between devices with their start and end apart: 4, of which 4 were waited for; matrix products, arithmetic and copies ran while one was open for 0% of the time, Pallas kernels for 0%

profile of v4, /device:TPU:6, one launch (start us, length us, event | category | flops | bytes accessed | tf_op | source)
XLA Modules:
  0.0 234.3 jit_solution(17228477343352800810)
XLA Ops:
  7.4 0.8 select_reduce_fusion
  10.4 0.9 bitcast_dynamic-update-slice_fusion.1
  11.3 0.9 bitcast_dynamic-update-slice_fusion
  14.8 1.3 copy.36
  16.0 10.2 %all-to-all-start = ((bf16[32,8,19,128]{3,1,2,0:T(8,128)(2,1)}), bf16[32,8,19,128]{3,1,2,0:T(8,128)(2,1)S(1)}, u32[]{:S(2)}, u32[]{:S(2)}) async-start(bf16[32,8,19,128]{3,1,2,0:T(8,128)(2,1)} %copy.36), calls=%async_computation | async-start | bytes 2490368 | tf_op jit(solution)/shard_map/all_to_all | solution.py:207
  26.4 30.4 %all-to-all-done = bf16[32,8,19,128]{3,1,2,0:T(8,128)(2,1)S(1)} async-done(((bf16[32,8,19,128]{3,1,2,0:T(8,128)(2,1)}), bf16[32,8,19,128]{3,1,2,0:T(8,128)(2,1)S(1)}, u32[]{:S(2)}, u32[]{:S(2)}) %all-to-all-start) | async-done | bytes 1245216 | tf_op jit(solution)/shard_map/all_to_all | solution.py:207
  57.1 1.0 slice_reduce_fusion
  61.2 1.9 scatter_custom_fusion.order_ref
  63.2 7.0 %shard_map.82 = f32[2,128,4096]{2,1,0:T(8,128)} custom-call(s32[256]{0:T(256)} %scatter_custom_fusion.order_ref, s32[256]{0:T(256)} %convert_convert_fusion.tile_ref, s32[1]{0:T(128)} %bitcast.16.count_ref, bf16[256,19,128]{2,1,0:T(8,128)(2,1)} %bitcast.119), custom_call_target="tpu_custom_call" | custom-call | tf_op jit(solution)/shard_map/pallas_call | solution.py:154
  70.2 2.5 %slice_bitcast_fusion = (f32[16,8,32,128]{3,1,2,0:T(8,128)S(1)}, f32[16,8,32,128]{3,1,2,0:T(8,128)S(1)}) fusion(f32[2,128,4096]{2,1,0:T(8,128)} %shard_map.82), kind=kLoop, calls=%fused_computation.4 | loop fusion | bytes 8388608
  73.1 1.1 fusion.62
  74.2 1.1 fusion.68
  75.7 1.2 convolution_add_fusion.1
  76.9 1.6 subtract_bitcast_fusion
  78.5 2.3 fusion.7
  80.8 2.3 fusion.5
  83.1 2.6 %fusion.19 = bf16[128,128,32]{0,1,2:T(8,128)(2,1)S(1)} fusion(f32[128,128,32]{1,0,2:T(8,128)S(1)} %fusion.7, f32[128,32,128]{2,1,0:T(8,128)S(1)} %get-tuple-element.19), kind=kOutput, calls=%fused_computation.32 | convolution fusion | flops 403931136 | bytes 5242880 | tf_op jit(solution)/shard_map/rkb,bm->rmk/dot_general | solution.py:67
  86.4 2.4 %fusion.22 = bf16[128,128,32]{0,1,2:T(8,128)(2,1)S(1)} fusion(f32[128,128,32]{1,0,2:T(8,128)S(1)} %fusion.5, f32[128,32,128]{2,1,0:T(8,128)S(1)} %get-tuple-element.19), kind=kOutput, calls=%fused_computation.33 | convolution fusion | flops 403931136 | bytes 5242880 | tf_op jit(solution)/shard_map/rkb,bm->rmk/dot_general | solution.py:70
  89.7 2.8 %copy.44 = bf16[2,128,32,128]{3,1,0,2:T(8,128)(2,1)} copy(bf16[2,128,32,128]{1,3,2,0:T(8,128)(2,1)S(1)} %pad_maximum_fusion) | data formatting | bytes 4194304 | tf_op jit(solution)/shard_map/stack | solution.py:226
  92.5 20.6 %all-to-all-start.1 = ((bf16[2,128,32,128]{3,1,0,2:T(8,128)(2,1)}), bf16[2,128,32,128]{3,1,0,2:T(8,128)(2,1)S(1)}, u32[]{:S(2)}, u32[]{:S(2)}) async-start(bf16[2,128,32,128]{3,1,0,2:T(8,128)(2,1)} %copy.44), calls=%async_computation.1 | async-start | bytes 4194304 | tf_op jit(solution)/shard_map/all_to_all | solution.py:230
  114.1 45.0 %all-to-all-done.1 = bf16[2,128,32,128]{3,1,0,2:T(8,128)(2,1)S(1)} async-done(((bf16[2,128,32,128]{3,1,0,2:T(8,128)(2,1)}), bf16[2,128,32,128]{3,1,0,2:T(8,128)(2,1)S(1)}, u32[]{:S(2)}, u32[]{:S(2)}) %all-to-all-start.1) | async-done | bytes 2097184 | tf_op jit(solution)/shard_map/all_to_all | solution.py:230
  159.1 1.4 copy.80
  162.8 1.7 multiply_subtract_fusion
  164.5 2.3 fusion.1
  166.8 2.4 %subtract_multiply_fusion = f32[128,32,128]{2,0,1:T(8,128)S(1)} fusion(f32[128,32,128]{2,0,1:T(8,128)S(1)} %fusion.1, f32[32,128,128]{2,0,1:T(8,128)S(1)} %get-tuple-element.17), kind=kOutput, calls=%fused_computation.12 | convolution fusion | flops 403931136 | bytes 6291456 | tf_op jit(solution)/shard_map/kbc,bm->mkc/dot_general | solution.py:92
  169.2 1.2 copy.50
  170.4 0.9 multiply_convert_fusion
  171.3 1.3 dynamic-slice_bitcast_fusion
  172.6 1.9 collective-permute-start
  174.5 3.7 %collective-permute-done = bf16[3,8,256,128]{3,2,0,1:T(8,128)(2,1)} collective-permute-done((bf16[3,8,256,128]{3,2,0,1:T(8,128)(2,1)}, bf16[3,8,256,128]{3,2,0,1:T(8,128)(2,1)}, u32[]{:S(2)}, u32[]{:S(2)}) %collective-permute-start) | collective-permute-done | bytes 1572896 | tf_op jit(solution)/shard_map/ppermute | solution.py:244
  178.2 3.0 %fusion = bf16[3,8,256,128]{3,2,0,1:T(8,128)(2,1)} fusion(bf16[3,8,256,128]{3,2,0,1:T(8,128)(2,1)} %collective-permute-done, bf16[3,8,2,256,128]{4,3,0,1,2:T(8,128)(2,1)S(1)} %multiply_convert_fusion, s32[]{:T(128)S(6)} %select_n.110), kind=kLoop, calls=%fused_computation.3 | loop fusion | flops 3145728 | bytes 4718596 | tf_op jit(solution)/shard_map/convert_element_type | solution.py:245
  181.3 46.2 %reduce-scatter.2.cloned.1.call-done = bf16[3,1,256,128]{3,2,0,1:T(8,128)(2,1)} async-done(((bf16[3,8,256,128]{3,2,0,1:T(8,128)(2,1)}), bf16[3,1,256,128]{3,2,0,1:T(8,128)(2,1)}) %reduce-scatter.2.cloned.1.call-update) | async-done | bytes 196624 | tf_op jit(solution)/shard_map/reduce_scatter | solution.py:246
  (46 shorter events, 14.0 us)
Async XLA Ops:
  16.0 40.7 %all-to-all-start = ((bf16[32,8,19,128]{3,1,2,0:T(8,128)(2,1)}), bf16[32,8,19,128]{3,1,2,0:T(8,128)(2,1)S(1)}, u32[]{:S(2)}, u32[]{:S(2)}) async-start(bf16[32,8,19,128]{3,1,2,0:T(8,128)(2,1)} %copy.36), calls=%async_computation | async-start | bytes 2490368 | tf_op jit(solution)/shard_map/all_to_all | solution.py:207
  57.1 6.0 %copy-start = (bf16[32,8,19,128]{3,2,1,0:T(8,128)(2,1)}, bf16[32,8,19,128]{3,2,1,0:T(8,128)(2,1)S(1)}, u32[]{:S(2)}) copy-start(bf16[32,8,19,128]{3,2,1,0:T(8,128)(2,1)S(1)} %copy.37) | copy-start | bytes 3735556
  92.5 66.6 %all-to-all-start.1 = ((bf16[2,128,32,128]{3,1,0,2:T(8,128)(2,1)}), bf16[2,128,32,128]{3,1,0,2:T(8,128)(2,1)S(1)}, u32[]{:S(2)}, u32[]{:S(2)}) async-start(bf16[2,128,32,128]{3,1,0,2:T(8,128)(2,1)} %copy.44), calls=%async_computation.1 | async-start | bytes 4194304 | tf_op jit(solution)/shard_map/all_to_all | solution.py:230
  113.1 114.3 %reduce-scatter.2.cloned.1.call-start = ((), (), s32[]{:S(2)}) async-start(), calls=%async_computation.3 | async-start | bytes 1769472 | tf_op jit(solution)/shard_map/reduce_scatter | solution.py:246
  172.6 5.6 %collective-permute-start = (bf16[3,8,256,128]{3,2,0,1:T(8,128)(2,1)}, bf16[3,8,256,128]{3,2,0,1:T(8,128)(2,1)}, u32[]{:S(2)}, u32[]{:S(2)}) collective-permute-start(bf16[3,8,256,128]{3,2,0,1:T(8,128)(2,1)} %dynamic-slice_bitcast_fusion), channel_id=1, source_target_pairs={{0,32},{32,0},{1,33},{33,1},{2,34},{34,2},{3,35},{35,3},{4,36},{36... | collective-permute-start | bytes 4718600 | tf_op jit(solution)/shard_map/ppermute | solution.py:244
Sparse Core Ops, SparseCore 0:
  181.4 46.0 reduce-scatter.1

commit v5 on v4

--- a/solution.py
+++ b/solution.py
@@ -48,49 +48,52 @@
     )
 
 
+def complex_weights(cos_part, sin_part, real_only=False):
+    top = jnp.concatenate([cos_part, sin_part], axis=1)
+    bottom = jnp.concatenate([-sin_part, cos_part], axis=1)
+    if real_only:
+        return jnp.stack([cos_part, -sin_part])
+    return jnp.stack([top, bottom])
+
+
 def transform_last(real_part, imag_part):
     row_total, length = real_part.shape
     outer_len = 32
     inner_len = length // outer_len
     cos_outer, sin_outer, cos_twist, sin_twist, cos_inner, sin_inner = dft_tables(length)
     product = partial(jnp.einsum, precision=lax.Precision.HIGH)
-    real_part = real_part.reshape(row_total, outer_len, inner_len)
-    imag_part = imag_part.reshape(row_total, outer_len, inner_len)
-    step_real = product("rab,ak->rkb", real_part, cos_outer) - product(
-        "rab,ak->rkb", imag_part, sin_outer
-    )
-    step_imag = product("rab,ak->rkb", real_part, sin_outer) + product(
-        "rab,ak->rkb", imag_part, cos_outer
-    )
+    both = jnp.stack([real_part, imag_part]).reshape(2, row_total, outer_len, inner_len)
+    step = product("prab,pak->rkb", both, complex_weights(cos_outer, sin_outer))
+    step_real = step[:, :outer_len]
+    step_imag = step[:, outer_len:]
     twist_real = step_real * cos_twist - step_imag * sin_twist
     twist_imag = step_real * sin_twist + step_imag * cos_twist
-    out_real = product("rkb,bm->rmk", twist_real, cos_inner) - product(
-        "rkb,bm->rmk", twist_imag, sin_inner
-    )
-    out_imag = product("rkb,bm->rmk", twist_real, sin_inner) + product(
-        "rkb,bm->rmk", twist_imag, cos_inner
-    )
-    return (out_real.reshape(row_total, length), out_imag.reshape(row_total, length))
-
-
-def transform_first_real(real_part, imag_part):
-    length, col_total = real_part.shape
+    out = product(
+        "qrkb,qbm->rmk",
+        jnp.stack([twist_real, twist_imag]),
+        complex_weights(cos_inner, sin_inner),
+    )
+    out_real = out[:, :inner_len].reshape(row_total, length)
+    out_imag = out[:, inner_len:].reshape(row_total, length)
+    return (out_real, out_imag)
+
+
+def transform_first_real(both):
+    _, length, col_total = both.shape
     outer_len = 32
     inner_len = length // outer_len
     cos_outer, sin_outer, cos_twist, sin_twist, cos_inner, sin_inner = dft_tables(length)
     product = partial(jnp.einsum, precision=lax.Precision.HIGH)
-    real_part = real_part.reshape(outer_len, inner_len, col_total)
-    imag_part = imag_part.reshape(outer_len, inner_len, col_total)
-    step_real = product("abc,ak->kbc", real_part, cos_outer) - product(
-        "abc,ak->kbc", imag_part, sin_outer
-    )
-    step_imag = product("abc,ak->kbc", real_part, sin_outer) + product(
-        "abc,ak->kbc", imag_part, cos_outer
-    )
+    both = both.reshape(2, outer_len, inner_len, col_total)
+    step = product("pabc,pak->kbc", both, complex_weights(cos_outer, sin_outer))
+    step_real = step[:outer_len]
+    step_imag = step[outer_len:]
     twist_real = step_real * cos_twist[:, :, None] - step_imag * sin_twist[:, :, None]
     twist_imag = step_real * sin_twist[:, :, None] + step_imag * cos_twist[:, :, None]
-    out_real = product("kbc,bm->mkc", twist_real, cos_inner) - product(
-        "kbc,bm->mkc", twist_imag, sin_inner
+    out_real = product(
+        "qkbc,qbm->mkc",
+        jnp.stack([twist_real, twist_imag]),
+        complex_weights(cos_inner, sin_inner, real_only=True),
     )
     return out_real.reshape(length, col_total)
 
@@ -231,9 +234,7 @@
         for_sending(spectrum), "row", split_axis=2, concat_axis=1, tiled=True
     ).astype(spectrum.dtype)
     width_here = received.shape[2] * received.shape[3]
-    real_cols = received[0].reshape(GRID, width_here)
-    imag_cols = received[1].reshape(GRID, width_here)
-    dirty_image = transform_first_real(real_cols, imag_cols) * image_scale
+    dirty_image = transform_first_real(received.reshape(2, GRID, width_here)) * image_scale
     taylor_terms = (weights[:, None, None] * dirty_image[None]).astype(jnp.bfloat16)
     chips = lax.axis_size("z")
     pair = lax.axis_size("core")

time: 235 us -> 230 us (0.979)
  matrix products: 23.9 us -> 14.3 us
  other arithmetic: 12.9 us -> 16.9 us
  Pallas kernels: 7.03 us -> 10.8 us
  starting transfers between devices: 32.8 us -> 29.7 us
    dot_general x14 -> x4, matrix products: 23.3 us -> 13.7 us  [the longest x1 5.95 us: transform_last(): product('qrkb,qbm->rmk', jnp.stack([twist_real, twist_imag]), complex_wei...]
    pallas_call x1, Pallas kernels: 7.03 us -> 10.8 us  [grid_into_slab(): pl.pallas_call(grid_kernel, out_shape=jax.ShapeDtypeStruct((2, slab_rows,...]
    all_to_all x1, starting transfers between devices: 20.6 us -> 17.3 us  [shards(): lax.all_to_all(for_sending(spectrum), 'row', split_axis=2, concat_axis=1,...]
    another operation x4 -> x10, other arithmetic: 0.69 us -> 3.74 us  [the longest x2 1.85 us: transform_first_real(): jnp.stack([twist_real, twist_imag])]
    unnamed x8 -> x6, local copies, waits for them, and re-layouts: 5.85 us -> 5.54 us
  transfers between devices with their start and end apart: 4 -> 4, of which waited for: 4 -> 4; matrix products, arithmetic and copies ran while one was open for 0% -> 1% of each run, Pallas kernels for 0% -> 0%
where the time goes in v5:
time: 230 us
  waiting for transfers between devices  126 us (55%)
  starting transfers between devices  29.7 us (13%)
  local copies, waits for them, and re-layouts  17.5 us (8%)
  other arithmetic  16.9 us (7%)
  matrix products  14.3 us (6%)
  between operations  14.3 us (6%)
  Pallas kernels  10.8 us (5%)
    reduce_scatter x1, waiting for transfers between devices, shards(): summed = lax.psum_scatter(partial_sum, 'z', scatter_dimension=1, tiled=True)  46.8 us
    all_to_all x1, waiting for transfers between devices, shards(): lax.all_to_all(for_sending(spectrum), 'row', split_axis=2, concat_axis=1,...  45.9 us
    all_to_all x1, waiting for transfers between devices, shards(): lax.all_to_all(send.reshape((row_count, capacity) + payload.shape[1:]), '...  29.6 us
    all_to_all x1, starting transfers between devices, shards(): lax.all_to_all(for_sending(spectrum), 'row', split_axis=2, concat_axis=1,...  17.3 us
    pallas_call x1, Pallas kernels, grid_into_slab(): pl.pallas_call(grid_kernel, out_shape=jax.ShapeDtypeStruct((2, slab_rows,...  10.8 us
    all_to_all x1, starting transfers between devices, shards(): lax.all_to_all(send.reshape((row_count, capacity) + payload.shape[1:]), '...  10.2 us
    dot_general x1, matrix products, transform_last(): product('qrkb,qbm->rmk', jnp.stack([twist_real, twist_imag]), complex_wei...  5.95 us
    unnamed x6, local copies, waits for them, and re-layouts  5.54 us
  transfers between devices with their start and end apart: 4, of which 4 were waited for; matrix products, arithmetic and copies ran while one was open for 1% of the time, Pallas kernels for 0%

profile of v5, /device:TPU:6, one launch (start us, length us, event | category | flops | bytes accessed | tf_op | source)
XLA Modules:
  0.0 229.5 jit_solution(18101359039521559443)
XLA Ops:
  6.5 0.7 fusion.41
  7.4 0.8 select_reduce_fusion
  8.2 0.7 multiply_add_fusion
  8.9 0.8 bitcast_dynamic-update-slice_fusion.2
  10.4 0.9 bitcast_dynamic-update-slice_fusion.1
  11.3 0.9 bitcast_dynamic-update-slice_fusion
  12.2 0.8 bitcast_dynamic-update-slice_fusion.4
  13.0 0.8 bitcast_dynamic-update-slice_fusion.3
  14.8 1.3 copy.30
  16.0 10.2 %all-to-all-start = ((bf16[32,8,19,128]{3,1,2,0:T(8,128)(2,1)}), bf16[32,8,19,128]{3,1,2,0:T(8,128)(2,1)S(1)}, u32[]{:S(2)}, u32[]{:S(2)}) async-start(bf16[32,8,19,128]{3,1,2,0:T(8,128)(2,1)} %copy.30), calls=%async_computation | async-start | bytes 2490368 | tf_op jit(solution)/shard_map/all_to_all | solution.py:210
  27.2 29.6 %all-to-all-done = bf16[32,8,19,128]{3,1,2,0:T(8,128)(2,1)S(1)} async-done(((bf16[32,8,19,128]{3,1,2,0:T(8,128)(2,1)}), bf16[32,8,19,128]{3,1,2,0:T(8,128)(2,1)S(1)}, u32[]{:S(2)}, u32[]{:S(2)}) %all-to-all-start) | async-done | bytes 1245216 | tf_op jit(solution)/shard_map/all_to_all | solution.py:210
  57.1 1.0 slice_reduce_fusion
  61.2 1.9 scatter_custom_fusion.order_ref
  63.2 10.8 %shard_map.82 = f32[2,128,4096]{2,1,0:T(8,128)} custom-call(s32[256]{0:T(256)} %scatter_custom_fusion.order_ref, s32[256]{0:T(256)} %convert_convert_fusion.tile_ref, s32[1]{0:T(128)} %bitcast.21.count_ref, bf16[256,19,128]{2,1,0:T(8,128)(2,1)} %bitcast.108), custom_call_target="tpu_custom_call" | custom-call | tf_op jit(solution)/shard_map/pallas_call | solution.py:157
  74.0 2.9 %copy.47 = f32[32,8,32,128]{3,2,1,0:T(8,128)S(1)} copy(f32[32,8,32,128]{3,1,2,0:T(8,128)} %bitcast.104) | data formatting | bytes 8388608
  76.9 1.9 fusion.7
  80.0 6.0 %fusion.10 = bf16[128,256,32]{0,1,2:T(8,128)(2,1)S(1)} fusion(f32[2,128,32,128]{3,2,1,0:T(8,128)S(1)} %pad_maximum_fusion, f32[1,128,256]{1,2,0:T(8,128)S(1)} %get-tuple-element.24, f32[1,128,256]{1,2,0:T(8,128)S(1)} %get-tuple-element.23), kind=kOutput, calls=%fused_computation.15 | convolution fusion | flops 1611726848 | bytes 6553600 | tf_op jit(solution)/shard_map/qrkb,qbm->rmk/dot_general | solution.py:71
  86.1 0.7 copy.34
  86.8 0.7 copy.35
  87.7 3.8 %copy.36 = bf16[2,128,32,128]{3,0,1,2:T(2,128)(2,1)} copy(bf16[2,128,32,128]{1,3,2,0:T(8,128)(2,1)S(1)} %pad_maximum_fusion.2) | data formatting | bytes 4194304 | tf_op jit(solution)/shard_map/stack | solution.py:229
  91.5 17.3 %all-to-all-start.1 = ((bf16[2,128,32,128]{3,0,1,2:T(2,128)(2,1)}), bf16[2,128,32,128]{3,0,1,2:T(2,128)(2,1)S(1)}, u32[]{:S(2)}, u32[]{:S(2)}) async-start(bf16[2,128,32,128]{3,0,1,2:T(2,128)(2,1)} %copy.36), calls=%async_computation.1 | async-start | bytes 4194304 | tf_op jit(solution)/shard_map/all_to_all | solution.py:233
  110.2 45.9 %all-to-all-done.1 = bf16[2,128,32,128]{3,0,1,2:T(2,128)(2,1)S(1)} async-done(((bf16[2,128,32,128]{3,0,1,2:T(2,128)(2,1)}), bf16[2,128,32,128]{3,0,1,2:T(2,128)(2,1)S(1)}, u32[]{:S(2)}, u32[]{:S(2)}) %all-to-all-start.1) | async-done | bytes 2097184 | tf_op jit(solution)/shard_map/all_to_all | solution.py:233
  156.1 2.3 %convolution_bitcast_fusion = f32[64,128,128]{2,0,1:T(8,128)S(1)} fusion(bf16[2,128,32,128]{3,0,1,2:T(2,128)(2,1)S(1)} %all-to-all-done.1, f32[1,32,64]{2,1,0:T(8,128)S(1)} %get-tuple-element.26, f32[1,32,64]{2,1,0:T(8,128)S(1)} %get-tuple-element.25), kind=kOutput, calls=%fused_computation.14 | convolution fusion | flops 402657280 | bytes 6307840 | tf_op jit(solution)/shard_map/pabc,pak->kbc/dot_general | solution.py:88
  158.4 1.4 subtract_bitcast_fusion
  160.3 3.5 %bitcast_multiply_fusion = f32[128,32,128]{2,0,1:T(8,128)S(1)} fusion(f32[2,32,128,128]{3,1,2,0:T(8,128)S(1)} %pad_maximum_fusion.1, f32[1,128,128]{1,2,0:T(8,128)S(1)} %get-tuple-element.35, f32[1,128,128]{1,2,0:T(8,128)S(1)} %get-tuple-element.36), kind=kOutput, calls=%fused_computation.18 | convolution fusion | flops 805863424 | bytes 6422528 | tf_op jit(solution)/shard_map/qkbc,qbm->mkc/dot_general | solution.py:93
  163.8 1.2 copy.41
  165.0 0.9 multiply_convert_fusion
  165.9 1.3 dynamic-slice_bitcast_fusion
  167.2 1.9 collective-permute-start
  169.1 3.7 %collective-permute-done = bf16[3,8,256,128]{3,2,0,1:T(8,128)(2,1)} collective-permute-done((bf16[3,8,256,128]{3,2,0,1:T(8,128)(2,1)}, bf16[3,8,256,128]{3,2,0,1:T(8,128)(2,1)}, u32[]{:S(2)}, u32[]{:S(2)}) %collective-permute-start) | collective-permute-done | bytes 1572896 | tf_op jit(solution)/shard_map/ppermute | solution.py:245
  172.8 3.0 %fusion.6 = bf16[3,8,256,128]{3,2,0,1:T(8,128)(2,1)} fusion(bf16[3,8,256,128]{3,2,0,1:T(8,128)(2,1)} %collective-permute-done, bf16[3,8,2,256,128]{4,3,0,1,2:T(8,128)(2,1)S(1)} %multiply_convert_fusion, s32[]{:T(128)S(6)} %select_n.114), kind=kLoop, calls=%fused_computation.12 | loop fusion | flops 3145728 | bytes 4718596 | tf_op jit(solution)/shard_map/convert_element_type | solution.py:246
  175.9 46.8 %reduce-scatter.2.cloned.1.call-done = bf16[3,1,256,128]{3,2,0,1:T(8,128)(2,1)} async-done(((bf16[3,8,256,128]{3,2,0,1:T(8,128)(2,1)}), bf16[3,1,256,128]{3,2,0,1:T(8,128)(2,1)}) %reduce-scatter.2.cloned.1.call-update) | async-done | bytes 196624 | tf_op jit(solution)/shard_map/reduce_scatter | solution.py:247
  (45 shorter events, 8.8 us)
Async XLA Ops:
  16.0 40.7 %all-to-all-start = ((bf16[32,8,19,128]{3,1,2,0:T(8,128)(2,1)}), bf16[32,8,19,128]{3,1,2,0:T(8,128)(2,1)S(1)}, u32[]{:S(2)}, u32[]{:S(2)}) async-start(bf16[32,8,19,128]{3,1,2,0:T(8,128)(2,1)} %copy.30), calls=%async_computation | async-start | bytes 2490368 | tf_op jit(solution)/shard_map/all_to_all | solution.py:210
  57.1 6.0 %copy-start = (bf16[32,8,19,128]{3,2,1,0:T(8,128)(2,1)}, bf16[32,8,19,128]{3,2,1,0:T(8,128)(2,1)S(1)}, u32[]{:S(2)}) copy-start(bf16[32,8,19,128]{3,2,1,0:T(8,128)(2,1)S(1)} %copy.31) | copy-start | bytes 3735556
  91.5 64.6 %all-to-all-start.1 = ((bf16[2,128,32,128]{3,0,1,2:T(2,128)(2,1)}), bf16[2,128,32,128]{3,0,1,2:T(2,128)(2,1)S(1)}, u32[]{:S(2)}, u32[]{:S(2)}) async-start(bf16[2,128,32,128]{3,0,1,2:T(2,128)(2,1)} %copy.36), calls=%async_computation.1 | async-start | bytes 4194304 | tf_op jit(solution)/shard_map/all_to_all | solution.py:233
  108.8 113.9 %reduce-scatter.2.cloned.1.call-start = ((), (), s32[]{:S(2)}) async-start(), calls=%async_computation.3 | async-start | bytes 1769472 | tf_op jit(solution)/shard_map/reduce_scatter | solution.py:247
  167.2 5.6 %collective-permute-start = (bf16[3,8,256,128]{3,2,0,1:T(8,128)(2,1)}, bf16[3,8,256,128]{3,2,0,1:T(8,128)(2,1)}, u32[]{:S(2)}, u32[]{:S(2)}) collective-permute-start(bf16[3,8,256,128]{3,2,0,1:T(8,128)(2,1)} %dynamic-slice_bitcast_fusion), channel_id=1, source_target_pairs={{0,32},{32,0},{1,33},{33,1},{2,34},{34,2},{3,35},{35,3},{4,36},{36... | collective-permute-start | bytes 4718600 | tf_op jit(solution)/shard_map/ppermute | solution.py:245
Sparse Core Ops, SparseCore 0:
  176.0 46.6 reduce-scatter.1

commit v6 on v5

--- a/solution.py
+++ b/solution.py
@@ -104,44 +104,49 @@
 GROUP = 8
 
 
-def grid_kernel(order_ref, tile_ref, count_ref, pay_ref, out_ref):
+def grid_kernel(tile_ref, pay_ref, out_ref, order_ref):
     tiles_total = out_ref.shape[1] // TU * (out_ref.shape[2] // TV)
     tile_cols = out_ref.shape[2] // TV
     lanes = pay_ref.shape[2]
     out_ref[...] = jnp.zeros(out_ref.shape, jnp.float32)
     du_base = lax.broadcasted_iota(jnp.int32, (TU, lanes), 0)
-    dv_base = lax.broadcasted_iota(jnp.int32, (TV, lanes), 0)
+    dv_base = lax.broadcasted_iota(jnp.int32, (TV, lanes), 0).astype(jnp.bfloat16)
 
     def one_block(slot):
         blk = pay_ref[slot].astype(jnp.float32)
         vis = blk[0:2]
         ku = blk[2:9]
-        kv = blk[9:16]
         ou = blk[16:17].astype(jnp.int32)
-        ov = blk[17:18].astype(jnp.int32)
         du = du_base - ou
         su = jnp.zeros((TU, lanes), jnp.float32)
         for t in range(7):
             su = jnp.where(du == t, ku[t : t + 1], su)
         left = jnp.concatenate([vis[0:1] * su, vis[1:2] * su], axis=0).astype(jnp.bfloat16)
-        dv = dv_base - ov
-        sv = jnp.zeros((TV, lanes), jnp.float32)
+        raw = pay_ref[slot]
+        dv = dv_base - raw[17:18]
+        sv = jnp.zeros((TV, lanes), jnp.bfloat16)
         for t in range(7):
-            sv = jnp.where(dv == t, kv[t : t + 1], sv)
-        sv = sv.astype(jnp.bfloat16)
+            sv = jnp.where(dv == t, raw[9 + t : 10 + t], sv)
         return lax.dot_general(
             left, sv, (((1,), (1,)), ((), ())), preferred_element_type=jnp.float32
         )
 
+    def fill(s, filled):
+        order_ref[filled] = s
+        return filled + (tile_ref[s] < tiles_total).astype(jnp.int32)
+
+    count = lax.fori_loop(0, pay_ref.shape[0], fill, jnp.int32(0))
+
     def body(i, carry):
-        slots = [order_ref[i * GROUP + g] for g in range(GROUP)]
+        places = [i * GROUP + g for g in range(GROUP)]
+        slots = [order_ref[jnp.minimum(q, count - 1)] for q in places]
         contribs = [one_block(s) for s in slots]
-        for s, contrib in zip(slots, contribs):
+        for q, s, contrib in zip(places, slots, contribs):
             tile = jnp.minimum(tile_ref[s], tiles_total - 1)
             row0 = pl.multiple_of((tile // tile_cols) * TU, TU)
             col0 = pl.multiple_of((tile % tile_cols) * TV, TV)
 
-            @pl.when(tile_ref[s] < tiles_total)
+            @pl.when(q < count)
             def _():
                 for p in range(2):
                     out_ref[p, pl.ds(row0, TU), pl.ds(col0, TV)] += contrib[
@@ -149,22 +154,21 @@
                     ]
         return carry
 
-    steps = (count_ref[0] + GROUP - 1) // GROUP
+    steps = (count + GROUP - 1) // GROUP
     lax.fori_loop(0, steps, body, 0)
 
 
-def grid_into_slab(order, tile_ids, count, payload, slab_rows):
+def grid_into_slab(tile_ids, payload, slab_rows):
     return pl.pallas_call(
         grid_kernel,
         out_shape=jax.ShapeDtypeStruct((2, slab_rows, GRID), jnp.float32),
         in_specs=[
             pl.BlockSpec(memory_space=pltpu.SMEM),
-            pl.BlockSpec(memory_space=pltpu.SMEM),
-            pl.BlockSpec(memory_space=pltpu.SMEM),
             pl.BlockSpec(memory_space=pltpu.VMEM),
         ],
         out_specs=pl.BlockSpec(memory_space=pltpu.VMEM),
-    )(order, tile_ids, count, payload)
+        scratch_shapes=[pltpu.SMEM((payload.shape[0],), jnp.int32)],
+    )(tile_ids, payload)
 
 
 def shards(
@@ -215,16 +219,7 @@
         tiled=True,
     ).reshape((slot_count,) + payload.shape[1:])
     tile_ids = jnp.max(recv[:, PAY_ROWS - 1, :].astype(jnp.float32), axis=1).astype(jnp.int32)
-    filled = tile_ids < tiles_total
-    filled_i = filled.astype(jnp.int32)
-    count = jnp.sum(filled_i)
-    place = jnp.where(
-        filled, jnp.cumsum(filled_i) - 1, count + jnp.cumsum(1 - filled_i) - 1
-    )
-    order = jnp.zeros((slot_count,), jnp.int32).at[place].set(
-        jnp.arange(slot_count, dtype=jnp.int32)
-    )
-    slab_grid = grid_into_slab(order, tile_ids, count.reshape(1), recv, slab_rows)
+    slab_grid = grid_into_slab(tile_ids, recv, slab_rows)
     spec_real, spec_imag = transform_last(slab_grid[0], slab_grid[1])
     spectrum = jnp.stack([spec_real, spec_imag]).reshape(2, slab_rows, row_count, GRID // row_count)
     image_scale = 1.0 / math.sqrt(block_count * row_count * vis_count)

time: 230 us -> 224 us (0.974)
  local copies, waits for them, and re-layouts: 17.5 us -> 15.2 us
where the time goes in v6:
time: 224 us
  waiting for transfers between devices  127 us (57%)
  starting transfers between devices  29.4 us (13%)
  local copies, waits for them, and re-layouts  15.2 us (7%)
  other arithmetic  14.8 us (7%)
  matrix products  14.3 us (6%)
  between operations  14.3 us (6%)
  Pallas kernels  8.97 us (4%)
    reduce_scatter x1, waiting for transfers between devices, shards(): summed = lax.psum_scatter(partial_sum, 'z', scatter_dimension=1, tiled=True)  47 us
    all_to_all x1, waiting for transfers between devices, shards(): lax.all_to_all(for_sending(spectrum), 'row', split_axis=2, concat_axis=1,...  46.5 us
    all_to_all x1, waiting for transfers between devices, shards(): lax.all_to_all(send.reshape((row_count, capacity) + payload.shape[1:]), '...  29.6 us
    all_to_all x1, starting transfers between devices, shards(): lax.all_to_all(for_sending(spectrum), 'row', split_axis=2, concat_axis=1,...  17 us
    all_to_all x1, starting transfers between devices, shards(): lax.all_to_all(send.reshape((row_count, capacity) + payload.shape[1:]), '...  10.2 us
    pallas_call x1, Pallas kernels, grid_into_slab(): pl.pallas_call(grid_kernel, out_shape=jax.ShapeDtypeStruct((2, slab_rows,...  8.97 us
    dot_general x1, matrix products, transform_last(): product('qrkb,qbm->rmk', jnp.stack([twist_real, twist_imag]), complex_wei...  5.96 us
    unnamed x6, local copies, waits for them, and re-layouts  5.54 us
  transfers between devices with their start and end apart: 4, of which 4 were waited for; matrix products, arithmetic and copies ran while one was open for 1% of the time, Pallas kernels for 0%

profile of v6, /device:TPU:6, one launch (start us, length us, event | category | flops | bytes accessed | tf_op | source)
XLA Modules:
  0.0 223.7 jit_solution(2343988975158778873)
XLA Ops:
  6.5 0.7 fusion.41
  7.4 0.8 select_reduce_fusion
  8.2 0.7 multiply_add_fusion
  8.9 0.8 bitcast_dynamic-update-slice_fusion.2
  10.4 0.9 bitcast_dynamic-update-slice_fusion.1
  11.3 0.9 bitcast_dynamic-update-slice_fusion
  12.2 0.8 bitcast_dynamic-update-slice_fusion.4
  13.0 0.8 bitcast_dynamic-update-slice_fusion.3
  14.8 1.3 copy.30
  16.0 10.2 %all-to-all-start = ((bf16[32,8,19,128]{3,1,2,0:T(8,128)(2,1)}), bf16[32,8,19,128]{3,1,2,0:T(8,128)(2,1)S(1)}, u32[]{:S(2)}, u32[]{:S(2)}) async-start(bf16[32,8,19,128]{3,1,2,0:T(8,128)(2,1)} %copy.30), calls=%async_computation | async-start | bytes 2490368 | tf_op jit(solution)/shard_map/all_to_all | solution.py:214
  27.2 29.6 %all-to-all-done = bf16[32,8,19,128]{3,1,2,0:T(8,128)(2,1)S(1)} async-done(((bf16[32,8,19,128]{3,1,2,0:T(8,128)(2,1)}), bf16[32,8,19,128]{3,1,2,0:T(8,128)(2,1)S(1)}, u32[]{:S(2)}, u32[]{:S(2)}) %all-to-all-start) | async-done | bytes 1245216 | tf_op jit(solution)/shard_map/all_to_all | solution.py:214
  57.1 1.0 slice_reduce_fusion
  58.7 9.0 %shard_map.82 = f32[2,128,4096]{2,1,0:T(8,128)} custom-call(s32[256]{0:T(256)} %convert_convert_fusion.tile_ref, bf16[256,19,128]{2,1,0:T(8,128)(2,1)} %bitcast.100), custom_call_target="tpu_custom_call" | custom-call | tf_op jit(solution)/shard_map/pallas_call | solution.py:162
  67.7 2.9 %copy.47 = f32[32,8,32,128]{3,2,1,0:T(8,128)S(1)} copy(f32[32,8,32,128]{3,1,2,0:T(8,128)} %bitcast.96) | data formatting | bytes 8388608
  70.7 1.9 fusion.7
  72.6 0.7 subtract_bitcast_fusion.1
  73.7 6.0 %fusion.10 = bf16[128,256,32]{0,1,2:T(8,128)(2,1)S(1)} fusion(f32[2,128,32,128]{3,2,1,0:T(8,128)S(1)} %pad_maximum_fusion, f32[1,128,256]{1,2,0:T(8,128)S(1)} %get-tuple-element.24, f32[1,128,256]{1,2,0:T(8,128)S(1)} %get-tuple-element.23), kind=kOutput, calls=%fused_computation.14 | convolution fusion | flops 1611726848 | bytes 6553600 | tf_op jit(solution)/shard_map/qrkb,qbm->rmk/dot_general | solution.py:71
  79.8 0.7 copy.34
  80.5 0.7 copy.35
  81.4 3.8 %copy.36 = bf16[2,128,32,128]{3,0,1,2:T(2,128)(2,1)} copy(bf16[2,128,32,128]{1,3,2,0:T(8,128)(2,1)S(1)} %pad_maximum_fusion.2) | data formatting | bytes 4194304 | tf_op jit(solution)/shard_map/stack | solution.py:224
  85.2 17.0 %all-to-all-start.1 = ((bf16[2,128,32,128]{3,0,1,2:T(2,128)(2,1)}), bf16[2,128,32,128]{3,0,1,2:T(2,128)(2,1)S(1)}, u32[]{:S(2)}, u32[]{:S(2)}) async-start(bf16[2,128,32,128]{3,0,1,2:T(2,128)(2,1)} %copy.36), calls=%async_computation.1 | async-start | bytes 4194304 | tf_op jit(solution)/shard_map/all_to_all | solution.py:228
  103.6 46.5 %all-to-all-done.1 = bf16[2,128,32,128]{3,0,1,2:T(2,128)(2,1)S(1)} async-done(((bf16[2,128,32,128]{3,0,1,2:T(2,128)(2,1)}), bf16[2,128,32,128]{3,0,1,2:T(2,128)(2,1)S(1)}, u32[]{:S(2)}, u32[]{:S(2)}) %all-to-all-start.1) | async-done | bytes 2097184 | tf_op jit(solution)/shard_map/all_to_all | solution.py:228
  150.1 2.3 %convolution_bitcast_fusion = f32[64,128,128]{2,0,1:T(8,128)S(1)} fusion(bf16[2,128,32,128]{3,0,1,2:T(2,128)(2,1)S(1)} %all-to-all-done.1, f32[1,32,64]{2,1,0:T(8,128)S(1)} %get-tuple-element.26, f32[1,32,64]{2,1,0:T(8,128)S(1)} %get-tuple-element.25), kind=kOutput, calls=%fused_computation.13 | convolution fusion | flops 402657280 | bytes 6307840 | tf_op jit(solution)/shard_map/pabc,pak->kbc/dot_general | solution.py:88
  152.4 1.4 subtract_bitcast_fusion
  154.3 3.5 %bitcast_multiply_fusion = f32[128,32,128]{2,0,1:T(8,128)S(1)} fusion(f32[2,32,128,128]{3,1,2,0:T(8,128)S(1)} %pad_maximum_fusion.1, f32[1,128,128]{1,2,0:T(8,128)S(1)} %get-tuple-element.33, f32[1,128,128]{1,2,0:T(8,128)S(1)} %get-tuple-element.34), kind=kOutput, calls=%fused_computation.17 | convolution fusion | flops 805863424 | bytes 6422528 | tf_op jit(solution)/shard_map/qkbc,qbm->mkc/dot_general | solution.py:93
  157.8 1.2 copy.41
  159.0 0.9 multiply_convert_fusion
  159.9 1.3 dynamic-slice_bitcast_fusion
  161.2 1.9 collective-permute-start
  163.1 3.7 %collective-permute-done = bf16[3,8,256,128]{3,2,0,1:T(8,128)(2,1)} collective-permute-done((bf16[3,8,256,128]{3,2,0,1:T(8,128)(2,1)}, bf16[3,8,256,128]{3,2,0,1:T(8,128)(2,1)}, u32[]{:S(2)}, u32[]{:S(2)}) %collective-permute-start) | collective-permute-done | bytes 1572896 | tf_op jit(solution)/shard_map/ppermute | solution.py:240
  166.8 3.1 %fusion.6 = bf16[3,8,256,128]{3,2,0,1:T(8,128)(2,1)} fusion(bf16[3,8,256,128]{3,2,0,1:T(8,128)(2,1)} %collective-permute-done, bf16[3,8,2,256,128]{4,3,0,1,2:T(8,128)(2,1)S(1)} %multiply_convert_fusion, s32[]{:T(128)S(6)} %select_n.91), kind=kLoop, calls=%fused_computation.11 | loop fusion | flops 3145728 | bytes 4718596 | tf_op jit(solution)/shard_map/convert_element_type | solution.py:241
  169.9 47.0 %reduce-scatter.2.cloned.1.call-done = bf16[3,1,256,128]{3,2,0,1:T(8,128)(2,1)} async-done(((bf16[3,8,256,128]{3,2,0,1:T(8,128)(2,1)}), bf16[3,1,256,128]{3,2,0,1:T(8,128)(2,1)}) %reduce-scatter.2.cloned.1.call-update) | async-done | bytes 196624 | tf_op jit(solution)/shard_map/reduce_scatter | solution.py:242
  (29 shorter events, 5.7 us)
Async XLA Ops:
  16.0 40.7 %all-to-all-start = ((bf16[32,8,19,128]{3,1,2,0:T(8,128)(2,1)}), bf16[32,8,19,128]{3,1,2,0:T(8,128)(2,1)S(1)}, u32[]{:S(2)}, u32[]{:S(2)}) async-start(bf16[32,8,19,128]{3,1,2,0:T(8,128)(2,1)} %copy.30), calls=%async_computation | async-start | bytes 2490368 | tf_op jit(solution)/shard_map/all_to_all | solution.py:214
  57.1 1.6 copy-start
  85.2 64.9 %all-to-all-start.1 = ((bf16[2,128,32,128]{3,0,1,2:T(2,128)(2,1)}), bf16[2,128,32,128]{3,0,1,2:T(2,128)(2,1)S(1)}, u32[]{:S(2)}, u32[]{:S(2)}) async-start(bf16[2,128,32,128]{3,0,1,2:T(2,128)(2,1)} %copy.36), calls=%async_computation.1 | async-start | bytes 4194304 | tf_op jit(solution)/shard_map/all_to_all | solution.py:228
  102.1 114.7 %reduce-scatter.2.cloned.1.call-start = ((), (), s32[]{:S(2)}) async-start(), calls=%async_computation.3 | async-start | bytes 1769472 | tf_op jit(solution)/shard_map/reduce_scatter | solution.py:242
  161.2 5.6 %collective-permute-start = (bf16[3,8,256,128]{3,2,0,1:T(8,128)(2,1)}, bf16[3,8,256,128]{3,2,0,1:T(8,128)(2,1)}, u32[]{:S(2)}, u32[]{:S(2)}) collective-permute-start(bf16[3,8,256,128]{3,2,0,1:T(8,128)(2,1)} %dynamic-slice_bitcast_fusion), channel_id=1, source_target_pairs={{0,32},{32,0},{1,33},{33,1},{2,34},{34,2},{3,35},{35,3},{4,36},{36... | collective-permute-start | bytes 4718600 | tf_op jit(solution)/shard_map/ppermute | solution.py:240
Sparse Core Ops, SparseCore 0:
  170.0 46.8 reduce-scatter.1

commit v7 on v6

--- a/solution.py
+++ b/solution.py
@@ -56,36 +56,30 @@
     return jnp.stack([top, bottom])
 
 
-def transform_last(real_part, imag_part):
-    row_total, length = real_part.shape
-    outer_len = 32
-    inner_len = length // outer_len
+def transform_last(both):
+    _, outer_len, row_total, inner_len = both.shape
+    length = outer_len * inner_len
     cos_outer, sin_outer, cos_twist, sin_twist, cos_inner, sin_inner = dft_tables(length)
     product = partial(jnp.einsum, precision=lax.Precision.HIGH)
-    both = jnp.stack([real_part, imag_part]).reshape(2, row_total, outer_len, inner_len)
-    step = product("prab,pak->rkb", both, complex_weights(cos_outer, sin_outer))
-    step_real = step[:, :outer_len]
-    step_imag = step[:, outer_len:]
-    twist_real = step_real * cos_twist - step_imag * sin_twist
-    twist_imag = step_real * sin_twist + step_imag * cos_twist
-    out = product(
-        "qrkb,qbm->rmk",
-        jnp.stack([twist_real, twist_imag]),
-        complex_weights(cos_inner, sin_inner),
-    )
-    out_real = out[:, :inner_len].reshape(row_total, length)
-    out_imag = out[:, inner_len:].reshape(row_total, length)
-    return (out_real, out_imag)
+    step = product("parb,pak->krb", both, complex_weights(cos_outer, sin_outer))
+    step_real = step[:outer_len]
+    step_imag = step[outer_len:]
+    twist_real = step_real * cos_twist[:, None, :] - step_imag * sin_twist[:, None, :]
+    twist_imag = step_real * sin_twist[:, None, :] + step_imag * cos_twist[:, None, :]
+    chunks = length // CHUNK
+    weights = complex_weights(cos_inner, sin_inner).reshape(
+        2, inner_len, 2, chunks, inner_len // chunks
+    )
+    out = product("qkrb,qbsdm->drsmk", jnp.stack([twist_real, twist_imag]), weights)
+    return out.reshape(chunks, row_total, 2, CHUNK)
 
 
 def transform_first_real(both):
-    _, length, col_total = both.shape
-    outer_len = 32
-    inner_len = length // outer_len
+    outer_len, inner_len, _, col_total = both.shape
+    length = outer_len * inner_len
     cos_outer, sin_outer, cos_twist, sin_twist, cos_inner, sin_inner = dft_tables(length)
     product = partial(jnp.einsum, precision=lax.Precision.HIGH)
-    both = both.reshape(2, outer_len, inner_len, col_total)
-    step = product("pabc,pak->kbc", both, complex_weights(cos_outer, sin_outer))
+    step = product("abpc,pak->kbc", both, complex_weights(cos_outer, sin_outer))
     step_real = step[:outer_len]
     step_imag = step[outer_len:]
     twist_real = step_real * cos_twist[:, :, None] - step_imag * sin_twist[:, :, None]
@@ -99,14 +93,15 @@
 
 
 PAY_ROWS = 19
+CHUNK = 128
 
 
 GROUP = 8
 
 
 def grid_kernel(tile_ref, pay_ref, out_ref, order_ref):
-    tiles_total = out_ref.shape[1] // TU * (out_ref.shape[2] // TV)
-    tile_cols = out_ref.shape[2] // TV
+    tiles_total = out_ref.shape[2] // TU * out_ref.shape[1]
+    tile_cols = out_ref.shape[1]
     lanes = pay_ref.shape[2]
     out_ref[...] = jnp.zeros(out_ref.shape, jnp.float32)
     du_base = lax.broadcasted_iota(jnp.int32, (TU, lanes), 0)
@@ -144,14 +139,12 @@
         for q, s, contrib in zip(places, slots, contribs):
             tile = jnp.minimum(tile_ref[s], tiles_total - 1)
             row0 = pl.multiple_of((tile // tile_cols) * TU, TU)
-            col0 = pl.multiple_of((tile % tile_cols) * TV, TV)
+            col = tile % tile_cols
 
             @pl.when(q < count)
             def _():
                 for p in range(2):
-                    out_ref[p, pl.ds(row0, TU), pl.ds(col0, TV)] += contrib[
-                        p * TU : (p + 1) * TU
-                    ]
+                    out_ref[p, col, pl.ds(row0, TU), :] += contrib[p * TU : (p + 1) * TU]
         return carry
 
     steps = (count + GROUP - 1) // GROUP
@@ -161,7 +154,7 @@
 def grid_into_slab(tile_ids, payload, slab_rows):
     return pl.pallas_call(
         grid_kernel,
-        out_shape=jax.ShapeDtypeStruct((2, slab_rows, GRID), jnp.float32),
+        out_shape=jax.ShapeDtypeStruct((2, GRID // TV, slab_rows, TV), jnp.float32),
         in_specs=[
             pl.BlockSpec(memory_space=pltpu.SMEM),
             pl.BlockSpec(memory_space=pltpu.VMEM),
@@ -220,16 +213,15 @@
     ).reshape((slot_count,) + payload.shape[1:])
     tile_ids = jnp.max(recv[:, PAY_ROWS - 1, :].astype(jnp.float32), axis=1).astype(jnp.int32)
     slab_grid = grid_into_slab(tile_ids, recv, slab_rows)
-    spec_real, spec_imag = transform_last(slab_grid[0], slab_grid[1])
-    spectrum = jnp.stack([spec_real, spec_imag]).reshape(2, slab_rows, row_count, GRID // row_count)
+    spectrum = transform_last(slab_grid)
     image_scale = 1.0 / math.sqrt(block_count * row_count * vis_count)
     offset_freq = (channel_freq[0] - 1.284) / 0.428
     weights = jnp.stack([jnp.ones_like(offset_freq), offset_freq, offset_freq * offset_freq])
     received = lax.all_to_all(
-        for_sending(spectrum), "row", split_axis=2, concat_axis=1, tiled=True
+        for_sending(spectrum), "row", split_axis=0, concat_axis=0, tiled=True
     ).astype(spectrum.dtype)
-    width_here = received.shape[2] * received.shape[3]
-    dirty_image = transform_first_real(received.reshape(2, GRID, width_here)) * image_scale
+    width_here = received.shape[3]
+    dirty_image = transform_first_real(received) * image_scale
     taylor_terms = (weights[:, None, None] * dirty_image[None]).astype(jnp.bfloat16)
     chips = lax.axis_size("z")
     pair = lax.axis_size("core")

time: 224 us -> 221 us (0.987)
  local copies, waits for them, and re-layouts: 15.2 us -> 9.97 us
  matrix products: 14.3 us -> 18.7 us
  starting transfers between devices: 29.4 us -> 27.1 us
    dot_general x3, matrix products: 10.2 us -> 14.6 us  [the longest x1 6.38 us: transform_last(): step = product('parb,pak->krb', both, complex_weights(cos_outer, sin_outer))]
    another operation x1 -> x2, local copies, waits for them, and re-layouts: 3.77 us -> 0.02 us  [complex_weights(): return jnp.stack([top, bottom])]
    convert_element_type x0 -> x1, local copies, waits for them, and re-layouts: none -> 2.97 us  [for_sending(): a.astype(jnp.bfloat16)]
    unnamed x6 -> x5, local copies, waits for them, and re-layouts: 5.54 us -> 2.6 us
    all_to_all x1, starting transfers between devices: 17 us -> 14.7 us  [shards(): lax.all_to_all(for_sending(spectrum), 'row', split_axis=0, concat_axis=0,...]
where the time goes in v7:
time: 221 us; the launch traced here: 220 us
  waiting for transfers between devices  126 us (57%)
  starting transfers between devices  27.1 us (12%)
  matrix products  18.7 us (8%)
  other arithmetic  14.6 us (7%)
  between operations  14.3 us (6%)
  local copies, waits for them, and re-layouts  9.97 us (5%)
  Pallas kernels  9.06 us (4%)
    reduce_scatter x1, waiting for transfers between devices, shards(): summed = lax.psum_scatter(partial_sum, 'z', scatter_dimension=1, tiled=True)  46.8 us
    all_to_all x1, waiting for transfers between devices, shards(): lax.all_to_all(for_sending(spectrum), 'row', split_axis=0, concat_axis=0,...  45.9 us
    all_to_all x1, waiting for transfers between devices, shards(): lax.all_to_all(send.reshape((row_count, capacity) + payload.shape[1:]), '...  29.5 us
    all_to_all x1, starting transfers between devices, shards(): lax.all_to_all(for_sending(spectrum), 'row', split_axis=0, concat_axis=0,...  14.7 us
    all_to_all x1, starting transfers between devices, shards(): lax.all_to_all(send.reshape((row_count, capacity) + payload.shape[1:]), '...  10.2 us
    pallas_call x1, Pallas kernels, grid_into_slab(): pl.pallas_call(grid_kernel, out_shape=jax.ShapeDtypeStruct((2, GRID // TV...  9.06 us
    dot_general x1, matrix products, transform_last(): step = product('parb,pak->krb', both, complex_weights(cos_outer, sin_outer))  6.38 us
    dot_general x1, matrix products, transform_last(): product('qkrb,qbsdm->drsmk', jnp.stack([twist_real, twist_imag]), weights)  5.95 us
  transfers between devices with their start and end apart: 4, of which 4 were waited for; matrix products, arithmetic and copies ran while one was open for 1% of the time, Pallas kernels for 0%

profile of v7, /device:TPU:6, one launch (start us, length us, event | category | flops | bytes accessed | tf_op | source)
XLA Modules:
  0.0 219.8 jit_solution(6148605565663099498)
XLA Ops:
  6.5 0.7 fusion.37
  7.4 0.8 select_reduce_fusion
  8.2 0.7 multiply_add_fusion
  8.9 0.8 bitcast_dynamic-update-slice_fusion.2
  9.6 0.7 convert_bitcast_fusion.1
  10.4 0.9 bitcast_dynamic-update-slice_fusion.1
  11.3 0.9 bitcast_dynamic-update-slice_fusion
  12.2 0.8 bitcast_dynamic-update-slice_fusion.4
  13.0 0.8 bitcast_dynamic-update-slice_fusion.3
  13.8 0.6 fusion.34
  14.8 1.3 copy.32
  16.0 10.2 %all-to-all-start = ((bf16[32,8,19,128]{3,1,2,0:T(8,128)(2,1)}), bf16[32,8,19,128]{3,1,2,0:T(8,128)(2,1)S(1)}, u32[]{:S(2)}, u32[]{:S(2)}) async-start(bf16[32,8,19,128]{3,1,2,0:T(8,128)(2,1)} %copy.32), calls=%async_computation | async-start | bytes 2490368 | tf_op jit(solution)/shard_map/all_to_all | solution.py:207
  27.2 29.5 %all-to-all-done = bf16[32,8,19,128]{3,1,2,0:T(8,128)(2,1)S(1)} async-done(((bf16[32,8,19,128]{3,1,2,0:T(8,128)(2,1)}), bf16[32,8,19,128]{3,1,2,0:T(8,128)(2,1)S(1)}, u32[]{:S(2)}, u32[]{:S(2)}) %all-to-all-start) | async-done | bytes 1245216 | tf_op jit(solution)/shard_map/all_to_all | solution.py:207
  57.1 1.0 slice_reduce_fusion
  58.2 0.6 convert_convert_fusion.tile_ref
  58.8 9.1 %shard_map.82 = f32[2,32,128,128]{3,2,1,0:T(8,128)} custom-call(s32[256]{0:T(256)} %convert_convert_fusion.tile_ref, bf16[256,19,128]{2,1,0:T(8,128)(2,1)} %bitcast.74), custom_call_target="tpu_custom_call" | custom-call | tf_op jit(solution)/shard_map/pallas_call | solution.py:155
  67.8 6.4 %fusion.7 = f32[64,128,128]{2,0,1:T(8,128)S(1)} fusion(f32[2,32,128,128]{3,2,1,0:T(8,128)} %shard_map.82, f32[1,32,64]{2,1,0:T(8,128)S(1)} %get-tuple-element.24, f32[1,32,64]{2,1,0:T(8,128)S(1)} %get-tuple-element.23), kind=kOutput, calls=%fused_computation.12 | convolution fusion | flops 402657280 | bytes 8404992 | tf_op jit(solution)/shard_map/parb,pak->krb/dot_general | solution.py:64
  74.2 0.7 subtract_bitcast_fusion.1
  75.3 6.0 %bitcast_convert_fusion = bf16[2,32,4,32,128]{4,1,3,2,0:T(8,128)(2,1)S(1)} fusion(f32[2,32,128,128,1,1]{3,1,2,0,5,4:T(8,128)S(1)} %maximum_bitcast_fusion, f32[1,128,2,32,4]{1,3,0,4,2:T(8,128)S(1)} %copy.30, f32[1,128,2,32,4]{1,3,0,4,2:T(8,128)S(1)} %copy.29), kind=kOutput, calls=%fused_computation.3 | convolution fusion | flops 1611726848 | bytes 6553600 | tf_op jit(solution)/shard_map/qkrb,qbsdm->drsmk/dot_general | solution.py:73
  81.3 3.0 %copy.36 = bf16[32,128,2,128]{3,2,1,0:T(2,128)(2,1)} copy(bf16[32,128,2,128]{1,0,3,2:T(8,128)(2,1)S(1)} %bitcast.71) | data formatting | bytes 4194304 | tf_op jit(solution)/shard_map/convert_element_type | solution.py:17
  84.3 14.7 %all-to-all-start.1 = ((bf16[32,128,2,128]{3,2,1,0:T(2,128)(2,1)}), bf16[32,128,2,128]{3,2,1,0:T(2,128)(2,1)S(1)}, u32[]{:S(2)}, u32[]{:S(2)}) async-start(bf16[32,128,2,128]{3,2,1,0:T(2,128)(2,1)} %copy.36), calls=%async_computation.1 | async-start | bytes 4194304 | tf_op jit(solution)/shard_map/all_to_all | solution.py:220
  100.5 45.9 %all-to-all-done.1 = bf16[32,128,2,128]{3,2,1,0:T(2,128)(2,1)S(1)} async-done(((bf16[32,128,2,128]{3,2,1,0:T(2,128)(2,1)}), bf16[32,128,2,128]{3,2,1,0:T(2,128)(2,1)S(1)}, u32[]{:S(2)}, u32[]{:S(2)}) %all-to-all-start.1) | async-done | bytes 2097184 | tf_op jit(solution)/shard_map/all_to_all | solution.py:220
  146.4 2.3 %convolution_bitcast_fusion = f32[64,128,128]{2,0,1:T(8,128)S(1)} fusion(bf16[32,128,2,128]{3,2,1,0:T(2,128)(2,1)S(1)} %all-to-all-done.1, f32[1,32,64]{2,1,0:T(8,128)S(1)} %get-tuple-element.24, f32[1,32,64]{2,1,0:T(8,128)S(1)} %get-tuple-element.23), kind=kOutput, calls=%fused_computation.13 | convolution fusion | flops 402657280 | bytes 6307840 | tf_op jit(solution)/shard_map/abpc,pak->kbc/dot_general | solution.py:82
  148.7 1.4 subtract_bitcast_fusion
  150.5 3.5 %bitcast_multiply_fusion = f32[128,32,128]{2,0,1:T(8,128)S(1)} fusion(f32[2,32,128,128]{3,1,2,0:T(8,128)S(1)} %pad_maximum_fusion, f32[1,128,128]{1,2,0:T(8,128)S(1)} %get-tuple-element.31, f32[1,128,128]{1,2,0:T(8,128)S(1)} %get-tuple-element.32), kind=kOutput, calls=%fused_computation.14 | convolution fusion | flops 805863424 | bytes 6422528 | tf_op jit(solution)/shard_map/qkbc,qbm->mkc/dot_general | solution.py:87
  154.0 1.2 copy.41
  155.3 0.9 multiply_convert_fusion
  156.1 1.3 dynamic-slice_bitcast_fusion
  157.4 1.9 collective-permute-start
  159.3 3.7 %collective-permute-done = bf16[3,8,256,128]{3,2,0,1:T(8,128)(2,1)} collective-permute-done((bf16[3,8,256,128]{3,2,0,1:T(8,128)(2,1)}, bf16[3,8,256,128]{3,2,0,1:T(8,128)(2,1)}, u32[]{:S(2)}, u32[]{:S(2)}) %collective-permute-start) | collective-permute-done | bytes 1572896 | tf_op jit(solution)/shard_map/ppermute | solution.py:232
  163.0 3.1 %fusion.6 = bf16[3,8,256,128]{3,2,0,1:T(8,128)(2,1)} fusion(bf16[3,8,256,128]{3,2,0,1:T(8,128)(2,1)} %collective-permute-done, bf16[3,8,2,256,128]{4,3,0,1,2:T(8,128)(2,1)S(1)} %multiply_convert_fusion, s32[]{:T(128)S(6)} %select_n.91), kind=kLoop, calls=%fused_computation.11 | loop fusion | flops 3145728 | bytes 4718596 | tf_op jit(solution)/shard_map/convert_element_type | solution.py:233
  166.1 46.8 %reduce-scatter.2.cloned.1.call-done = bf16[3,1,256,128]{3,2,0,1:T(8,128)(2,1)} async-done(((bf16[3,8,256,128]{3,2,0,1:T(8,128)(2,1)}), bf16[3,1,256,128]{3,2,0,1:T(8,128)(2,1)}) %reduce-scatter.2.cloned.1.call-update) | async-done | bytes 196624 | tf_op jit(solution)/shard_map/reduce_scatter | solution.py:234
  (26 shorter events, 3.6 us)
Async XLA Ops:
  16.0 40.7 %all-to-all-start = ((bf16[32,8,19,128]{3,1,2,0:T(8,128)(2,1)}), bf16[32,8,19,128]{3,1,2,0:T(8,128)(2,1)S(1)}, u32[]{:S(2)}, u32[]{:S(2)}) async-start(bf16[32,8,19,128]{3,1,2,0:T(8,128)(2,1)} %copy.32), calls=%async_computation | async-start | bytes 2490368 | tf_op jit(solution)/shard_map/all_to_all | solution.py:207
  57.1 1.6 copy-start
  84.3 62.1 %all-to-all-start.1 = ((bf16[32,128,2,128]{3,2,1,0:T(2,128)(2,1)}), bf16[32,128,2,128]{3,2,1,0:T(2,128)(2,1)S(1)}, u32[]{:S(2)}, u32[]{:S(2)}) async-start(bf16[32,128,2,128]{3,2,1,0:T(2,128)(2,1)} %copy.36), calls=%async_computation.1 | async-start | bytes 4194304 | tf_op jit(solution)/shard_map/all_to_all | solution.py:220
  99.0 114.0 %reduce-scatter.2.cloned.1.call-start = ((), (), s32[]{:S(2)}) async-start(), calls=%async_computation.3 | async-start | bytes 1769472 | tf_op jit(solution)/shard_map/reduce_scatter | solution.py:234
  157.4 5.6 %collective-permute-start = (bf16[3,8,256,128]{3,2,0,1:T(8,128)(2,1)}, bf16[3,8,256,128]{3,2,0,1:T(8,128)(2,1)}, u32[]{:S(2)}, u32[]{:S(2)}) collective-permute-start(bf16[3,8,256,128]{3,2,0,1:T(8,128)(2,1)} %dynamic-slice_bitcast_fusion), channel_id=1, source_target_pairs={{0,32},{32,0},{1,33},{33,1},{2,34},{34,2},{3,35},{35,3},{4,36},{36... | collective-permute-start | bytes 4718600 | tf_op jit(solution)/shard_map/ppermute | solution.py:232
Sparse Core Ops, SparseCore 0:
  166.2 46.6 reduce-scatter.1

commit v8 on v7

--- a/solution.py
+++ b/solution.py
@@ -222,15 +222,18 @@
     ).astype(spectrum.dtype)
     width_here = received.shape[3]
     dirty_image = transform_first_real(received) * image_scale
-    taylor_terms = (weights[:, None, None] * dirty_image[None]).astype(jnp.bfloat16)
     chips = lax.axis_size("z")
     pair = lax.axis_size("core")
     core = lax.axis_index("core")
-    terms = taylor_terms.reshape(3, chips, pair, GRID // chips // pair, width_here)
-    keep = lax.dynamic_index_in_dim(terms, core, axis=2, keepdims=False)
-    give = lax.dynamic_index_in_dim(terms, pair - 1 - core, axis=2, keepdims=False)
-    got = lax.ppermute(give, "core", [(0, 1), (1, 0)])
-    partial_sum = (keep.astype(jnp.float32) + got.astype(jnp.float32)).astype(jnp.bfloat16)
+    halves = dirty_image.reshape(chips, pair, GRID // chips // pair, width_here)
+    keep = lax.dynamic_index_in_dim(halves, core, axis=1, keepdims=False)
+    give = lax.dynamic_index_in_dim(halves, pair - 1 - core, axis=1, keepdims=False)
+    swap = [(0, 1), (1, 0)]
+    got = lax.ppermute(give, "core", swap)
+    got_weights = lax.ppermute(weights, "core", swap)
+    mine = (weights[:, None, None, None] * keep[None]).astype(jnp.bfloat16)
+    theirs = (got_weights[:, None, None, None] * got[None]).astype(jnp.bfloat16)
+    partial_sum = (mine.astype(jnp.float32) + theirs.astype(jnp.float32)).astype(jnp.bfloat16)
     summed = lax.psum_scatter(partial_sum, "z", scatter_dimension=1, tiled=True)
     summed = summed.reshape(3, GRID // chips // pair, width_here)
     return summed

time: 221 us -> 216 us (0.977)
  waiting for transfers between devices: 126 us -> 121 us
    ppermute x1 -> x2, waiting for transfers between devices: 3.72 us -> 0.8 us  [the longest x1 0.8 us: shards(): got_weights = lax.ppermute(weights, 'core', swap)]
    ppermute x1 -> x2, starting transfers between devices: 1.91 us -> 4.32 us  [the longest x1 2.4 us: shards(): got_weights = lax.ppermute(weights, 'core', swap)]
    convert_element_type x2 -> x1, other arithmetic: 3.91 us -> 1.67 us  [shards(): (mine.astype(jnp.float32) + theirs.astype(jnp.float32)).astype(jnp.bfloat16)]
  transfers between devices with their start and end apart: 4 -> 5, of which waited for: 4 -> 4; matrix products, arithmetic and copies ran while one was open for 1% -> 1% of each run, Pallas kernels for 0% -> 0%
where the time goes in v8:
time: 216 us; the launch traced here: 213 us
  waiting for transfers between devices  121 us (56%)
  starting transfers between devices  28.9 us (13%)
  matrix products  18.7 us (9%)
  between operations  14.3 us (7%)
  other arithmetic  12.4 us (6%)
  local copies, waits for them, and re-layouts  8.88 us (4%)
  Pallas kernels  8.7 us (4%)
    reduce_scatter x1, waiting for transfers between devices, shards(): summed = lax.psum_scatter(partial_sum, 'z', scatter_dimension=1, tiled=True)  46.2 us
    all_to_all x1, waiting for transfers between devices, shards(): lax.all_to_all(for_sending(spectrum), 'row', split_axis=0, concat_axis=0,...  44.9 us
    all_to_all x1, waiting for transfers between devices, shards(): lax.all_to_all(send.reshape((row_count, capacity) + payload.shape[1:]), '...  29.5 us
    all_to_all x1, starting transfers between devices, shards(): lax.all_to_all(for_sending(spectrum), 'row', split_axis=0, concat_axis=0,...  14.1 us
    all_to_all x1, starting transfers between devices, shards(): lax.all_to_all(send.reshape((row_count, capacity) + payload.shape[1:]), '...  10.2 us
    pallas_call x1, Pallas kernels, grid_into_slab(): pl.pallas_call(grid_kernel, out_shape=jax.ShapeDtypeStruct((2, GRID // TV...  8.7 us
    dot_general x1, matrix products, transform_last(): step = product('parb,pak->krb', both, complex_weights(cos_outer, sin_outer))  6.38 us
    dot_general x1, matrix products, transform_last(): product('qkrb,qbsdm->drsmk', jnp.stack([twist_real, twist_imag]), weights)  5.95 us
  transfers between devices with their start and end apart: 5, of which 4 were waited for; matrix products, arithmetic and copies ran while one was open for 1% of the time, Pallas kernels for 0%

profile of v8, /device:TPU:6, one launch (start us, length us, event | category | flops | bytes accessed | tf_op | source)
XLA Modules:
  0.0 213.4 jit_solution(1076731107795238566)
XLA Ops:
  6.5 0.7 fusion.36
  7.4 0.8 select_reduce_fusion
  8.2 0.7 multiply_add_fusion
  8.9 0.8 bitcast_dynamic-update-slice_fusion.2
  9.6 0.7 convert_bitcast_fusion.1
  10.4 0.9 bitcast_dynamic-update-slice_fusion.1
  11.3 0.9 bitcast_dynamic-update-slice_fusion
  12.2 0.8 bitcast_dynamic-update-slice_fusion.4
  13.0 0.8 bitcast_dynamic-update-slice_fusion.3
  13.8 0.6 fusion.33
  14.8 1.3 copy.31
  16.0 10.2 %all-to-all-start = ((bf16[32,8,19,128]{3,1,2,0:T(8,128)(2,1)}), bf16[32,8,19,128]{3,1,2,0:T(8,128)(2,1)S(1)}, u32[]{:S(2)}, u32[]{:S(2)}) async-start(bf16[32,8,19,128]{3,1,2,0:T(8,128)(2,1)} %copy.31), calls=%async_computation | async-start | bytes 2490368 | tf_op jit(solution)/shard_map/all_to_all | solution.py:207
  27.2 29.5 %all-to-all-done = bf16[32,8,19,128]{3,1,2,0:T(8,128)(2,1)S(1)} async-done(((bf16[32,8,19,128]{3,1,2,0:T(8,128)(2,1)}), bf16[32,8,19,128]{3,1,2,0:T(8,128)(2,1)S(1)}, u32[]{:S(2)}, u32[]{:S(2)}) %all-to-all-start) | async-done | bytes 1245216 | tf_op jit(solution)/shard_map/all_to_all | solution.py:207
  57.2 1.0 slice_reduce_fusion
  58.2 0.6 convert_convert_fusion.tile_ref
  58.8 8.7 %shard_map.82 = f32[2,32,128,128]{3,2,1,0:T(8,128)} custom-call(s32[256]{0:T(256)} %convert_convert_fusion.tile_ref, bf16[256,19,128]{2,1,0:T(8,128)(2,1)} %bitcast.73), custom_call_target="tpu_custom_call" | custom-call | tf_op jit(solution)/shard_map/pallas_call | solution.py:155
  67.5 6.4 %fusion.6 = f32[64,128,128]{2,0,1:T(8,128)S(1)} fusion(f32[2,32,128,128]{3,2,1,0:T(8,128)} %shard_map.82, f32[1,32,64]{2,1,0:T(8,128)S(1)} %get-tuple-element.26, f32[1,32,64]{2,1,0:T(8,128)S(1)} %get-tuple-element.25), kind=kOutput, calls=%fused_computation.12 | convolution fusion | flops 402657280 | bytes 8404992 | tf_op jit(solution)/shard_map/parb,pak->krb/dot_general | solution.py:64
  73.9 0.7 subtract_bitcast_fusion.1
  74.5 0.4 maximum_bitcast_fusion
  75.0 6.0 %bitcast_convert_fusion = bf16[2,32,4,32,128]{4,1,3,2,0:T(8,128)(2,1)S(1)} fusion(f32[2,32,128,128,1,1]{3,1,2,0,5,4:T(8,128)S(1)} %maximum_bitcast_fusion, f32[1,128,2,32,4]{1,3,0,4,2:T(8,128)S(1)} %copy.29, f32[1,128,2,32,4]{1,3,0,4,2:T(8,128)S(1)} %copy.28), kind=kOutput, calls=%fused_computation.2 | convolution fusion | flops 1611726848 | bytes 6553600 | tf_op jit(solution)/shard_map/qkrb,qbsdm->drsmk/dot_general | solution.py:73
  80.9 3.0 %copy.35 = bf16[32,128,2,128]{3,2,1,0:T(2,128)(2,1)} copy(bf16[32,128,2,128]{1,0,3,2:T(8,128)(2,1)S(1)} %bitcast.70) | data formatting | bytes 4194304 | tf_op jit(solution)/shard_map/convert_element_type | solution.py:17
  83.9 14.1 %all-to-all-start.1 = ((bf16[32,128,2,128]{3,2,1,0:T(2,128)(2,1)}), bf16[32,128,2,128]{3,2,1,0:T(2,128)(2,1)S(1)}, u32[]{:S(2)}, u32[]{:S(2)}) async-start(bf16[32,128,2,128]{3,2,1,0:T(2,128)(2,1)} %copy.35), calls=%async_computation.1 | async-start | bytes 4194304 | tf_op jit(solution)/shard_map/all_to_all | solution.py:220
  98.8 44.9 %all-to-all-done.1 = bf16[32,128,2,128]{3,2,1,0:T(2,128)(2,1)S(1)} async-done(((bf16[32,128,2,128]{3,2,1,0:T(2,128)(2,1)}), bf16[32,128,2,128]{3,2,1,0:T(2,128)(2,1)S(1)}, u32[]{:S(2)}, u32[]{:S(2)}) %all-to-all-start.1) | async-done | bytes 2097184 | tf_op jit(solution)/shard_map/all_to_all | solution.py:220
  143.7 2.3 %convolution_bitcast_fusion = f32[64,128,128]{2,0,1:T(8,128)S(1)} fusion(bf16[32,128,2,128]{3,2,1,0:T(2,128)(2,1)S(1)} %all-to-all-done.1, f32[1,32,64]{2,1,0:T(8,128)S(1)} %get-tuple-element.26, f32[1,32,64]{2,1,0:T(8,128)S(1)} %get-tuple-element.25), kind=kOutput, calls=%fused_computation.13 | convolution fusion | flops 402657280 | bytes 6307840 | tf_op jit(solution)/shard_map/abpc,pak->kbc/dot_general | solution.py:82
  146.0 1.4 subtract_bitcast_fusion
  147.8 3.5 %bitcast_multiply_fusion = f32[128,32,128]{2,0,1:T(8,128)S(1)} fusion(f32[2,32,128,128]{3,1,2,0:T(8,128)S(1)} %pad_maximum_fusion, f32[1,128,128]{1,2,0:T(8,128)S(1)} %get-tuple-element.33, f32[1,128,128]{1,2,0:T(8,128)S(1)} %get-tuple-element.34), kind=kOutput, calls=%fused_computation.14 | convolution fusion | flops 805863424 | bytes 6422528 | tf_op jit(solution)/shard_map/qkbc,qbm->mkc/dot_general | solution.py:87
  151.3 1.2 copy.40
  152.8 1.9 collective-permute-start.1
  155.4 2.4 %collective-permute-start = (f32[3]{0:T(128)S(1)}, f32[3]{0:T(128)S(1)}, u32[]{:S(2)}, u32[]{:S(2)}) collective-permute-start(f32[3]{0:T(128)S(1)} %pad_maximum_fusion.3), channel_id=1, source_target_pairs={{0,32},{32,0},{1,33},{33,1},{2,34},{34,2},{3,35},{35,3},{4,36},{36... | collective-permute-start | bytes 44 | tf_op jit(solution)/shard_map/ppermute | solution.py:233
  157.8 0.8 collective-permute-done
  158.6 1.7 add_convert_fusion
  160.3 46.2 %reduce-scatter.2.cloned.1.call-done = bf16[3,1,256,128]{3,2,0,1:T(8,128)(2,1)} async-done(((bf16[3,8,256,128]{3,2,0,1:T(8,128)(2,1)}), bf16[3,1,256,128]{3,2,0,1:T(8,128)(2,1)}) %reduce-scatter.2.cloned.1.call-update) | async-done | bytes 196624 | tf_op jit(solution)/shard_map/reduce_scatter | solution.py:237
  (27 shorter events, 3.3 us)
Async XLA Ops:
  16.0 40.7 %all-to-all-start = ((bf16[32,8,19,128]{3,1,2,0:T(8,128)(2,1)}), bf16[32,8,19,128]{3,1,2,0:T(8,128)(2,1)S(1)}, u32[]{:S(2)}, u32[]{:S(2)}) async-start(bf16[32,8,19,128]{3,1,2,0:T(8,128)(2,1)} %copy.31), calls=%async_computation | async-start | bytes 2490368 | tf_op jit(solution)/shard_map/all_to_all | solution.py:207
  57.1 1.6 copy-start
  83.9 59.8 %all-to-all-start.1 = ((bf16[32,128,2,128]{3,2,1,0:T(2,128)(2,1)}), bf16[32,128,2,128]{3,2,1,0:T(2,128)(2,1)S(1)}, u32[]{:S(2)}, u32[]{:S(2)}) async-start(bf16[32,128,2,128]{3,2,1,0:T(2,128)(2,1)} %copy.35), calls=%async_computation.1 | async-start | bytes 4194304 | tf_op jit(solution)/shard_map/all_to_all | solution.py:220
  98.0 108.5 %reduce-scatter.2.cloned.1.call-start = ((), (), s32[]{:S(2)}) async-start(), calls=%async_computation.3 | async-start | bytes 1769472 | tf_op jit(solution)/shard_map/reduce_scatter | solution.py:237
  152.8 5.9 %collective-permute-start.1 = (f32[8,256,128]{2,1,0:T(8,128)S(1)}, f32[8,256,128]{2,1,0:T(8,128)S(1)}, u32[]{:S(2)}, u32[]{:S(2)}) collective-permute-start(f32[8,256,128]{2,1,0:T(8,128)S(1)} %get-tuple-element.22), channel_id=1, source_target_pairs={{0,32},{32,0},{1,33},{33,1},{2,34},{34,2},{3,35},{35,3},{4,36},{36... | collective-permute-start | bytes 3145736 | tf_op jit(solution)/shard_map/ppermute | solution.py:232
  155.4 3.2 %collective-permute-start = (f32[3]{0:T(128)S(1)}, f32[3]{0:T(128)S(1)}, u32[]{:S(2)}, u32[]{:S(2)}) collective-permute-start(f32[3]{0:T(128)S(1)} %pad_maximum_fusion.3), channel_id=1, source_target_pairs={{0,32},{32,0},{1,33},{33,1},{2,34},{34,2},{3,35},{35,3},{4,36},{36... | collective-permute-start | bytes 44 | tf_op jit(solution)/shard_map/ppermute | solution.py:233
Sparse Core Ops, SparseCore 0:
  160.4 46.0 reduce-scatter.1

commit v9 on v8

--- a/solution.py
+++ b/solution.py
@@ -229,8 +229,10 @@
     keep = lax.dynamic_index_in_dim(halves, core, axis=1, keepdims=False)
     give = lax.dynamic_index_in_dim(halves, pair - 1 - core, axis=1, keepdims=False)
     swap = [(0, 1), (1, 0)]
-    got = lax.ppermute(give, "core", swap)
-    got_weights = lax.ppermute(weights, "core", swap)
+    packed = jnp.concatenate([give.reshape(-1), weights])
+    got_packed = lax.ppermute(packed, "core", swap)
+    got = got_packed[: give.size].reshape(give.shape)
+    got_weights = got_packed[give.size :]
     mine = (weights[:, None, None, None] * keep[None]).astype(jnp.bfloat16)
     theirs = (got_weights[:, None, None, None] * got[None]).astype(jnp.bfloat16)
     partial_sum = (mine.astype(jnp.float32) + theirs.astype(jnp.float32)).astype(jnp.bfloat16)

time: 216 us -> 217 us (level)
  waiting for transfers between devices: 121 us -> 125 us
    all_to_all x1, starting transfers between devices: 14.1 us -> 16.8 us  [shards(): lax.all_to_all(for_sending(spectrum), 'row', split_axis=0, concat_axis=0,...]
    ppermute x2 -> x1, starting transfers between devices: 4.32 us -> 1.91 us  [shards(): got_packed = lax.ppermute(packed, 'core', swap)]
  transfers between devices with their start and end apart: 5 -> 4, of which waited for: 4 -> 4; matrix products, arithmetic and copies ran while one was open for 1% -> 1% of each run, Pallas kernels for 0% -> 0%
where the time goes in v9:
time: 217 us; the launch traced here: 216 us
  waiting for transfers between devices  125 us (58%)
  starting transfers between devices  29.2 us (13%)
  matrix products  18.7 us (9%)
  between operations  14.3 us (7%)
  other arithmetic  12.4 us (6%)
  local copies, waits for them, and re-layouts  9.5 us (4%)
  Pallas kernels  7.14 us (3%)
    reduce_scatter x1, waiting for transfers between devices, shards(): summed = lax.psum_scatter(partial_sum, 'z', scatter_dimension=1, tiled=True)  46.8 us
    all_to_all x1, waiting for transfers between devices, shards(): lax.all_to_all(for_sending(spectrum), 'row', split_axis=0, concat_axis=0,...  46 us
    all_to_all x1, waiting for transfers between devices, shards(): lax.all_to_all(send.reshape((row_count, capacity) + payload.shape[1:]), '...  29.5 us
    all_to_all x1, starting transfers between devices, shards(): lax.all_to_all(for_sending(spectrum), 'row', split_axis=0, concat_axis=0,...  16.8 us
    all_to_all x1, starting transfers between devices, shards(): lax.all_to_all(send.reshape((row_count, capacity) + payload.shape[1:]), '...  10.2 us
    pallas_call x1, Pallas kernels, grid_into_slab(): pl.pallas_call(grid_kernel, out_shape=jax.ShapeDtypeStruct((2, GRID // TV...  7.14 us
    dot_general x1, matrix products, transform_last(): step = product('parb,pak->krb', both, complex_weights(cos_outer, sin_outer))  6.39 us
    dot_general x1, matrix products, transform_last(): product('qkrb,qbsdm->drsmk', jnp.stack([twist_real, twist_imag]), weights)  5.95 us
  transfers between devices with their start and end apart: 4, of which 4 were waited for; matrix products, arithmetic and copies ran while one was open for 1% of the time, Pallas kernels for 0%

profile of v9, /device:TPU:6, one launch (start us, length us, event | category | flops | bytes accessed | tf_op | source)
XLA Modules:
  0.0 216.1 jit_solution(6272484216334555118)
XLA Ops:
  6.5 0.7 fusion.36
  7.4 0.8 select_reduce_fusion
  8.2 0.7 multiply_add_fusion
  8.9 0.8 bitcast_dynamic-update-slice_fusion.2
  9.6 0.7 convert_bitcast_fusion.1
  10.4 0.9 bitcast_dynamic-update-slice_fusion.1
  11.3 0.9 bitcast_dynamic-update-slice_fusion
  12.2 0.8 bitcast_dynamic-update-slice_fusion.4
  13.0 0.8 bitcast_dynamic-update-slice_fusion.3
  13.8 0.6 fusion.33
  14.8 1.3 copy.31
  16.0 10.2 %all-to-all-start = ((bf16[32,8,19,128]{3,1,2,0:T(8,128)(2,1)}), bf16[32,8,19,128]{3,1,2,0:T(8,128)(2,1)S(1)}, u32[]{:S(2)}, u32[]{:S(2)}) async-start(bf16[32,8,19,128]{3,1,2,0:T(8,128)(2,1)} %copy.31), calls=%async_computation | async-start | bytes 2490368 | tf_op jit(solution)/shard_map/all_to_all | solution.py:207
  27.2 29.5 %all-to-all-done = bf16[32,8,19,128]{3,1,2,0:T(8,128)(2,1)S(1)} async-done(((bf16[32,8,19,128]{3,1,2,0:T(8,128)(2,1)}), bf16[32,8,19,128]{3,1,2,0:T(8,128)(2,1)S(1)}, u32[]{:S(2)}, u32[]{:S(2)}) %all-to-all-start) | async-done | bytes 1245216 | tf_op jit(solution)/shard_map/all_to_all | solution.py:207
  57.1 1.0 slice_reduce_fusion
  58.2 0.6 convert_convert_fusion.tile_ref
  58.7 7.1 %shard_map.82 = f32[2,32,128,128]{3,2,1,0:T(8,128)} custom-call(s32[256]{0:T(256)} %convert_convert_fusion.tile_ref, bf16[256,19,128]{2,1,0:T(8,128)(2,1)} %bitcast.73), custom_call_target="tpu_custom_call" | custom-call | tf_op jit(solution)/shard_map/pallas_call | solution.py:155
  65.9 6.4 %fusion.6 = f32[64,128,128]{2,0,1:T(8,128)S(1)} fusion(f32[2,32,128,128]{3,2,1,0:T(8,128)} %shard_map.82, f32[1,32,64]{2,1,0:T(8,128)S(1)} %get-tuple-element.26, f32[1,32,64]{2,1,0:T(8,128)S(1)} %get-tuple-element.25), kind=kOutput, calls=%fused_computation.12 | convolution fusion | flops 402657280 | bytes 8404992 | tf_op jit(solution)/shard_map/parb,pak->krb/dot_general | solution.py:64
  72.3 0.7 subtract_bitcast_fusion.1
  73.0 0.4 maximum_bitcast_fusion
  73.4 6.0 %bitcast_convert_fusion = bf16[2,32,4,32,128]{4,1,3,2,0:T(8,128)(2,1)S(1)} fusion(f32[2,32,128,128,1,1]{3,1,2,0,5,4:T(8,128)S(1)} %maximum_bitcast_fusion, f32[1,128,2,32,4]{1,3,0,4,2:T(8,128)S(1)} %copy.29, f32[1,128,2,32,4]{1,3,0,4,2:T(8,128)S(1)} %copy.28), kind=kOutput, calls=%fused_computation.2 | convolution fusion | flops 1611726848 | bytes 6553600 | tf_op jit(solution)/shard_map/qkrb,qbsdm->drsmk/dot_general | solution.py:73
  79.4 3.0 %copy.35 = bf16[32,128,2,128]{3,2,1,0:T(2,128)(2,1)} copy(bf16[32,128,2,128]{1,0,3,2:T(8,128)(2,1)S(1)} %bitcast.70) | data formatting | bytes 4194304 | tf_op jit(solution)/shard_map/convert_element_type | solution.py:17
  82.3 16.8 %all-to-all-start.1 = ((bf16[32,128,2,128]{3,2,1,0:T(2,128)(2,1)}), bf16[32,128,2,128]{3,2,1,0:T(2,128)(2,1)S(1)}, u32[]{:S(2)}, u32[]{:S(2)}) async-start(bf16[32,128,2,128]{3,2,1,0:T(2,128)(2,1)} %copy.35), calls=%async_computation.1 | async-start | bytes 4194304 | tf_op jit(solution)/shard_map/all_to_all | solution.py:220
  100.6 46.0 %all-to-all-done.1 = bf16[32,128,2,128]{3,2,1,0:T(2,128)(2,1)S(1)} async-done(((bf16[32,128,2,128]{3,2,1,0:T(2,128)(2,1)}), bf16[32,128,2,128]{3,2,1,0:T(2,128)(2,1)S(1)}, u32[]{:S(2)}, u32[]{:S(2)}) %all-to-all-start.1) | async-done | bytes 2097184 | tf_op jit(solution)/shard_map/all_to_all | solution.py:220
  146.5 2.3 %convolution_bitcast_fusion = f32[64,128,128]{2,0,1:T(8,128)S(1)} fusion(bf16[32,128,2,128]{3,2,1,0:T(2,128)(2,1)S(1)} %all-to-all-done.1, f32[1,32,64]{2,1,0:T(8,128)S(1)} %get-tuple-element.26, f32[1,32,64]{2,1,0:T(8,128)S(1)} %get-tuple-element.25), kind=kOutput, calls=%fused_computation.13 | convolution fusion | flops 402657280 | bytes 6307840 | tf_op jit(solution)/shard_map/abpc,pak->kbc/dot_general | solution.py:82
  148.8 1.4 subtract_bitcast_fusion
  150.7 3.5 %bitcast_multiply_fusion = f32[128,32,128]{2,0,1:T(8,128)S(1)} fusion(f32[2,32,128,128]{3,1,2,0:T(8,128)S(1)} %pad_maximum_fusion, f32[1,128,128]{1,2,0:T(8,128)S(1)} %get-tuple-element.33, f32[1,128,128]{1,2,0:T(8,128)S(1)} %get-tuple-element.34), kind=kOutput, calls=%fused_computation.14 | convolution fusion | flops 805863424 | bytes 6422528 | tf_op jit(solution)/shard_map/qkbc,qbm->mkc/dot_general | solution.py:87
  154.2 1.2 copy.40
  155.6 0.6 concatenate.29
  156.2 1.9 collective-permute-start
  158.2 2.6 %collective-permute-done = f32[262147]{0:T(1024)S(1)} collective-permute-done((f32[262147]{0:T(1024)S(1)}, f32[262147]{0:T(1024)S(1)}, u32[]{:S(2)}, u32[]{:S(2)}) %collective-permute-start) | collective-permute-done | bytes 1048620 | tf_op jit(solution)/shard_map/ppermute | solution.py:233
  160.8 1.7 add_convert_fusion
  162.5 46.8 %reduce-scatter.2.cloned.1.call-done = bf16[3,1,256,128]{3,2,0,1:T(8,128)(2,1)} async-done(((bf16[3,8,256,128]{3,2,0,1:T(8,128)(2,1)}), bf16[3,1,256,128]{3,2,0,1:T(8,128)(2,1)}) %reduce-scatter.2.cloned.1.call-update) | async-done | bytes 196624 | tf_op jit(solution)/shard_map/reduce_scatter | solution.py:239
  (28 shorter events, 3.4 us)
Async XLA Ops:
  16.0 40.7 %all-to-all-start = ((bf16[32,8,19,128]{3,1,2,0:T(8,128)(2,1)}), bf16[32,8,19,128]{3,1,2,0:T(8,128)(2,1)S(1)}, u32[]{:S(2)}, u32[]{:S(2)}) async-start(bf16[32,8,19,128]{3,1,2,0:T(8,128)(2,1)} %copy.31), calls=%async_computation | async-start | bytes 2490368 | tf_op jit(solution)/shard_map/all_to_all | solution.py:207
  57.1 1.6 copy-start
  82.3 64.2 %all-to-all-start.1 = ((bf16[32,128,2,128]{3,2,1,0:T(2,128)(2,1)}), bf16[32,128,2,128]{3,2,1,0:T(2,128)(2,1)S(1)}, u32[]{:S(2)}, u32[]{:S(2)}) async-start(bf16[32,128,2,128]{3,2,1,0:T(2,128)(2,1)} %copy.35), calls=%async_computation.1 | async-start | bytes 4194304 | tf_op jit(solution)/shard_map/all_to_all | solution.py:220
  99.1 110.1 %reduce-scatter.2.cloned.1.call-start = ((), (), s32[]{:S(2)}) async-start(), calls=%async_computation.3 | async-start | bytes 1769472 | tf_op jit(solution)/shard_map/reduce_scatter | solution.py:239
  156.2 4.5 %collective-permute-start = (f32[262147]{0:T(1024)S(1)}, f32[262147]{0:T(1024)S(1)}, u32[]{:S(2)}, u32[]{:S(2)}) collective-permute-start(f32[262147]{0:T(1024)S(1)} %concatenate.29), channel_id=1, source_target_pairs={{0,32},{32,0},{1,33},{33,1},{2,34},{34,2},{3,35},{35,3},{4,36},{36... | collective-permute-start | bytes 3145772 | tf_op jit(solution)/shard_map/ppermute | solution.py:233
Sparse Core Ops, SparseCore 0:
  162.6 46.6 reduce-scatter.1

commit v10 on v8

--- a/solution.py
+++ b/solution.py
@@ -215,8 +215,15 @@
     slab_grid = grid_into_slab(tile_ids, recv, slab_rows)
     spectrum = transform_last(slab_grid)
     image_scale = 1.0 / math.sqrt(block_count * row_count * vis_count)
-    offset_freq = (channel_freq[0] - 1.284) / 0.428
-    weights = jnp.stack([jnp.ones_like(offset_freq), offset_freq, offset_freq * offset_freq])
+    def weights_of(frequency):
+        offset = (frequency - 1.284) / 0.428
+        return jnp.stack([jnp.ones_like(offset), offset, offset * offset])
+
+    here = lax.axis_index("z") * lax.axis_size("core") + lax.axis_index("core")
+    weights = weights_of(lax.dynamic_index_in_dim(channel_freq, here, keepdims=False))
+    partner_weights = weights_of(
+        lax.dynamic_index_in_dim(channel_freq, here + 1 - 2 * lax.axis_index("core"), keepdims=False)
+    )
     received = lax.all_to_all(
         for_sending(spectrum), "row", split_axis=0, concat_axis=0, tiled=True
     ).astype(spectrum.dtype)
@@ -230,7 +237,7 @@
     give = lax.dynamic_index_in_dim(halves, pair - 1 - core, axis=1, keepdims=False)
     swap = [(0, 1), (1, 0)]
     got = lax.ppermute(give, "core", swap)
-    got_weights = lax.ppermute(weights, "core", swap)
+    got_weights = partner_weights
     mine = (weights[:, None, None, None] * keep[None]).astype(jnp.bfloat16)
     theirs = (got_weights[:, None, None, None] * got[None]).astype(jnp.bfloat16)
     partial_sum = (mine.astype(jnp.float32) + theirs.astype(jnp.float32)).astype(jnp.bfloat16)
@@ -254,7 +261,7 @@
             P(freq, "row", None),
             P(freq, "row", None),
             P(freq, "row"),
-            P(freq),
+            P(),
         ),
         out_specs=P(None, freq, "row"),
         check_vma=False,

time: 216 us -> 243 us (1.12)
  blocking collectives: 0 us -> 32.7 us
  waiting for transfers between devices: 121 us -> 115 us
  starting transfers between devices: 28.9 us -> 23.2 us
  Pallas kernels: 8.7 us -> 12.6 us
  local copies, waits for them, and re-layouts: 8.88 us -> 11.6 us
    unnamed x0 -> x1, blocking collectives: none -> 32.7 us
    reduce_scatter x1, waiting for transfers between devices: 46.2 us -> 38.5 us  [shards(): summed = lax.psum_scatter(partial_sum, 'z', scatter_dimension=1, tiled=True)]
    pallas_call x1, Pallas kernels: 8.7 us -> 12.6 us  [grid_into_slab(): pl.pallas_call(grid_kernel, out_shape=jax.ShapeDtypeStruct((2, GRID // TV...]
    all_to_all x1, starting transfers between devices: 14.1 us -> 10.7 us  [shards(): lax.all_to_all(for_sending(spectrum), 'row', split_axis=0, concat_axis=0,...]
  transfers between devices with their start and end apart: 5 -> 4, of which waited for: 4 -> 3; matrix products, arithmetic and copies ran while one was open for 1% -> 2% of each run, Pallas kernels for 0% -> 0%
where the time goes in v10:
time: 243 us; the launch traced here: 242 us
  waiting for transfers between devices  115 us (47%)
  blocking collectives  32.7 us (13%)
  starting transfers between devices  23.2 us (10%)
  matrix products  18.7 us (8%)
  between operations  15.6 us (6%)
  Pallas kernels  12.6 us (5%)
  other arithmetic  12.4 us (5%)
  local copies, waits for them, and re-layouts  11.6 us (5%)
    all_to_all x1, waiting for transfers between devices, shards(): lax.all_to_all(for_sending(spectrum), 'row', split_axis=0, concat_axis=0,...  47.2 us
    reduce_scatter x1, waiting for transfers between devices, shards(): summed = lax.psum_scatter(partial_sum, 'z', scatter_dimension=1, tiled=True)  38.5 us
    unnamed x1, blocking collectives  32.7 us
    all_to_all x1, waiting for transfers between devices, shards(): lax.all_to_all(send.reshape((row_count, capacity) + payload.shape[1:]), '...  29.5 us
    pallas_call x1, Pallas kernels, grid_into_slab(): pl.pallas_call(grid_kernel, out_shape=jax.ShapeDtypeStruct((2, GRID // TV...  12.6 us
    all_to_all x1, starting transfers between devices, shards(): lax.all_to_all(for_sending(spectrum), 'row', split_axis=0, concat_axis=0,...  10.7 us
    all_to_all x1, starting transfers between devices, shards(): lax.all_to_all(send.reshape((row_count, capacity) + payload.shape[1:]), '...  10.2 us
    dot_general x1, matrix products, transform_last(): step = product('parb,pak->krb', both, complex_weights(cos_outer, sin_outer))  6.39 us
  transfers between devices with their start and end apart: 4, of which 3 were waited for; matrix products, arithmetic and copies ran while one was open for 2% of the time, Pallas kernels for 0%

profile of v10, /device:TPU:6, one launch (start us, length us, event | category | flops | bytes accessed | tf_op | source)
XLA Modules:
  0.0 242.0 jit_solution(16312064685085359062)
XLA Ops:
  6.5 0.7 fusion.36
  7.4 0.8 select_reduce_fusion
  8.2 0.7 multiply_add_fusion
  8.9 0.8 bitcast_dynamic-update-slice_fusion.2
  9.6 0.7 convert_bitcast_fusion.1
  10.4 0.9 bitcast_dynamic-update-slice_fusion.1
  11.3 0.9 bitcast_dynamic-update-slice_fusion
  12.2 0.8 bitcast_dynamic-update-slice_fusion.4
  13.0 0.8 bitcast_dynamic-update-slice_fusion.3
  13.8 0.6 fusion.33
  14.8 1.3 copy.31
  16.0 10.2 %all-to-all-start = ((bf16[32,8,19,128]{3,1,2,0:T(8,128)(2,1)}), bf16[32,8,19,128]{3,1,2,0:T(8,128)(2,1)S(1)}, u32[]{:S(2)}, u32[]{:S(2)}) async-start(bf16[32,8,19,128]{3,1,2,0:T(8,128)(2,1)} %copy.31), calls=%async_computation | async-start | bytes 2490368 | tf_op jit(solution)/shard_map/all_to_all | solution.py:207
  27.2 29.5 %all-to-all-done = bf16[32,8,19,128]{3,1,2,0:T(8,128)(2,1)S(1)} async-done(((bf16[32,8,19,128]{3,1,2,0:T(8,128)(2,1)}), bf16[32,8,19,128]{3,1,2,0:T(8,128)(2,1)S(1)}, u32[]{:S(2)}, u32[]{:S(2)}) %all-to-all-start) | async-done | bytes 1245216 | tf_op jit(solution)/shard_map/all_to_all | solution.py:207
  57.1 1.0 slice_reduce_fusion
  58.8 12.6 %shard_map.82 = f32[2,32,128,128]{3,2,1,0:T(8,128)} custom-call(s32[256]{0:T(256)} %convert_convert_fusion.tile_ref, bf16[256,19,128]{2,1,0:T(8,128)(2,1)} %bitcast.74), custom_call_target="tpu_custom_call" | custom-call | tf_op jit(solution)/shard_map/pallas_call | solution.py:155
  71.4 6.4 %fusion.6 = f32[64,128,128]{2,0,1:T(8,128)S(1)} fusion(f32[2,32,128,128]{3,2,1,0:T(8,128)} %shard_map.82, f32[1,32,64]{2,1,0:T(8,128)S(1)} %get-tuple-element.26, f32[1,32,64]{2,1,0:T(8,128)S(1)} %get-tuple-element.25), kind=kOutput, calls=%fused_computation.12 | convolution fusion | flops 402657280 | bytes 8404992 | tf_op jit(solution)/shard_map/parb,pak->krb/dot_general | solution.py:64
  77.8 0.7 subtract_bitcast_fusion.1
  78.9 6.0 %bitcast_convert_fusion = bf16[2,32,4,32,128]{4,1,3,2,0:T(8,128)(2,1)S(1)} fusion(f32[2,32,128,128,1,1]{3,1,2,0,5,4:T(8,128)S(1)} %maximum_bitcast_fusion, f32[1,128,2,32,4]{1,3,0,4,2:T(8,128)S(1)} %copy.29, f32[1,128,2,32,4]{1,3,0,4,2:T(8,128)S(1)} %copy.28), kind=kOutput, calls=%fused_computation.2 | convolution fusion | flops 1611726848 | bytes 6553600 | tf_op jit(solution)/shard_map/qkrb,qbsdm->drsmk/dot_general | solution.py:73
  84.8 3.0 %copy.35 = bf16[32,128,2,128]{3,2,1,0:T(2,128)(2,1)} copy(bf16[32,128,2,128]{1,0,3,2:T(8,128)(2,1)S(1)} %bitcast.71) | data formatting | bytes 4194304 | tf_op jit(solution)/shard_map/convert_element_type | solution.py:17
  87.8 10.7 %all-to-all-start.1 = ((bf16[32,128,2,128]{3,2,1,0:T(2,128)(2,1)}), bf16[32,128,2,128]{3,2,1,0:T(2,128)(2,1)S(1)}, u32[]{:S(2)}, u32[]{:S(2)}) async-start(bf16[32,128,2,128]{3,2,1,0:T(2,128)(2,1)} %copy.35), calls=%async_computation.1 | async-start | bytes 4194304 | tf_op jit(solution)/shard_map/all_to_all | solution.py:227
  99.3 47.2 %all-to-all-done.1 = bf16[32,128,2,128]{3,2,1,0:T(2,128)(2,1)S(1)} async-done(((bf16[32,128,2,128]{3,2,1,0:T(2,128)(2,1)}), bf16[32,128,2,128]{3,2,1,0:T(2,128)(2,1)S(1)}, u32[]{:S(2)}, u32[]{:S(2)}) %all-to-all-start.1) | async-done | bytes 2097184 | tf_op jit(solution)/shard_map/all_to_all | solution.py:227
  146.5 2.3 convolution_bitcast_fusion
  148.9 1.4 subtract_bitcast_fusion
  150.7 3.5 %bitcast_multiply_fusion = f32[128,32,128]{2,0,1:T(8,128)S(1)} fusion(f32[2,32,128,128]{3,1,2,0:T(8,128)S(1)} %pad_maximum_fusion, f32[1,128,128]{1,2,0:T(8,128)S(1)} %get-tuple-element.35, f32[1,128,128]{1,2,0:T(8,128)S(1)} %get-tuple-element.36), kind=kOutput, calls=%fused_computation.14 | convolution fusion | flops 805863424 | bytes 6422528 | tf_op jit(solution)/shard_map/qkbc,qbm->mkc/dot_general | solution.py:87
  154.2 1.2 copy.40
  155.6 1.9 collective-permute-start
  158.2 1.3 dynamic-slice.7
  159.5 0.8 dynamic-update-slice.3
  160.3 32.7 %all-reduce = f32[16]{0:T(128)S(1)} all-reduce(f32[16]{0:T(128)S(1)} %dynamic-update-slice.3), channel_id=2, replica_groups=mesh['z'=8,'core'=2,'row'=32] {'z','core'}, use_global_device_ids=true, to_apply=%add | all-reduce | flops 16 | bytes 128
  192.9 0.7 fusion.64
  195.0 1.7 add_convert_fusion
  196.7 38.5 %reduce-scatter.2.cloned.1.call-done = bf16[3,1,256,128]{3,2,0,1:T(8,128)(2,1)} async-done(((bf16[3,8,256,128]{3,2,0,1:T(8,128)(2,1)}), bf16[3,1,256,128]{3,2,0,1:T(8,128)(2,1)}) %reduce-scatter.2.cloned.1.call-update) | async-done | bytes 196624 | tf_op jit(solution)/shard_map/reduce_scatter | solution.py:244
  (30 shorter events, 4.3 us)
Async XLA Ops:
  16.0 40.7 %all-to-all-start = ((bf16[32,8,19,128]{3,1,2,0:T(8,128)(2,1)}), bf16[32,8,19,128]{3,1,2,0:T(8,128)(2,1)S(1)}, u32[]{:S(2)}, u32[]{:S(2)}) async-start(bf16[32,8,19,128]{3,1,2,0:T(8,128)(2,1)} %copy.31), calls=%async_computation | async-start | bytes 2490368 | tf_op jit(solution)/shard_map/all_to_all | solution.py:207
  57.1 1.6 copy-start
  87.8 58.7 %all-to-all-start.1 = ((bf16[32,128,2,128]{3,2,1,0:T(2,128)(2,1)}), bf16[32,128,2,128]{3,2,1,0:T(2,128)(2,1)S(1)}, u32[]{:S(2)}, u32[]{:S(2)}) async-start(bf16[32,128,2,128]{3,2,1,0:T(2,128)(2,1)} %copy.35), calls=%async_computation.1 | async-start | bytes 4194304 | tf_op jit(solution)/shard_map/all_to_all | solution.py:227
  98.6 136.6 %reduce-scatter.2.cloned.1.call-start = ((), (), s32[]{:S(2)}) async-start(), calls=%async_computation.3 | async-start | bytes 1769472 | tf_op jit(solution)/shard_map/reduce_scatter | solution.py:244
  155.6 39.3 %collective-permute-start = (f32[8,256,128]{2,1,0:T(8,128)S(1)}, f32[8,256,128]{2,1,0:T(8,128)S(1)}, u32[]{:S(2)}, u32[]{:S(2)}) collective-permute-start(f32[8,256,128]{2,1,0:T(8,128)S(1)} %get-tuple-element.22), channel_id=1, source_target_pairs={{0,32},{32,0},{1,33},{33,1},{2,34},{34,2},{3,35},{35,3},{4,36},{36... | collective-permute-start | bytes 3145736 | tf_op jit(solution)/shard_map/ppermute | solution.py:239
Sparse Core Ops, SparseCore 0:
  196.8 38.3 reduce-scatter.1

commit v11 on v8

--- a/solution.py
+++ b/solution.py
@@ -96,7 +96,7 @@
 CHUNK = 128
 
 
-GROUP = 8
+GROUP = 16
 
 
 def grid_kernel(tile_ref, pay_ref, out_ref, order_ref):

time: 216 us -> 215 us (level)
  no operation moved by 1% of the time
where the time goes in v11:
time: 215 us; the launch traced here: 214 us
  waiting for transfers between devices  123 us (57%)
  starting transfers between devices  28.8 us (13%)
  matrix products  18.7 us (9%)
  between operations  14.3 us (7%)
  other arithmetic  12.4 us (6%)
  local copies, waits for them, and re-layouts  8.88 us (4%)
  Pallas kernels  8.58 us (4%)
    reduce_scatter x1, waiting for transfers between devices, shards(): summed = lax.psum_scatter(partial_sum, 'z', scatter_dimension=1, tiled=True)  46.5 us
    all_to_all x1, waiting for transfers between devices, shards(): lax.all_to_all(for_sending(spectrum), 'row', split_axis=0, concat_axis=0,...  45.7 us
    all_to_all x1, waiting for transfers between devices, shards(): lax.all_to_all(send.reshape((row_count, capacity) + payload.shape[1:]), '...  29.5 us
    all_to_all x1, starting transfers between devices, shards(): lax.all_to_all(for_sending(spectrum), 'row', split_axis=0, concat_axis=0,...  14 us
    all_to_all x1, starting transfers between devices, shards(): lax.all_to_all(send.reshape((row_count, capacity) + payload.shape[1:]), '...  10.2 us
    pallas_call x1, Pallas kernels, grid_into_slab(): pl.pallas_call(grid_kernel, out_shape=jax.ShapeDtypeStruct((2, GRID // TV...  8.58 us
    dot_general x1, matrix products, transform_last(): step = product('parb,pak->krb', both, complex_weights(cos_outer, sin_outer))  6.39 us
    dot_general x1, matrix products, transform_last(): product('qkrb,qbsdm->drsmk', jnp.stack([twist_real, twist_imag]), weights)  5.95 us
  transfers between devices with their start and end apart: 5, of which 4 were waited for; matrix products, arithmetic and copies ran while one was open for 1% of the time, Pallas kernels for 0%

profile of v11, /device:TPU:6, one launch (start us, length us, event | category | flops | bytes accessed | tf_op | source)
XLA Modules:
  0.0 214.2 jit_solution(18153593950684077610)
XLA Ops:
  6.5 0.7 fusion.36
  7.4 0.8 select_reduce_fusion
  8.2 0.7 multiply_add_fusion
  8.9 0.8 bitcast_dynamic-update-slice_fusion.2
  9.6 0.7 convert_bitcast_fusion.1
  10.4 0.9 bitcast_dynamic-update-slice_fusion.1
  11.3 0.9 bitcast_dynamic-update-slice_fusion
  12.2 0.8 bitcast_dynamic-update-slice_fusion.4
  13.0 0.8 bitcast_dynamic-update-slice_fusion.3
  13.8 0.6 fusion.33
  14.8 1.3 copy.31
  16.0 10.2 %all-to-all-start = ((bf16[32,8,19,128]{3,1,2,0:T(8,128)(2,1)}), bf16[32,8,19,128]{3,1,2,0:T(8,128)(2,1)S(1)}, u32[]{:S(2)}, u32[]{:S(2)}) async-start(bf16[32,8,19,128]{3,1,2,0:T(8,128)(2,1)} %copy.31), calls=%async_computation | async-start | bytes 2490368 | tf_op jit(solution)/shard_map/all_to_all | solution.py:207
  27.2 29.5 %all-to-all-done = bf16[32,8,19,128]{3,1,2,0:T(8,128)(2,1)S(1)} async-done(((bf16[32,8,19,128]{3,1,2,0:T(8,128)(2,1)}), bf16[32,8,19,128]{3,1,2,0:T(8,128)(2,1)S(1)}, u32[]{:S(2)}, u32[]{:S(2)}) %all-to-all-start) | async-done | bytes 1245216 | tf_op jit(solution)/shard_map/all_to_all | solution.py:207
  57.2 1.0 slice_reduce_fusion
  58.2 0.6 convert_convert_fusion.tile_ref
  58.8 8.6 %shard_map.82 = f32[2,32,128,128]{3,2,1,0:T(8,128)} custom-call(s32[256]{0:T(256)} %convert_convert_fusion.tile_ref, bf16[256,19,128]{2,1,0:T(8,128)(2,1)} %bitcast.73), custom_call_target="tpu_custom_call" | custom-call | tf_op jit(solution)/shard_map/pallas_call | solution.py:155
  67.3 6.4 %fusion.6 = f32[64,128,128]{2,0,1:T(8,128)S(1)} fusion(f32[2,32,128,128]{3,2,1,0:T(8,128)} %shard_map.82, f32[1,32,64]{2,1,0:T(8,128)S(1)} %get-tuple-element.26, f32[1,32,64]{2,1,0:T(8,128)S(1)} %get-tuple-element.25), kind=kOutput, calls=%fused_computation.12 | convolution fusion | flops 402657280 | bytes 8404992 | tf_op jit(solution)/shard_map/parb,pak->krb/dot_general | solution.py:64
  73.7 0.7 subtract_bitcast_fusion.1
  74.4 0.4 maximum_bitcast_fusion
  74.9 6.0 %bitcast_convert_fusion = bf16[2,32,4,32,128]{4,1,3,2,0:T(8,128)(2,1)S(1)} fusion(f32[2,32,128,128,1,1]{3,1,2,0,5,4:T(8,128)S(1)} %maximum_bitcast_fusion, f32[1,128,2,32,4]{1,3,0,4,2:T(8,128)S(1)} %copy.29, f32[1,128,2,32,4]{1,3,0,4,2:T(8,128)S(1)} %copy.28), kind=kOutput, calls=%fused_computation.2 | convolution fusion | flops 1611726848 | bytes 6553600 | tf_op jit(solution)/shard_map/qkrb,qbsdm->drsmk/dot_general | solution.py:73
  80.8 3.0 %copy.35 = bf16[32,128,2,128]{3,2,1,0:T(2,128)(2,1)} copy(bf16[32,128,2,128]{1,0,3,2:T(8,128)(2,1)S(1)} %bitcast.70) | data formatting | bytes 4194304 | tf_op jit(solution)/shard_map/convert_element_type | solution.py:17
  83.8 14.0 %all-to-all-start.1 = ((bf16[32,128,2,128]{3,2,1,0:T(2,128)(2,1)}), bf16[32,128,2,128]{3,2,1,0:T(2,128)(2,1)S(1)}, u32[]{:S(2)}, u32[]{:S(2)}) async-start(bf16[32,128,2,128]{3,2,1,0:T(2,128)(2,1)} %copy.35), calls=%async_computation.1 | async-start | bytes 4194304 | tf_op jit(solution)/shard_map/all_to_all | solution.py:220
  98.6 45.7 %all-to-all-done.1 = bf16[32,128,2,128]{3,2,1,0:T(2,128)(2,1)S(1)} async-done(((bf16[32,128,2,128]{3,2,1,0:T(2,128)(2,1)}), bf16[32,128,2,128]{3,2,1,0:T(2,128)(2,1)S(1)}, u32[]{:S(2)}, u32[]{:S(2)}) %all-to-all-start.1) | async-done | bytes 2097184 | tf_op jit(solution)/shard_map/all_to_all | solution.py:220
  144.3 2.3 %convolution_bitcast_fusion = f32[64,128,128]{2,0,1:T(8,128)S(1)} fusion(bf16[32,128,2,128]{3,2,1,0:T(2,128)(2,1)S(1)} %all-to-all-done.1, f32[1,32,64]{2,1,0:T(8,128)S(1)} %get-tuple-element.26, f32[1,32,64]{2,1,0:T(8,128)S(1)} %get-tuple-element.25), kind=kOutput, calls=%fused_computation.13 | convolution fusion | flops 402657280 | bytes 6307840 | tf_op jit(solution)/shard_map/abpc,pak->kbc/dot_general | solution.py:82
  146.6 1.4 subtract_bitcast_fusion
  148.4 3.5 %bitcast_multiply_fusion = f32[128,32,128]{2,0,1:T(8,128)S(1)} fusion(f32[2,32,128,128]{3,1,2,0:T(8,128)S(1)} %pad_maximum_fusion, f32[1,128,128]{1,2,0:T(8,128)S(1)} %get-tuple-element.33, f32[1,128,128]{1,2,0:T(8,128)S(1)} %get-tuple-element.34), kind=kOutput, calls=%fused_computation.14 | convolution fusion | flops 805863424 | bytes 6422528 | tf_op jit(solution)/shard_map/qkbc,qbm->mkc/dot_general | solution.py:87
  151.9 1.2 copy.40
  153.4 1.9 collective-permute-start.1
  156.0 2.4 %collective-permute-start = (f32[3]{0:T(128)S(1)}, f32[3]{0:T(128)S(1)}, u32[]{:S(2)}, u32[]{:S(2)}) collective-permute-start(f32[3]{0:T(128)S(1)} %pad_maximum_fusion.3), channel_id=1, source_target_pairs={{0,32},{32,0},{1,33},{33,1},{2,34},{34,2},{3,35},{35,3},{4,36},{36... | collective-permute-start | bytes 44 | tf_op jit(solution)/shard_map/ppermute | solution.py:233
  158.4 0.8 collective-permute-done
  159.2 1.7 add_convert_fusion
  160.9 46.5 %reduce-scatter.2.cloned.1.call-done = bf16[3,1,256,128]{3,2,0,1:T(8,128)(2,1)} async-done(((bf16[3,8,256,128]{3,2,0,1:T(8,128)(2,1)}), bf16[3,1,256,128]{3,2,0,1:T(8,128)(2,1)}) %reduce-scatter.2.cloned.1.call-update) | async-done | bytes 196624 | tf_op jit(solution)/shard_map/reduce_scatter | solution.py:237
  (27 shorter events, 3.3 us)
Async XLA Ops:
  16.0 40.7 %all-to-all-start = ((bf16[32,8,19,128]{3,1,2,0:T(8,128)(2,1)}), bf16[32,8,19,128]{3,1,2,0:T(8,128)(2,1)S(1)}, u32[]{:S(2)}, u32[]{:S(2)}) async-start(bf16[32,8,19,128]{3,1,2,0:T(8,128)(2,1)} %copy.31), calls=%async_computation | async-start | bytes 2490368 | tf_op jit(solution)/shard_map/all_to_all | solution.py:207
  57.1 1.6 copy-start
  83.8 60.5 %all-to-all-start.1 = ((bf16[32,128,2,128]{3,2,1,0:T(2,128)(2,1)}), bf16[32,128,2,128]{3,2,1,0:T(2,128)(2,1)S(1)}, u32[]{:S(2)}, u32[]{:S(2)}) async-start(bf16[32,128,2,128]{3,2,1,0:T(2,128)(2,1)} %copy.35), calls=%async_computation.1 | async-start | bytes 4194304 | tf_op jit(solution)/shard_map/all_to_all | solution.py:220
  97.8 109.6 %reduce-scatter.2.cloned.1.call-start = ((), (), s32[]{:S(2)}) async-start(), calls=%async_computation.3 | async-start | bytes 1769472 | tf_op jit(solution)/shard_map/reduce_scatter | solution.py:237
  153.4 5.9 %collective-permute-start.1 = (f32[8,256,128]{2,1,0:T(8,128)S(1)}, f32[8,256,128]{2,1,0:T(8,128)S(1)}, u32[]{:S(2)}, u32[]{:S(2)}) collective-permute-start(f32[8,256,128]{2,1,0:T(8,128)S(1)} %get-tuple-element.22), channel_id=1, source_target_pairs={{0,32},{32,0},{1,33},{33,1},{2,34},{34,2},{3,35},{35,3},{4,36},{36... | collective-permute-start | bytes 3145736 | tf_op jit(solution)/shard_map/ppermute | solution.py:232
  156.0 3.2 %collective-permute-start = (f32[3]{0:T(128)S(1)}, f32[3]{0:T(128)S(1)}, u32[]{:S(2)}, u32[]{:S(2)}) collective-permute-start(f32[3]{0:T(128)S(1)} %pad_maximum_fusion.3), channel_id=1, source_target_pairs={{0,32},{32,0},{1,33},{33,1},{2,34},{34,2},{3,35},{35,3},{4,36},{36... | collective-permute-start | bytes 44 | tf_op jit(solution)/shard_map/ppermute | solution.py:233
Sparse Core Ops, SparseCore 0:
  161.0 46.3 reduce-scatter.1
